TPU v7x, 256 devices: a whole 4x4x8 slice. The times are simulated.
256 devices in a mesh: dom: 16 (over z, core), grp: 16 (over y, x).
Axes of the slice: x: 4, y: 4, z: 8, core: 2. Of those that a mesh axis runs over, the one named last changes fastest.
Arguments:
- positions: float32 [65536, 3, 128], P(('dom', 'grp')), may hold values from -4 to 4
- velocities: float32 [65536, 3, 128], P(('dom', 'grp')), may hold values from -9 to 9
- masses: float32 [65536, 128], P(('dom', 'grp')), may hold values from 0.3 to 3
- destination: int32 [65536], P(('dom', 'grp')), may hold values from 0 to 15, as said below
- group_ids: int32 [65536, 128], P(('dom', 'grp')), may hold values from 0 to 1023, as said below
- boundary_set: int32 [256, 64], P(('dom', 'grp')), may hold values from 0 to 511, as said below
- send_list: int32 [256, 16, 16], P(('dom', 'grp')), may hold values from 0 to 63, as said below
- send_count: int32 [256, 16], P(('dom', 'grp')), may hold values from 0 to 16, as said below
- partners: int32 [131072, 4], P(('dom', 'grp')), may hold values from 0 to 767, as said below
Outputs:
- energy: float32 [65536, 128], P(('dom', 'grp'))
- group_kinetic: float32 [1024], replicated
Inputs may be any that keep to these rules, and one draw needn't show every extreme that they name: Each block of 256 leaves sends at most 32 leaves to one destination; in each dom index one destination receives exactly 32 leaves from every block. `group_ids`: the particles of block b carry the 16 group numbers 4 * b to 4 * b + 15, taken modulo 1024, each at least once and no others. `boundary_set`: each row holds 64 distinct slot numbers. `send_list`: each row of 16 holds distinct positions. `send_count`: A block sends nothing to its own grp index; in each dom index one grp index receives 16 from every other block. `partners`: each row holds 4 distinct entry numbers of combined.
All inputs are finite; a program needn't handle non-finite values.
Results may differ from a plain program's by a relative error of at most 0.0003.
Values sent between devices are 32-bit elements; how exact they have to be, the bound alone decides.
No kernel may reach another device: no remote copies, remote signals or barrier semaphores. Data moves between devices by JAX's collectives and lax.ppermute only.
A program may use at most 64 MiB of HBM per device.

v0:
```python
import jax
import jax.numpy as jnp
from jax import lax
from jax.sharding import PartitionSpec as P

GSPAN = 16
GROUP_DEV = 4


softening = 0.0025
exact = lax.Precision.HIGHEST


def select_rows(table, index):
    count = table.shape[0]
    flat = table.reshape(count, -1)
    picker = (index.reshape(-1)[:, None] == jnp.arange(count, dtype=jnp.int32)[None, :]).astype(
        jnp.float32
    )
    chosen = jnp.dot(picker, flat, precision=exact, preferred_element_type=jnp.float32)
    return chosen.reshape(index.shape + table.shape[1:])


def tile_potential(targets, sources):
    distance = softening
    for component in range(3):
        offset = targets[:, None, component, :, None] - sources[:, :, component, None, :]
        distance = distance + offset * offset
    weights = sources[:, :, 3, None, :] * lax.rsqrt(distance)
    return -jnp.sum(weights, axis=(1, 3))


def slot_potential(owned, combined, pair_index, coupling):
    slot_count = owned.shape[0]
    leaf_width = owned.shape[2]
    block_rows = max(32, slot_count // 16)

    def one_block(inputs):
        targets, indices = inputs
        sources = select_rows(combined, indices)
        return tile_potential(targets, sources)

    result = lax.map(
        one_block,
        (
            owned.reshape(slot_count // block_rows, block_rows, 4, leaf_width),
            pair_index.reshape(slot_count // block_rows, block_rows, pair_index.shape[1]),
        ),
    )
    return result.reshape(slot_count, leaf_width) * coupling


def shards(
    positions,
    velocities,
    masses,
    destination,
    group_ids,
    boundary_set,
    send_list,
    send_count,
    partners,
):
    owners = lax.axis_size("grp")
    leaves = positions.shape[0]
    leaf_width = positions.shape[2]
    capacity = 2 * leaves // owners
    slot_count = owners * capacity
    groups = GROUP_DEV * lax.axis_size("dom") * owners
    block_index = lax.axis_index("dom") * owners + lax.axis_index("grp")
    first_group = block_index * GROUP_DEV
    mass_flat = masses.reshape(-1)
    group_flat = group_ids.reshape(-1)
    speeds = jnp.transpose(velocities, (1, 0, 2)).reshape(3, -1)
    local_ids = (group_flat - first_group) % groups
    member = (jnp.arange(GSPAN, dtype=jnp.int32)[:, None] == local_ids[None, :]).astype(jnp.float32)
    place = (
        (first_group + jnp.arange(GSPAN, dtype=jnp.int32))[:, None] % groups
        == jnp.arange(groups, dtype=jnp.int32)[None, :]
    ).astype(jnp.float32)

    def group_sums(stats):
        local_sums = jnp.einsum(
            "kp,gp->kg", stats, member, precision=exact, preferred_element_type=jnp.float32
        )
        return jnp.dot(local_sums, place, precision=exact, preferred_element_type=jnp.float32)

    first_sums = group_sums(
        jnp.concatenate([mass_flat[None, :], mass_flat[None, :] * speeds], axis=0)
    )
    mass_total, momentum = lax.psum((first_sums[0], first_sums[1:]), ("dom", "grp"))
    bulk_velocity = momentum / mass_total[None, :]
    bulk_local = jnp.einsum(
        "kq,gq->kg", bulk_velocity, place, precision=exact, preferred_element_type=jnp.float32
    )
    per_particle = jnp.dot(bulk_local, member, precision=exact, preferred_element_type=jnp.float32)
    relative = speeds - per_particle
    kinetic = 0.5 * jnp.sum(relative * relative, axis=0)
    heat_sum = lax.psum(group_sums((mass_flat * kinetic)[None, :])[0], ("dom", "grp"))
    group_kinetic = heat_sum / mass_total
    onehot = (destination[:, None] == jnp.arange(owners, dtype=jnp.int32)[None, :]).astype(
        jnp.int32
    )
    leaf_rank = jnp.sum((jnp.cumsum(onehot, axis=0) - onehot) * onehot, axis=1)
    target = destination * capacity + leaf_rank
    payload = jnp.concatenate([positions, masses[:, None, :]], axis=1)
    placing = (jnp.arange(slot_count, dtype=jnp.int32)[:, None] == target[None, :]).astype(
        jnp.float32
    )
    outgoing = jnp.dot(
        placing, payload.reshape(leaves, -1), precision=exact, preferred_element_type=jnp.float32
    ).reshape(slot_count, 4, leaf_width)
    owned = lax.all_to_all(outgoing, "grp", split_axis=0, concat_axis=0, tiled=True)
    set_size = boundary_set.shape[1]
    per_peer = send_list.shape[2]
    boundary = select_rows(owned, boundary_set[0])
    every_set = lax.all_gather(boundary, "grp", axis=0, tiled=True)
    all_lists, all_counts = (
        lax.all_gather(send_list, "grp", axis=0, tiled=True),
        lax.all_gather(send_count, "grp", axis=0, tiled=True),
    )
    my_index = lax.axis_index("grp")
    my_lists = jnp.take(all_lists, my_index, axis=1)
    my_counts = jnp.take(all_counts, my_index, axis=1)
    positions_in = jnp.arange(owners, dtype=jnp.int32)[:, None] * set_size + my_lists
    remote = select_rows(every_set, positions_in)
    is_live = jnp.arange(per_peer, dtype=jnp.int32)[None, :] < my_counts[:, None]
    remote = jnp.where(is_live[:, :, None, None], remote, jnp.zeros_like(remote))
    remote = remote.reshape(owners * per_peer, 4, leaf_width)
    combined = jnp.concatenate([owned, remote], axis=0)
    coupling = 1.0 / (partners.shape[1] * leaf_width)
    potential = slot_potential(owned, combined, partners, coupling)
    returned = lax.all_to_all(potential, "grp", split_axis=0, concat_axis=0, tiled=True)
    own_potential = jnp.einsum(
        "sl,sp->lp", placing, returned, precision=exact, preferred_element_type=jnp.float32
    )
    energy = kinetic.reshape(leaves, leaf_width) + own_potential
    return (energy, group_kinetic)


def solution(mesh):
    in_specs = (
        P(("dom", "grp"), None, None),
        P(("dom", "grp"), None, None),
        P(("dom", "grp"), None),
        P(("dom", "grp")),
        P(("dom", "grp"), None),
        P(("dom", "grp"), None),
        P(("dom", "grp"), None, None),
        P(("dom", "grp"), None),
        P(("dom", "grp"), None),
    )
    out_specs = (P(("dom", "grp"), None), P())
    return jax.shard_map(shards, mesh=mesh, in_specs=in_specs, out_specs=out_specs, check_vma=False)
```

profile of v0, /device:TPU:1, one launch (start us, length us, event | category | flops | bytes accessed | tf_op | source)
XLA Modules:
  0.0 366.0 jit_solution(14305169449429546651)
XLA Ops:
  8.7 0.8 fusion.45
  10.2 1.2 copy.63
  11.3 1.0 copy.62
  13.7 23.4 %all_to_all.14 = f32[512,4,128]{2,1,0:T(4,128)S(1)} all-to-all(f32[512,4,128]{2,1,0:T(4,128)S(1)} %copy.64), channel_id=1, replica_groups=mesh['dom'=16,'grp'=16] {'grp'}, dimensions={0} | all-to-all | bytes 2097152 | tf_op jit(solution)/shard_map/all_to_all | solution.py:113
  37.5 1.4 fusion.15
  39.4 1.6 fusion.9
  42.0 14.1 %all-gather = s32[16,1,16]{2,1,0:T(1,128)S(1)} all-gather(s32[1,1,16]{2,1,0:T(1,128)S(1)} %bitcast.158), channel_id=1, replica_groups=mesh['dom'=16,'grp'=16] {'grp'}, dimensions={0}, use_global_device_ids=true | all-gather | bytes 1088 | tf_op jit(solution)/shard_map/all_gather | solution.py:120
  56.6 17.3 %all_gather.10 = s32[16,16,16]{2,1,0:T(8,128)S(1)} all-gather(s32[1,16,16]{2,1,0:T(8,128)S(1)} %copy-done.7), channel_id=1, replica_groups=mesh['dom'=16,'grp'=16] {'grp'}, dimensions={0}, use_global_device_ids=true | all-gather | bytes 17408 | tf_op jit(solution)/shard_map/all_gather | solution.py:119
  73.9 89.0 %all-reduce = (f32[3,1024]{1,0:T(4,128)S(1)}, f32[1024]{0:T(1024)S(1)}) all-reduce(f32[3,1024]{1,0:T(4,128)S(1)} %slice.60, f32[1024]{0:T(1024)S(1)} %bitcast.154), channel_id=1, replica_groups=mesh['dom'=16,'grp'=16] {'dom','grp'}, use_global_device_ids=true, to_apply=%region_0.1 | all-reduce | flops 4096 | bytes 32768 | tf_op jit(solution)/shard_map/psum | solution.py:91
  163.1 1.1 fusion.13
  165.0 1.9 copy.66
  166.9 1.3 fusion.10
  168.6 1.5 pad_maximum_fusion
  170.1 1.7 copy.70
  171.8 104.0 %while.12 = (s32[]{:T(128)}, f32[16,32,128]{2,1,0:T(8,128)S(1)}, s32[16,32,4]{1,0,2:T(8,128)}, f32[768,4,128]{0,2,1:T(8,128)S(1)}, f32[16,32,4,128]{3,2,1,0:T(4,128)S(1)}, /*index=5*/s32[]{:T(128)}) while((s32[]{:T(128)}, f32[16,32,128]{2,1,0:T(8,128)S(1)}, s32[16,32,4]{1,0,2:T(8,128)}, f32[768,4,128]{0,2,1:T(8,128)S(1)}, ...), condition=%wide.region_8.9_spmd, body=%wide.region_6.8_spmd.sunk | while | flops 627146752 | bytes 3606097 | solution.py:43
  171.8 0.8 constant_dynamic-slice_fusion.4
  172.7 1.0 fusion.63
  174.0 4.4 %multiply_reduce_fusion.2 = f32[32,128]{1,0:T(8,128)S(1)} fusion(f32[32,4,128]{2,1,0:T(4,128)S(1)} %copy.88, f32[32,128]{1,0:T(8,128)S(1)} %get-tuple-element.135, f32[32,4,128]{2,1,0:T(4,128)S(1)} %copy.90, f32[32,128]{1,0:T(8,128)S(1)} %get-tuple-element.137, f32[32,4,128]{2,1,0:T(4,128)S(1)} %copy.91, f32[32,128]{1,0:T(8,128)S(1)} %get-tuple-element.139, ...), kind=kLoop, calls=%fused_computation.clone.1 | loop fusion | flops 23064576 | bytes 327680 | tf_op jit(solution)/shard_map/while/body/eval_jaxpr/reduce_sum | solution.py:30
  178.4 0.7 constant_dynamic-slice_fusion.4
  179.1 1.0 fusion.63
  180.5 4.4 %multiply_reduce_fusion.2 = f32[32,128]{1,0:T(8,128)S(1)} fusion(f32[32,4,128]{2,1,0:T(4,128)S(1)} %copy.88, f32[32,128]{1,0:T(8,128)S(1)} %get-tuple-element.135, f32[32,4,128]{2,1,0:T(4,128)S(1)} %copy.90, f32[32,128]{1,0:T(8,128)S(1)} %get-tuple-element.137, f32[32,4,128]{2,1,0:T(4,128)S(1)} %copy.91, f32[32,128]{1,0:T(8,128)S(1)} %get-tuple-element.139, ...), kind=kLoop, calls=%fused_computation.clone.1 | loop fusion | flops 23064576 | bytes 327680 | tf_op jit(solution)/shard_map/while/body/eval_jaxpr/reduce_sum | solution.py:30
  184.9 0.7 constant_dynamic-slice_fusion.4
  185.6 1.0 fusion.63
  187.0 4.4 %multiply_reduce_fusion.2 = f32[32,128]{1,0:T(8,128)S(1)} fusion(f32[32,4,128]{2,1,0:T(4,128)S(1)} %copy.88, f32[32,128]{1,0:T(8,128)S(1)} %get-tuple-element.135, f32[32,4,128]{2,1,0:T(4,128)S(1)} %copy.90, f32[32,128]{1,0:T(8,128)S(1)} %get-tuple-element.137, f32[32,4,128]{2,1,0:T(4,128)S(1)} %copy.91, f32[32,128]{1,0:T(8,128)S(1)} %get-tuple-element.139, ...), kind=kLoop, calls=%fused_computation.clone.1 | loop fusion | flops 23064576 | bytes 327680 | tf_op jit(solution)/shard_map/while/body/eval_jaxpr/reduce_sum | solution.py:30
  191.4 0.7 constant_dynamic-slice_fusion.4
  192.1 1.0 fusion.63
  193.5 4.4 %multiply_reduce_fusion.2 = f32[32,128]{1,0:T(8,128)S(1)} fusion(f32[32,4,128]{2,1,0:T(4,128)S(1)} %copy.88, f32[32,128]{1,0:T(8,128)S(1)} %get-tuple-element.135, f32[32,4,128]{2,1,0:T(4,128)S(1)} %copy.90, f32[32,128]{1,0:T(8,128)S(1)} %get-tuple-element.137, f32[32,4,128]{2,1,0:T(4,128)S(1)} %copy.91, f32[32,128]{1,0:T(8,128)S(1)} %get-tuple-element.139, ...), kind=kLoop, calls=%fused_computation.clone.1 | loop fusion | flops 23064576 | bytes 327680 | tf_op jit(solution)/shard_map/while/body/eval_jaxpr/reduce_sum | solution.py:30
  197.9 0.7 constant_dynamic-slice_fusion.4
  198.6 1.0 fusion.63
  200.0 4.4 %multiply_reduce_fusion.2 = f32[32,128]{1,0:T(8,128)S(1)} fusion(f32[32,4,128]{2,1,0:T(4,128)S(1)} %copy.88, f32[32,128]{1,0:T(8,128)S(1)} %get-tuple-element.135, f32[32,4,128]{2,1,0:T(4,128)S(1)} %copy.90, f32[32,128]{1,0:T(8,128)S(1)} %get-tuple-element.137, f32[32,4,128]{2,1,0:T(4,128)S(1)} %copy.91, f32[32,128]{1,0:T(8,128)S(1)} %get-tuple-element.139, ...), kind=kLoop, calls=%fused_computation.clone.1 | loop fusion | flops 23064576 | bytes 327680 | tf_op jit(solution)/shard_map/while/body/eval_jaxpr/reduce_sum | solution.py:30
  204.4 0.7 constant_dynamic-slice_fusion.4
  205.1 1.0 fusion.63
  206.5 4.4 %multiply_reduce_fusion.2 = f32[32,128]{1,0:T(8,128)S(1)} fusion(f32[32,4,128]{2,1,0:T(4,128)S(1)} %copy.88, f32[32,128]{1,0:T(8,128)S(1)} %get-tuple-element.135, f32[32,4,128]{2,1,0:T(4,128)S(1)} %copy.90, f32[32,128]{1,0:T(8,128)S(1)} %get-tuple-element.137, f32[32,4,128]{2,1,0:T(4,128)S(1)} %copy.91, f32[32,128]{1,0:T(8,128)S(1)} %get-tuple-element.139, ...), kind=kLoop, calls=%fused_computation.clone.1 | loop fusion | flops 23064576 | bytes 327680 | tf_op jit(solution)/shard_map/while/body/eval_jaxpr/reduce_sum | solution.py:30
  210.9 0.7 constant_dynamic-slice_fusion.4
  211.6 1.0 fusion.63
  213.0 4.4 %multiply_reduce_fusion.2 = f32[32,128]{1,0:T(8,128)S(1)} fusion(f32[32,4,128]{2,1,0:T(4,128)S(1)} %copy.88, f32[32,128]{1,0:T(8,128)S(1)} %get-tuple-element.135, f32[32,4,128]{2,1,0:T(4,128)S(1)} %copy.90, f32[32,128]{1,0:T(8,128)S(1)} %get-tuple-element.137, f32[32,4,128]{2,1,0:T(4,128)S(1)} %copy.91, f32[32,128]{1,0:T(8,128)S(1)} %get-tuple-element.139, ...), kind=kLoop, calls=%fused_computation.clone.1 | loop fusion | flops 23064576 | bytes 327680 | tf_op jit(solution)/shard_map/while/body/eval_jaxpr/reduce_sum | solution.py:30
  217.4 0.7 constant_dynamic-slice_fusion.4
  218.1 1.0 fusion.63
  219.4 4.4 %multiply_reduce_fusion.2 = f32[32,128]{1,0:T(8,128)S(1)} fusion(f32[32,4,128]{2,1,0:T(4,128)S(1)} %copy.88, f32[32,128]{1,0:T(8,128)S(1)} %get-tuple-element.135, f32[32,4,128]{2,1,0:T(4,128)S(1)} %copy.90, f32[32,128]{1,0:T(8,128)S(1)} %get-tuple-element.137, f32[32,4,128]{2,1,0:T(4,128)S(1)} %copy.91, f32[32,128]{1,0:T(8,128)S(1)} %get-tuple-element.139, ...), kind=kLoop, calls=%fused_computation.clone.1 | loop fusion | flops 23064576 | bytes 327680 | tf_op jit(solution)/shard_map/while/body/eval_jaxpr/reduce_sum | solution.py:30
  224.6 1.0 fusion.63
  225.9 4.4 %multiply_reduce_fusion.2 = f32[32,128]{1,0:T(8,128)S(1)} fusion(f32[32,4,128]{2,1,0:T(4,128)S(1)} %copy.88, f32[32,128]{1,0:T(8,128)S(1)} %get-tuple-element.135, f32[32,4,128]{2,1,0:T(4,128)S(1)} %copy.90, f32[32,128]{1,0:T(8,128)S(1)} %get-tuple-element.137, f32[32,4,128]{2,1,0:T(4,128)S(1)} %copy.91, f32[32,128]{1,0:T(8,128)S(1)} %get-tuple-element.139, ...), kind=kLoop, calls=%fused_computation.clone.1 | loop fusion | flops 23064576 | bytes 327680 | tf_op jit(solution)/shard_map/while/body/eval_jaxpr/reduce_sum | solution.py:30
  230.4 0.7 constant_dynamic-slice_fusion.4
  231.1 1.0 fusion.63
  232.4 4.4 %multiply_reduce_fusion.2 = f32[32,128]{1,0:T(8,128)S(1)} fusion(f32[32,4,128]{2,1,0:T(4,128)S(1)} %copy.88, f32[32,128]{1,0:T(8,128)S(1)} %get-tuple-element.135, f32[32,4,128]{2,1,0:T(4,128)S(1)} %copy.90, f32[32,128]{1,0:T(8,128)S(1)} %get-tuple-element.137, f32[32,4,128]{2,1,0:T(4,128)S(1)} %copy.91, f32[32,128]{1,0:T(8,128)S(1)} %get-tuple-element.139, ...), kind=kLoop, calls=%fused_computation.clone.1 | loop fusion | flops 23064576 | bytes 327680 | tf_op jit(solution)/shard_map/while/body/eval_jaxpr/reduce_sum | solution.py:30
  236.9 0.7 constant_dynamic-slice_fusion.4
  237.6 1.0 fusion.63
  238.9 4.4 %multiply_reduce_fusion.2 = f32[32,128]{1,0:T(8,128)S(1)} fusion(f32[32,4,128]{2,1,0:T(4,128)S(1)} %copy.88, f32[32,128]{1,0:T(8,128)S(1)} %get-tuple-element.135, f32[32,4,128]{2,1,0:T(4,128)S(1)} %copy.90, f32[32,128]{1,0:T(8,128)S(1)} %get-tuple-element.137, f32[32,4,128]{2,1,0:T(4,128)S(1)} %copy.91, f32[32,128]{1,0:T(8,128)S(1)} %get-tuple-element.139, ...), kind=kLoop, calls=%fused_computation.clone.1 | loop fusion | flops 23064576 | bytes 327680 | tf_op jit(solution)/shard_map/while/body/eval_jaxpr/reduce_sum | solution.py:30
  243.3 0.7 constant_dynamic-slice_fusion.4
  244.1 1.0 fusion.63
  245.4 4.4 %multiply_reduce_fusion.2 = f32[32,128]{1,0:T(8,128)S(1)} fusion(f32[32,4,128]{2,1,0:T(4,128)S(1)} %copy.88, f32[32,128]{1,0:T(8,128)S(1)} %get-tuple-element.135, f32[32,4,128]{2,1,0:T(4,128)S(1)} %copy.90, f32[32,128]{1,0:T(8,128)S(1)} %get-tuple-element.137, f32[32,4,128]{2,1,0:T(4,128)S(1)} %copy.91, f32[32,128]{1,0:T(8,128)S(1)} %get-tuple-element.139, ...), kind=kLoop, calls=%fused_computation.clone.1 | loop fusion | flops 23064576 | bytes 327680 | tf_op jit(solution)/shard_map/while/body/eval_jaxpr/reduce_sum | solution.py:30
  249.8 0.7 constant_dynamic-slice_fusion.4
  250.6 1.0 fusion.63
  251.9 4.4 %multiply_reduce_fusion.2 = f32[32,128]{1,0:T(8,128)S(1)} fusion(f32[32,4,128]{2,1,0:T(4,128)S(1)} %copy.88, f32[32,128]{1,0:T(8,128)S(1)} %get-tuple-element.135, f32[32,4,128]{2,1,0:T(4,128)S(1)} %copy.90, f32[32,128]{1,0:T(8,128)S(1)} %get-tuple-element.137, f32[32,4,128]{2,1,0:T(4,128)S(1)} %copy.91, f32[32,128]{1,0:T(8,128)S(1)} %get-tuple-element.139, ...), kind=kLoop, calls=%fused_computation.clone.1 | loop fusion | flops 23064576 | bytes 327680 | tf_op jit(solution)/shard_map/while/body/eval_jaxpr/reduce_sum | solution.py:30
  257.1 1.0 fusion.63
  258.4 4.4 %multiply_reduce_fusion.2 = f32[32,128]{1,0:T(8,128)S(1)} fusion(f32[32,4,128]{2,1,0:T(4,128)S(1)} %copy.88, f32[32,128]{1,0:T(8,128)S(1)} %get-tuple-element.135, f32[32,4,128]{2,1,0:T(4,128)S(1)} %copy.90, f32[32,128]{1,0:T(8,128)S(1)} %get-tuple-element.137, f32[32,4,128]{2,1,0:T(4,128)S(1)} %copy.91, f32[32,128]{1,0:T(8,128)S(1)} %get-tuple-element.139, ...), kind=kLoop, calls=%fused_computation.clone.1 | loop fusion | flops 23064576 | bytes 327680 | tf_op jit(solution)/shard_map/while/body/eval_jaxpr/reduce_sum | solution.py:30
  262.8 0.7 constant_dynamic-slice_fusion.4
  263.6 1.0 fusion.63
  264.9 4.4 %multiply_reduce_fusion.2 = f32[32,128]{1,0:T(8,128)S(1)} fusion(f32[32,4,128]{2,1,0:T(4,128)S(1)} %copy.88, f32[32,128]{1,0:T(8,128)S(1)} %get-tuple-element.135, f32[32,4,128]{2,1,0:T(4,128)S(1)} %copy.90, f32[32,128]{1,0:T(8,128)S(1)} %get-tuple-element.137, f32[32,4,128]{2,1,0:T(4,128)S(1)} %copy.91, f32[32,128]{1,0:T(8,128)S(1)} %get-tuple-element.139, ...), kind=kLoop, calls=%fused_computation.clone.1 | loop fusion | flops 23064576 | bytes 327680 | tf_op jit(solution)/shard_map/while/body/eval_jaxpr/reduce_sum | solution.py:30
  270.0 1.0 fusion.63
  271.4 4.4 %multiply_reduce_fusion.2 = f32[32,128]{1,0:T(8,128)S(1)} fusion(f32[32,4,128]{2,1,0:T(4,128)S(1)} %copy.88, f32[32,128]{1,0:T(8,128)S(1)} %get-tuple-element.135, f32[32,4,128]{2,1,0:T(4,128)S(1)} %copy.90, f32[32,128]{1,0:T(8,128)S(1)} %get-tuple-element.137, f32[32,4,128]{2,1,0:T(4,128)S(1)} %copy.91, f32[32,128]{1,0:T(8,128)S(1)} %get-tuple-element.139, ...), kind=kLoop, calls=%fused_computation.clone.1 | loop fusion | flops 23064576 | bytes 327680 | tf_op jit(solution)/shard_map/while/body/eval_jaxpr/reduce_sum | solution.py:30
  276.5 3.5 all-to-all-start.1
  280.1 1.4 fusion.14
  281.7 75.6 %psum.23 = f32[1024]{0:T(1024)S(1)} all-reduce(f32[1024]{0:T(1024)S(1)} %bitcast.156), channel_id=1, replica_groups=mesh['dom'=16,'grp'=16] {'dom','grp'}, use_global_device_ids=true, to_apply=%region_9.10 | all-reduce | flops 1024 | bytes 8192 | tf_op jit(solution)/shard_map/psum | solution.py:99
  357.9 1.3 convolution_add_fusion
  (208 shorter events, 14.6 us)
Async XLA Ops:
  7.2 157.8 %all-gather.3.cloned.1.call-start = ((), (), s32[]{:S(2)}) async-start(), calls=%async_computation.2 | async-start | bytes 2228224 | tf_op jit(solution)/shard_map/all_gather | solution.py:117
  13.7 23.8 %copy-start.10 = (s32[1,64]{1,0:T(1,128)S(1)}, s32[1,64]{1,0:T(1,128)}, u32[]{:S(2)}) copy-start(s32[1,64]{1,0:T(1,128)} %param.16) | copy-start | bytes 772
  37.1 1.8 copy-start
  37.1 1.8 copy-start.1
  37.1 2.2 copy-start.3
  37.5 3.8 %copy-start.6 = (s32[512,4]{0,1:T(4,128)S(1)}, s32[512,4]{0,1:T(4,128)}, u32[]{:S(2)}) copy-start(s32[512,4]{0,1:T(4,128)} %param.19) | copy-start | bytes 24580
  37.5 4.5 %copy-start.11 = (s32[1,16]{1,0:T(1,128)S(1)}, s32[1,16]{1,0:T(1,128)}, u32[]{:S(2)}) copy-start(s32[1,16]{1,0:T(1,128)} %param.18) | copy-start | bytes 196
  37.5 19.0 %copy-start.7 = (s32[1,16,16]{2,1,0:T(8,128)S(1)}, s32[1,16,16]{2,1,0:T(8,128)}, u32[]{:S(2)}) copy-start(s32[1,16,16]{2,1,0:T(8,128)} %param.17) | copy-start | bytes 3076
  39.3 125.7 %copy-start.12 = (s32[16]{0:T(128)}, s32[16]{0:T(128)S(1)}, u32[]{:S(2)}) copy-start(s32[16]{0:T(128)S(1)} %and_select_fusion) | copy-start | bytes 196
  39.4 125.6 %copy-start.4 = (s32[32768]{0:T(1024)}, s32[32768]{0:T(1024)S(1)}, u32[]{:S(2)}) copy-start(s32[32768]{0:T(1024)S(1)} %add_select_fusion) | copy-start | bytes 393220
  162.8 1.4 copy-start.8
  171.8 108.3 %copy-start.2 = (f32[32768]{0:T(1024)S(1)}, f32[32768]{0:T(1024)}, u32[]{:S(2)}) copy-start(f32[32768]{0:T(1024)} %multiply_multiply_fusion) | copy-start | bytes 393220
  171.8 108.3 %copy-start.5 = (s32[32768]{0:T(1024)S(1)}, s32[32768]{0:T(1024)}, u32[]{:S(2)}) copy-start(s32[32768]{0:T(1024)} %copy-done.4) | copy-start | bytes 393220
  171.8 109.7 %copy-start.13 = (s32[16]{0:T(128)S(1)}, s32[16]{0:T(128)}, u32[]{:S(2)}) copy-start(s32[16]{0:T(128)} %copy-done.12) | copy-start | bytes 196
  171.8 185.5 %copy-start.9 = (f32[1024]{0:T(1024)S(1)}, f32[1024]{0:T(1024)}, u32[]{:S(2)}) copy-start(f32[1024]{0:T(1024)} %copy-done.8) | copy-start | bytes 12292
  276.5 81.4 %all-to-all-start.1 = ((f32[16,32,128]{2,1,0:T(8,128)}), f32[16,32,128]{2,1,0:T(8,128)S(1)}, u32[]{:S(2)}, u32[]{:S(2)}) async-start(f32[16,32,128]{2,1,0:T(8,128)} %broadcast_multiply_fusion), calls=%async_computation.1 | async-start | bytes 524288 | tf_op jit(solution)/shard_map/all_to_all | solution.py:133
Sparse Core Ops, SparseCore 0:
  39.0 48.9 all-gather.2
where the time goes:
time: 367 us; the launch traced here: 366 us
  blocking collectives  219 us (60%)
  other arithmetic  77.5 us (21%)
  matrix products  26 us (7%)
  local copies, waits for them, and re-layouts  23.5 us (6%)
  between operations  14.4 us (4%)
    psum x1, blocking collectives, shards(): lax.psum((first_sums[0], first_sums[1:]), ('dom', 'grp'))  89 us
    psum x1, blocking collectives, shards(): lax.psum(group_sums((mass_flat * kinetic)[None, :])[0], ('dom', 'grp'))  75.6 us
    reduce_sum x16, other arithmetic, tile_potential(): return -jnp.sum(weights, axis=(1, 3))  70.1 us
    all_to_all x1, blocking collectives, shards(): lax.all_to_all(outgoing, 'grp', split_axis=0, concat_axis=0, tiled=True)  23.4 us
    dot_general x18, matrix products, select_rows(): jnp.dot(picker, flat, precision=exact, preferred_element_type=jnp.float32)  19.3 us
    all_gather x1, blocking collectives, shards(): lax.all_gather(send_list, 'grp', axis=0, tiled=True)  17.3 us
    all_gather x1, blocking collectives, shards(): lax.all_gather(send_count, 'grp', axis=0, tiled=True)  14.1 us
    dynamic_slice x48, local copies, waits for them, and re-layouts, slot_potential(): lax.map(one_block, (owned.reshape(slot_count // block_rows, block_rows, 4...  12.1 us
  transfers between devices with their start and end apart: 2, of which 0 were waited for; matrix products, arithmetic and copies ran while one was open for 2% of the time, Pallas kernels for 0%

commit v1 on v0

v1 whole, which is shorter than its diff:
```python
import jax
import jax.numpy as jnp
from jax import lax
from jax.sharding import PartitionSpec as P

GSPAN = 16
GROUP_DEV = 4


softening = 0.0025
exact = lax.Precision.HIGHEST


def tile_potential(targets, sources):
    distance = softening
    for component in range(3):
        offset = targets[:, None, component, :, None] - sources[:, :, component, None, :]
        distance = distance + offset * offset
    weights = sources[:, :, 3, None, :] * lax.rsqrt(distance)
    return -jnp.sum(weights, axis=(1, 3))


def group_totals(gathered):
    blocks, stats, span = gathered.shape
    split = gathered.reshape(blocks, stats, span // GROUP_DEV, GROUP_DEV)
    total = split[:, :, 0, :]
    for shift in range(1, span // GROUP_DEV):
        total = total + jnp.roll(split[:, :, shift, :], shift, axis=0)
    return jnp.transpose(total, (1, 0, 2)).reshape(stats, blocks * GROUP_DEV)


def shards(
    positions,
    velocities,
    masses,
    destination,
    group_ids,
    boundary_set,
    send_list,
    send_count,
    partners,
):
    owners = lax.axis_size("grp")
    leaves = positions.shape[0]
    leaf_width = positions.shape[2]
    capacity = 2 * leaves // owners
    slot_count = owners * capacity
    groups = GROUP_DEV * lax.axis_size("dom") * owners
    block_index = lax.axis_index("dom") * owners + lax.axis_index("grp")
    first_group = block_index * GROUP_DEV
    mass_flat = masses.reshape(-1)
    group_flat = group_ids.reshape(-1)
    speeds = jnp.transpose(velocities, (1, 0, 2)).reshape(3, -1)
    local_ids = (group_flat - first_group) % groups
    member = (jnp.arange(GSPAN, dtype=jnp.int32)[:, None] == local_ids[None, :]).astype(jnp.float32)

    def local_sums(stats):
        return jnp.einsum(
            "kp,gp->kg", stats, member, precision=exact, preferred_element_type=jnp.float32
        )

    def near_groups(table):
        doubled = jnp.concatenate([table, table[:, :GSPAN]], axis=1)
        return lax.dynamic_slice_in_dim(doubled, first_group, GSPAN, axis=1)

    first_sums = local_sums(jnp.concatenate([mass_flat[None, :], mass_flat[None, :] * speeds], axis=0))
    every_first = lax.all_gather(first_sums, ("dom", "grp"), axis=0, tiled=False)
    totals = group_totals(every_first)
    mass_total = totals[0]
    near = near_groups(totals)
    bulk_local = near[1:] / near[0:1]
    per_particle = jnp.dot(bulk_local, member, precision=exact, preferred_element_type=jnp.float32)
    relative = speeds - per_particle
    kinetic = 0.5 * jnp.sum(relative * relative, axis=0)
    heat_local = local_sums((mass_flat * kinetic)[None, :])
    every_heat = lax.all_gather(heat_local, ("dom", "grp"), axis=0, tiled=False)
    heat_sum = group_totals(every_heat)[0]
    group_kinetic = heat_sum / mass_total

    onehot = (destination[:, None] == jnp.arange(owners, dtype=jnp.int32)[None, :]).astype(jnp.int32)
    leaf_rank = jnp.sum((jnp.cumsum(onehot, axis=0) - onehot) * onehot, axis=1)
    target = destination * capacity + leaf_rank
    payload = jnp.concatenate([positions, masses[:, None, :]], axis=1)
    placing = (jnp.arange(slot_count, dtype=jnp.int32)[:, None] == target[None, :]).astype(jnp.float32)
    outgoing = jnp.dot(
        placing, payload.reshape(leaves, -1), precision=exact, preferred_element_type=jnp.float32
    ).reshape(slot_count, 4, leaf_width)
    owned = lax.all_to_all(outgoing, "grp", split_axis=0, concat_axis=0, tiled=True)

    per_peer = send_list.shape[2]
    pick = jnp.take(boundary_set[0], send_list[0], axis=0)
    live = jnp.arange(per_peer, dtype=jnp.int32)[None, :] < send_count[0][:, None]
    sending = jnp.take(owned, pick, axis=0)
    sending = jnp.where(live[:, :, None, None], sending, jnp.zeros_like(sending))
    remote = lax.all_to_all(sending, "grp", split_axis=0, concat_axis=0, tiled=True)
    remote = remote.reshape(owners * per_peer, 4, leaf_width)
    combined = jnp.concatenate([owned, remote], axis=0)

    coupling = 1.0 / (partners.shape[1] * leaf_width)
    sources = jnp.take(combined, partners, axis=0)
    potential = tile_potential(owned, sources) * coupling
    returned = lax.all_to_all(potential, "grp", split_axis=0, concat_axis=0, tiled=True)
    own_potential = jnp.take(returned, target, axis=0)
    energy = kinetic.reshape(leaves, leaf_width) + own_potential
    return (energy, group_kinetic)


def solution(mesh):
    in_specs = (
        P(("dom", "grp"), None, None),
        P(("dom", "grp"), None, None),
        P(("dom", "grp"), None),
        P(("dom", "grp")),
        P(("dom", "grp"), None),
        P(("dom", "grp"), None),
        P(("dom", "grp"), None, None),
        P(("dom", "grp"), None),
        P(("dom", "grp"), None),
    )
    out_specs = (P(("dom", "grp"), None), P())
    return jax.shard_map(shards, mesh=mesh, in_specs=in_specs, out_specs=out_specs, check_vma=False)
```

time: 367 us -> 358 us (0.975)
  matrix products: 26 us -> 4.79 us
  blocking collectives: 219 us -> 199 us
  waiting for transfers between devices: 0.02 us -> 14.9 us
  between operations: 14.4 us -> 1.11 us
  other arithmetic: 77.5 us -> 89.3 us
  starting transfers between devices: 3.57 us -> 14.9 us
  local copies, waits for them, and re-layouts: 23.5 us -> 32.3 us
    psum x2 -> x0, blocking collectives: 165 us -> none  [the longest x1 89 us: shards(): lax.psum((first_sums[0], first_sums[1:]), ('dom', 'grp'))]
    all_gather x2 -> x1, blocking collectives: 31.4 us -> 122 us  [shards(): lax.all_gather(first_sums, ('dom', 'grp'), axis=0, tiled=False)]
    unnamed x0 -> x1, blocking collectives: none -> 76.8 us
    all_to_all x1 -> x0, blocking collectives: 23.4 us -> none  [shards(): lax.all_to_all(outgoing, 'grp', split_axis=0, concat_axis=0, tiled=True)]
    dot_general x24 -> x2, matrix products: 24.2 us -> 3.01 us  [local_sums(): jnp.einsum('kp,gp->kg', stats, member, precision=exact, preferred_element...]
    gather x0 -> x6, local copies, waits for them, and re-layouts: none -> 19.1 us  [the longest x1 15.4 us: shards(): sources = jnp.take(combined, partners, axis=0)]
    dynamic_slice x48 -> x0, local copies, waits for them, and re-layouts: 12.1 us -> none  [slot_potential(): lax.map(one_block, (owned.reshape(slot_count // block_rows, block_rows, 4...]
    all_to_all x0 -> x2, starting transfers between devices: none -> 11.4 us  [the longest x1 7.58 us: shards(): lax.all_to_all(outgoing, 'grp', split_axis=0, concat_axis=0, tiled=True)]
  transfers between devices with their start and end apart: 2 -> 3, of which waited for: 0 -> 2; matrix products, arithmetic and copies ran while one was open for 2% -> 4% of each run, Pallas kernels for 0% -> 0%
where the time goes in v1:
time: 358 us; the launch traced here: 356 us
  blocking collectives  199 us (56%)
  other arithmetic  89.3 us (25%)
  local copies, waits for them, and re-layouts  32.3 us (9%)
  starting transfers between devices  14.9 us (4%)
  waiting for transfers between devices  14.9 us (4%)
  matrix products  4.79 us (1%)
    all_gather x1, blocking collectives, shards(): lax.all_gather(first_sums, ('dom', 'grp'), axis=0, tiled=False)  122 us
    unnamed x1, blocking collectives  76.8 us
    reduce_sum x1, other arithmetic, tile_potential(): return -jnp.sum(weights, axis=(1, 3))  71.1 us
    gather x1, local copies, waits for them, and re-layouts, shards(): sources = jnp.take(combined, partners, axis=0)  15.4 us
    select_n x2, other arithmetic, shards(): sources = jnp.take(combined, partners, axis=0)  10.1 us
    all_to_all x1, waiting for transfers between devices, shards(): lax.all_to_all(sending, 'grp', split_axis=0, concat_axis=0, tiled=True)  8.93 us
    all_to_all x1, starting transfers between devices, shards(): lax.all_to_all(outgoing, 'grp', split_axis=0, concat_axis=0, tiled=True)  7.58 us
  transfers between devices with their start and end apart: 3, of which 2 were waited for; matrix products, arithmetic and copies ran while one was open for 4% of the time, Pallas kernels for 0%

profile of v1, /device:TPU:1, one launch (start us, length us, event | category | flops | bytes accessed | tf_op | source)
XLA Modules:
  0.0 355.9 jit_solution(11283541280344338220)
XLA Ops:
  0.7 0.7 fusion.27
  1.4 0.6 reduce-window.6
  1.9 0.2 slice_reduce_fusion.1
  2.2 0.8 fusion.22
  2.9 0.7 compare_and_fusion.2
  3.6 1.0 copy.74
  4.6 1.2 copy.75
  5.8 0.6 fusion.12
  6.5 1.7 copy.76
  8.1 7.6 %all-to-all-start = ((f32[512,4,128]{2,1,0:T(4,128)}), f32[512,4,128]{2,1,0:T(4,128)S(1)}, u32[]{:S(2)}, u32[]{:S(2)}) async-start(f32[512,4,128]{2,1,0:T(4,128)} %copy.76), calls=%async_computation | async-start | bytes 2097152 | tf_op jit(solution)/shard_map/all_to_all | solution.py:88
  15.8 0.1 reshape.247
  15.9 1.9 gather_fusion
  17.8 0.1 gather.19
  17.9 0.1 reshape.246
  18.0 0.3 bitcast_multiply_fusion
  18.4 1.6 fusion.4
  20.0 121.9 %all-gather.2 = f32[256,4,16]{2,1,0:T(4,128)S(1)} all-gather(f32[1,4,16]{2,1,0:T(4,128)S(1)} %fusion.4), channel_id=2, replica_groups=mesh['dom'=16,'grp'=16] {'dom','grp'}, dimensions={0}, use_global_device_ids=true | all-gather | bytes 65792 | tf_op jit(solution)/shard_map/all_gather | solution.py:67
  141.9 0.2 copy.64
  142.1 0.1 slice_bitcast_fusion.7
  142.3 0.1 copy.65
  142.4 0.1 copy.66
  142.6 0.1 fusion.26
  142.7 0.2 copy.71
  142.9 0.3 reshape.240
  143.2 0.1 fusion.29
  143.3 1.1 fusion.3
  144.5 1.4 fusion.5
  145.9 0.2 dynamic-update-slice
  146.1 76.8 %all-reduce = f32[4096]{0:T(1024)S(1)} all-reduce(f32[4096]{0:T(1024)S(1)} %dynamic-update-slice), channel_id=3, replica_groups=mesh['dom'=16,'grp'=16] {'dom','grp'}, use_global_device_ids=true, to_apply=%add | all-reduce | flops 4096 | bytes 32768
  222.9 0.7 reshape.244
  223.6 0.1 slice_bitcast_fusion.1
  223.7 0.1 slice_bitcast_fusion
  223.9 0.1 reshape.255
  224.0 0.2 copy.73
  224.2 0.1 copy.79
  224.3 0.2 reshape.263
  224.5 0.1 copy.81
  224.6 0.1 squeeze.28
  224.8 0.8 maximum_reduce_fusion
  225.6 0.4 slice_reduce_fusion
  226.0 0.1 iota_compare_fusion.13
  226.1 0.1 slice_bitcast_fusion.2
  226.2 1.0 gather_fusion.1
  227.2 0.9 fusion.15
  228.1 3.8 %all-to-all-start.1 = ((f32[16,16,4,128]{3,1,2,0:T(8,128)}), f32[16,16,4,128]{3,1,2,0:T(8,128)S(1)}, u32[]{:S(2)}, u32[]{:S(2)}) async-start(f32[16,16,4,128]{3,1,2,0:T(8,128)} %fusion.15), calls=%async_computation.1 | async-start | bytes 1048576 | tf_op jit(solution)/shard_map/all_to_all | solution.py:95
  231.9 1.5 fusion.35
  233.4 8.9 %all-to-all-done.1 = f32[16,16,4,128]{3,1,2,0:T(8,128)S(1)} async-done(((f32[16,16,4,128]{3,1,2,0:T(8,128)}), f32[16,16,4,128]{3,1,2,0:T(8,128)S(1)}, u32[]{:S(2)}, u32[]{:S(2)}) %all-to-all-start.1) | async-done | bytes 524320 | tf_op jit(solution)/shard_map/all_to_all | solution.py:95
  242.3 0.2 copy.78
  242.6 0.3 pad_maximum_fusion
  242.9 15.4 %gather_fusion.2 = f32[2048,4,128]{2,1,0:T(4,128)} fusion(f32[768,4,128]{2,1,0:T(4,128)S(1)} %pad_maximum_fusion, s32[2048]{0:T(1024)S(1)} %broadcast_clamp_fusion), kind=kCustom, calls=%fused_computation.2 | custom fusion | bytes 8396800 | tf_op jit(solution)/shard_map/jit(_take)/gather | solution.py:100
  258.3 10.1 %broadcast_select_fusion = f32[512,4,4,128]{3,2,1,0:T(4,128)S(1)} fusion(f32[512,4,4,128]{3,2,1,0:T(4,128)} %bitcast.118, pred[512,4]{1,0:T(8,128)(4,1)S(1)} %copy.73), kind=kLoop, calls=%fused_computation.7 | loop fusion | flops 1048576 | bytes 8390656 | tf_op jit(solution)/shard_map/jit(_take)/select_n | solution.py:100
  268.4 3.1 fusion.34
  271.5 71.1 %multiply_reduce_fusion = f32[512,128]{1,0:T(8,128)S(1)} fusion(f32[512,4,128]{2,1,0:T(4,128)S(1)} %bitcast.125, f32[512,128]{1,0:T(8,128)S(1)} %bitcast.139, f32[512,4,128]{2,1,0:T(4,128)S(1)} %bitcast.126, f32[512,128]{1,0:T(8,128)S(1)} %bitcast.140, f32[512,4,128]{2,1,0:T(4,128)S(1)} %bitcast.127, f32[512,128]{1,0:T(8,128)S(1)} %bitcast.138, ...), kind=kLoop, calls=%fused_computation.4 | loop fusion | flops 369033216 | bytes 5242880 | tf_op jit(solution)/shard_map/reduce_sum | solution.py:20
  342.7 0.7 negate_multiply_fusion
  343.4 3.5 all-to-all-start.2
  346.9 0.4 maximum_reduce_fusion.2
  347.3 0.1 concatenate.78
  347.5 0.1 squeeze.27
  347.6 0.1 concatenate.70
  347.7 0.1 concatenate.74
  347.8 0.6 add_divide_fusion
  348.4 6.0 %all-to-all-done.2 = f32[16,32,128]{2,1,0:T(8,128)S(1)} async-done(((f32[16,32,128]{2,1,0:T(8,128)}), f32[16,32,128]{2,1,0:T(8,128)S(1)}, u32[]{:S(2)}, u32[]{:S(2)}) %all-to-all-start.2) | async-done | bytes 262176 | tf_op jit(solution)/shard_map/all_to_all | solution.py:102
  354.4 0.7 gather_fusion.3
  355.2 0.8 bitcast_add_fusion
  (46 shorter events, 0.4 us)
Async XLA Ops:
  0.6 15.2 %copy-start = (s32[1,64]{1,0:T(1,128)S(1)}, s32[1,64]{1,0:T(1,128)}, u32[]{:S(2)}) copy-start(s32[1,64]{1,0:T(1,128)} %param.14) | copy-start | bytes 772
  0.6 15.1 %copy-start.8 = (s32[512,4]{0,1:T(4,128)S(1)}, s32[512,4]{0,1:T(4,128)}, u32[]{:S(2)}) copy-start(s32[512,4]{0,1:T(4,128)} %param.17) | copy-start | bytes 24580
  0.7 15.1 %copy-start.7 = (s32[1,16,16]{2,1,0:T(8,128)S(1)}, s32[1,16,16]{2,1,0:T(8,128)}, u32[]{:S(2)}) copy-start(s32[1,16,16]{2,1,0:T(8,128)} %param.15) | copy-start | bytes 3076
  8.1 218.1 %all-to-all-start = ((f32[512,4,128]{2,1,0:T(4,128)}), f32[512,4,128]{2,1,0:T(4,128)S(1)}, u32[]{:S(2)}, u32[]{:S(2)}) async-start(f32[512,4,128]{2,1,0:T(4,128)} %copy.76), calls=%async_computation | async-start | bytes 2097152 | tf_op jit(solution)/shard_map/all_to_all | solution.py:88
  15.9 2.1 copy-start.6
  15.9 2.1 copy-start.1
  15.9 2.1 copy-start.2
  20.0 206.0 %copy-start.9 = (s32[1,16]{1,0:T(1,128)S(1)}, s32[1,16]{1,0:T(1,128)}, u32[]{:S(2)}) copy-start(s32[1,16]{1,0:T(1,128)} %param.16) | copy-start | bytes 196
  228.1 14.2 %all-to-all-start.1 = ((f32[16,16,4,128]{3,1,2,0:T(8,128)}), f32[16,16,4,128]{3,1,2,0:T(8,128)S(1)}, u32[]{:S(2)}, u32[]{:S(2)}) async-start(f32[16,16,4,128]{3,1,2,0:T(8,128)} %fusion.15), calls=%async_computation.1 | async-start | bytes 1048576 | tf_op jit(solution)/shard_map/all_to_all | solution.py:95
  268.3 3.2 copy-start.3
  268.4 3.2 copy-start.4
  268.4 3.2 copy-start.5
  343.4 11.0 %all-to-all-start.2 = ((f32[16,32,128]{2,1,0:T(8,128)}), f32[16,32,128]{2,1,0:T(8,128)S(1)}, u32[]{:S(2)}, u32[]{:S(2)}) async-start(f32[16,32,128]{2,1,0:T(8,128)} %bitcast.37), calls=%async_computation.2 | async-start | bytes 524288 | tf_op jit(solution)/shard_map/all_to_all | solution.py:102

commit v2 on v1

--- a/solution.py
+++ b/solution.py
@@ -18,15 +18,6 @@
         distance = distance + offset * offset
     weights = sources[:, :, 3, None, :] * lax.rsqrt(distance)
     return -jnp.sum(weights, axis=(1, 3))
-
-
-def group_totals(gathered):
-    blocks, stats, span = gathered.shape
-    split = gathered.reshape(blocks, stats, span // GROUP_DEV, GROUP_DEV)
-    total = split[:, :, 0, :]
-    for shift in range(1, span // GROUP_DEV):
-        total = total + jnp.roll(split[:, :, shift, :], shift, axis=0)
-    return jnp.transpose(total, (1, 0, 2)).reshape(stats, blocks * GROUP_DEV)
 
 
 def shards(
@@ -59,23 +50,39 @@
             "kp,gp->kg", stats, member, precision=exact, preferred_element_type=jnp.float32
         )
 
-    def near_groups(table):
-        doubled = jnp.concatenate([table, table[:, :GSPAN]], axis=1)
-        return lax.dynamic_slice_in_dim(doubled, first_group, GSPAN, axis=1)
+    blocks = lax.axis_size("dom") * owners
+    quarters = GSPAN // GROUP_DEV
+
+    def from_block(value, step):
+        if step == 0:
+            return value
+        ring = [(i, (i - step) % blocks) for i in range(blocks)]
+        return lax.ppermute(value, ("dom", "grp"), ring)
 
     first_sums = local_sums(jnp.concatenate([mass_flat[None, :], mass_flat[None, :] * speeds], axis=0))
-    every_first = lax.all_gather(first_sums, ("dom", "grp"), axis=0, tiled=False)
-    totals = group_totals(every_first)
-    mass_total = totals[0]
-    near = near_groups(totals)
+    near_sums = {step: from_block(first_sums, step) for step in range(-quarters + 1, quarters)}
+    near_parts = []
+    for ahead in range(quarters):
+        part = 0.0
+        for back in range(quarters):
+            part = part + near_sums[ahead - back][:, back * GROUP_DEV:(back + 1) * GROUP_DEV]
+        near_parts.append(part)
+    near = jnp.concatenate(near_parts, axis=1)
     bulk_local = near[1:] / near[0:1]
     per_particle = jnp.dot(bulk_local, member, precision=exact, preferred_element_type=jnp.float32)
     relative = speeds - per_particle
     kinetic = 0.5 * jnp.sum(relative * relative, axis=0)
-    heat_local = local_sums((mass_flat * kinetic)[None, :])
-    every_heat = lax.all_gather(heat_local, ("dom", "grp"), axis=0, tiled=False)
-    heat_sum = group_totals(every_heat)[0]
-    group_kinetic = heat_sum / mass_total
+    heat_local = local_sums((mass_flat * kinetic)[None, :])[0]
+    heat_own = heat_local[:GROUP_DEV]
+    for back in range(1, quarters):
+        heat_own = heat_own + from_block(heat_local[back * GROUP_DEV:(back + 1) * GROUP_DEV], -back)
+    kinetic_own = heat_own / near[0, :GROUP_DEV]
+    across = jnp.broadcast_to(kinetic_own[None, :], (owners, GROUP_DEV))
+    across = lax.all_to_all(across, "grp", split_axis=0, concat_axis=0, tiled=True)
+    domains = lax.axis_size("dom")
+    every = jnp.broadcast_to(across[None], (domains, owners, GROUP_DEV))
+    every = lax.all_to_all(every, "dom", split_axis=0, concat_axis=0, tiled=True)
+    group_kinetic = every.reshape(groups)
 
     onehot = (destination[:, None] == jnp.arange(owners, dtype=jnp.int32)[None, :]).astype(jnp.int32)
     leaf_rank = jnp.sum((jnp.cumsum(onehot, axis=0) - onehot) * onehot, axis=1)

time: 358 us -> 212 us (0.59)
  blocking collectives: 199 us -> 0 us
  starting transfers between devices: 14.9 us -> 45.9 us
  waiting for transfers between devices: 14.9 us -> 38.3 us
    all_gather x1 -> x0, blocking collectives: 122 us -> none  [shards(): lax.all_gather(first_sums, ('dom', 'grp'), axis=0, tiled=False)]
    unnamed x1 -> x0, blocking collectives: 76.8 us -> none
    ppermute x0 -> x9, waiting for transfers between devices: none -> 18.6 us  [from_block(): return lax.ppermute(value, ('dom', 'grp'), ring)]
    all_to_all x0 -> x2, starting transfers between devices: none -> 16.8 us  [the longest x1 12.9 us: shards(): lax.all_to_all(every, 'dom', split_axis=0, concat_axis=0, tiled=True)]
    ppermute x0 -> x9, starting transfers between devices: none -> 14.1 us  [from_block(): return lax.ppermute(value, ('dom', 'grp'), ring)]
    all_to_all x0 -> x2, waiting for transfers between devices: none -> 4.43 us  [the longest x1 4.42 us: shards(): lax.all_to_all(across, 'grp', split_axis=0, concat_axis=0, tiled=True)]
  transfers between devices with their start and end apart: 3 -> 14, of which waited for: 2 -> 6; matrix products, arithmetic and copies ran while one was open for 4% -> 56% of each run, Pallas kernels for 0% -> 0%
where the time goes in v2:
time: 212 us; the launch traced here: 211 us
  other arithmetic  89.4 us (42%)
  starting transfers between devices  45.9 us (22%)
  waiting for transfers between devices  38.3 us (18%)
  local copies, waits for them, and re-layouts  30.7 us (14%)
  matrix products  5.61 us (3%)
    reduce_sum x1, other arithmetic, tile_potential(): return -jnp.sum(weights, axis=(1, 3))  71.1 us
    ppermute x9, waiting for transfers between devices, from_block(): return lax.ppermute(value, ('dom', 'grp'), ring)  18.6 us
    gather x1, local copies, waits for them, and re-layouts, shards(): sources = jnp.take(combined, partners, axis=0)  15.4 us
    ppermute x9, starting transfers between devices, from_block(): return lax.ppermute(value, ('dom', 'grp'), ring)  14.1 us
    all_to_all x1, starting transfers between devices, shards(): lax.all_to_all(every, 'dom', split_axis=0, concat_axis=0, tiled=True)  12.9 us
    select_n x2, other arithmetic, shards(): sources = jnp.take(combined, partners, axis=0)  10.1 us
    all_to_all x1, starting transfers between devices, shards(): lax.all_to_all(outgoing, 'grp', split_axis=0, concat_axis=0, tiled=True)  7.92 us
    all_to_all x1, waiting for transfers between devices, shards(): lax.all_to_all(sending, 'grp', split_axis=0, concat_axis=0, tiled=True)  7.71 us
  transfers between devices with their start and end apart: 14, of which 6 were waited for; matrix products, arithmetic and copies ran while one was open for 56% of the time, Pallas kernels for 0%

profile of v2, /device:TPU:1, one launch (start us, length us, event | category | flops | bytes accessed | tf_op | source)
XLA Modules:
  0.0 211.0 jit_solution(5542695271476946327)
XLA Ops:
  0.6 0.0 copy-start
  0.7 1.0 add_select_fusion
  1.6 1.4 bitcast_multiply_fusion
  3.0 0.0 copy-start.5
  3.0 2.4 %fusion.2 = f32[4,16]{1,0:T(4,128)S(1)} fusion(s32[32768]{0:T(1024)S(1)} %add_select_fusion, f32[3,32768]{1,0:T(4,128)S(1)} %bitcast_multiply_fusion, f32[1,32768]{1,0:T(1,128)} %bitcast.86), kind=kOutput, calls=%fused_computation.10 | convolution fusion | flops 25821184 | bytes 655616 | tf_op jit(solution)/shard_map/kp,gp->kg/dot_general | solution.py:49
  5.4 6.6 %collective-permute-start.4 = (f32[4,16]{1,0:T(4,128)S(1)}, f32[4,16]{1,0:T(4,128)S(1)}, u32[]{:S(2)}, u32[]{:S(2)}) collective-permute-start(f32[4,16]{1,0:T(4,128)S(1)} %fusion.2), channel_id=1, source_target_pairs={{0,254},{1,255},{2,0},{3,1},{4,2},{5,3},{6,4},{7,5},{8,6},{9,7},{1... | collective-permute-start | bytes 776 | tf_op jit(solution)/shard_map/ppermute | solution.py:60
  12.0 0.8 collective-permute-start.5
  12.8 2.6 %collective-permute-start.3 = (f32[4,16]{1,0:T(4,128)S(1)}, f32[4,16]{1,0:T(4,128)S(1)}, u32[]{:S(2)}, u32[]{:S(2)}) collective-permute-start(f32[4,16]{1,0:T(4,128)S(1)} %fusion.2), channel_id=1, source_target_pairs={{0,255},{1,0},{2,1},{3,2},{4,3},{5,4},{6,5},{7,6},{8,7},{9,8},{10,... | collective-permute-start | bytes 776 | tf_op jit(solution)/shard_map/ppermute | solution.py:60
  15.5 1.0 collective-permute-start.1
  16.5 1.0 copy.34
  17.5 0.7 fusion.22
  18.2 0.6 reduce-window.6
  18.8 0.2 slice_reduce_fusion
  19.0 0.8 fusion.21
  19.8 0.7 compare_and_fusion.2
  20.5 1.2 copy.35
  21.6 0.6 fusion.11
  22.3 1.7 copy.36
  23.9 7.9 %all-to-all-start = ((f32[512,4,128]{2,1,0:T(4,128)}), f32[512,4,128]{2,1,0:T(4,128)S(1)}, u32[]{:S(2)}, u32[]{:S(2)}) async-start(f32[512,4,128]{2,1,0:T(4,128)} %copy.36), calls=%async_computation | async-start | bytes 2097152 | tf_op jit(solution)/shard_map/all_to_all | solution.py:95
  31.9 0.1 reshape.201
  32.0 0.0 copy-start.1
  32.0 1.9 gather_fusion
  33.9 0.1 gather.19
  34.0 0.1 reshape.200
  34.1 0.1 reshape.209
  34.2 0.1 iota_compare_fusion.11
  34.3 0.2 copy.33
  34.5 0.1 copy.39
  34.6 1.4 collective-permute-start
  36.1 0.2 reshape.217
  36.3 12.0 %collective-permute-done = f32[4,16]{1,0:T(4,128)S(1)} collective-permute-done((f32[4,16]{1,0:T(4,128)S(1)}, f32[4,16]{1,0:T(4,128)S(1)}, u32[]{:S(2)}, u32[]{:S(2)}) %collective-permute-start) | collective-permute-done | bytes 288 | tf_op jit(solution)/shard_map/ppermute | solution.py:60
  48.3 0.1 slice_add_fusion.3
  48.4 0.1 pad_maximum_fusion.1
  48.4 1.1 fusion.3
  49.6 1.4 fusion.4
  51.0 0.1 fusion.30
  51.1 0.2 collective-permute-start.6
  51.3 1.4 collective-permute-start.8
  52.7 4.9 %collective-permute-done.6 = f32[4]{0:T(128)S(1)} collective-permute-done((f32[4]{0:T(128)S(1)}, f32[4]{0:T(128)S(1)}, u32[]{:S(2)}, u32[]{:S(2)}) %collective-permute-start.6) | collective-permute-done | bytes 48 | tf_op jit(solution)/shard_map/ppermute | solution.py:60
  57.6 1.7 collective-permute-done.7
  59.3 0.6 broadcast_in_dim.92
  59.9 3.9 %all-to-all-start.3 = ((f32[16,1,4]{2,1,0:T(1,128)}), f32[16,1,4]{2,1,0:T(1,128)S(1)}, u32[]{:S(2)}, u32[]{:S(2)}) async-start(f32[16,1,4]{2,1,0:T(1,128)} %broadcast_in_dim.92), calls=%async_computation.3 | async-start | bytes 16384 | tf_op jit(solution)/shard_map/all_to_all | solution.py:81
  63.8 1.0 gather_fusion.1
  64.8 0.9 fusion.14
  65.8 4.4 %all-to-all-done.3 = f32[16,1,4]{2,1,0:T(1,128)S(1)} async-done(((f32[16,1,4]{2,1,0:T(1,128)}), f32[16,1,4]{2,1,0:T(1,128)S(1)}, u32[]{:S(2)}, u32[]{:S(2)}) %all-to-all-start.3) | async-done | bytes 288 | tf_op jit(solution)/shard_map/all_to_all | solution.py:81
  70.2 3.6 %all-to-all-start.1 = ((f32[16,16,4,128]{3,1,2,0:T(8,128)}), f32[16,16,4,128]{3,1,2,0:T(8,128)S(1)}, u32[]{:S(2)}, u32[]{:S(2)}) async-start(f32[16,16,4,128]{3,1,2,0:T(8,128)} %fusion.14), calls=%async_computation.1 | async-start | bytes 1048576 | tf_op jit(solution)/shard_map/all_to_all | solution.py:102
  73.8 0.1 copy.40
  73.9 1.3 fusion.29
  75.1 7.7 %all-to-all-done.1 = f32[16,16,4,128]{3,1,2,0:T(8,128)S(1)} async-done(((f32[16,16,4,128]{3,1,2,0:T(8,128)}), f32[16,16,4,128]{3,1,2,0:T(8,128)S(1)}, u32[]{:S(2)}, u32[]{:S(2)}) %all-to-all-start.1) | async-done | bytes 524320 | tf_op jit(solution)/shard_map/all_to_all | solution.py:102
  82.8 0.6 broadcast_in_dim.94
  83.4 12.9 %all-to-all-start.4 = ((f32[16,16,4]{1,2,0:T(4,128)}), f32[16,16,4]{1,2,0:T(4,128)S(1)}, u32[]{:S(2)}, u32[]{:S(2)}) async-start(f32[16,16,4]{1,2,0:T(4,128)} %broadcast_in_dim.94), calls=%async_computation.4 | async-start | bytes 65536 | tf_op jit(solution)/shard_map/all_to_all | solution.py:84
  96.4 0.2 copy.38
  96.6 0.3 pad_maximum_fusion
  96.9 15.4 %gather_fusion.2 = f32[2048,4,128]{2,1,0:T(4,128)} fusion(f32[768,4,128]{2,1,0:T(4,128)S(1)} %pad_maximum_fusion, s32[2048]{0:T(1024)S(1)} %broadcast_clamp_fusion), kind=kCustom, calls=%fused_computation.2 | custom fusion | bytes 8396800 | tf_op jit(solution)/shard_map/jit(_take)/gather | solution.py:107
  112.3 10.1 %broadcast_select_fusion = f32[512,4,4,128]{3,2,1,0:T(4,128)S(1)} fusion(f32[512,4,4,128]{3,2,1,0:T(4,128)} %bitcast.81, pred[512,4]{1,0:T(8,128)(4,1)S(1)} %copy.33), kind=kLoop, calls=%fused_computation.7 | loop fusion | flops 1048576 | bytes 8390656 | tf_op jit(solution)/shard_map/jit(_take)/select_n | solution.py:107
  122.4 3.1 %fusion.28 = (f32[512,4,1,128]{3,2,1,0:T(1,128)S(1)}, f32[512,4,1,128]{3,2,1,0:T(1,128)S(1)}, f32[512,4,1,128]{3,2,1,0:T(1,128)S(1)}, f32[512,4,1,128]{3,2,1,0:T(1,128)S(1)}) fusion(f32[512,4,4,128]{3,2,1,0:T(4,128)S(1)} %broadcast_select_fusion), kind=kLoop, calls=%fused_computation.73 | loop fusion | bytes 8388608 | tf_op jit(solution)/shard_map/slice | solution.py:19
  125.6 71.1 %multiply_reduce_fusion = f32[512,128]{1,0:T(8,128)S(1)} fusion(f32[512,4,128]{2,1,0:T(4,128)S(1)} %bitcast.88, f32[512,128]{1,0:T(8,128)S(1)} %bitcast.95, f32[512,4,128]{2,1,0:T(4,128)S(1)} %bitcast.89, f32[512,128]{1,0:T(8,128)S(1)} %bitcast.96, f32[512,4,128]{2,1,0:T(4,128)S(1)} %bitcast.90, f32[512,128]{1,0:T(8,128)S(1)} %bitcast.94, ...), kind=kLoop, calls=%fused_computation.4 | loop fusion | flops 369033216 | bytes 5242880 | tf_op jit(solution)/shard_map/reduce_sum | solution.py:20
  196.7 0.7 negate_multiply_fusion
  197.4 3.5 %all-to-all-start.2 = ((f32[16,32,128]{2,1,0:T(8,128)}), f32[16,32,128]{2,1,0:T(8,128)S(1)}, u32[]{:S(2)}, u32[]{:S(2)}) async-start(f32[16,32,128]{2,1,0:T(8,128)} %bitcast.27), calls=%async_computation.2 | async-start | bytes 524288 | tf_op jit(solution)/shard_map/all_to_all | solution.py:109
  201.0 0.2 copy.41
  201.2 0.7 reshape.198
  201.9 7.6 %all-to-all-done.2 = f32[16,32,128]{2,1,0:T(8,128)S(1)} async-done(((f32[16,32,128]{2,1,0:T(8,128)}), f32[16,32,128]{2,1,0:T(8,128)S(1)}, u32[]{:S(2)}, u32[]{:S(2)}) %all-to-all-start.2) | async-done | bytes 262176 | tf_op jit(solution)/shard_map/all_to_all | solution.py:109
  209.5 0.7 gather_fusion.3
  210.2 0.8 bitcast_add_fusion
  (35 shorter events, 0.2 us)
Async XLA Ops:
  0.6 31.4 %copy-start = (s32[1,64]{1,0:T(1,128)S(1)}, s32[1,64]{1,0:T(1,128)}, u32[]{:S(2)}) copy-start(s32[1,64]{1,0:T(1,128)} %param.14) | copy-start | bytes 772
  3.0 28.9 %copy-start.5 = (s32[512,4]{0,1:T(4,128)S(1)}, s32[512,4]{0,1:T(4,128)}, u32[]{:S(2)}) copy-start(s32[512,4]{0,1:T(4,128)} %param.17) | copy-start | bytes 24580
  3.0 28.9 %copy-start.4 = (s32[1,16,16]{2,1,0:T(8,128)S(1)}, s32[1,16,16]{2,1,0:T(8,128)}, u32[]{:S(2)}) copy-start(s32[1,16,16]{2,1,0:T(8,128)} %param.15) | copy-start | bytes 3076
  5.4 29.2 %collective-permute-start.4 = (f32[4,16]{1,0:T(4,128)S(1)}, f32[4,16]{1,0:T(4,128)S(1)}, u32[]{:S(2)}, u32[]{:S(2)}) collective-permute-start(f32[4,16]{1,0:T(4,128)S(1)} %fusion.2), channel_id=1, source_target_pairs={{0,254},{1,255},{2,0},{3,1},{4,2},{5,3},{6,4},{7,5},{8,6},{9,7},{1... | collective-permute-start | bytes 776 | tf_op jit(solution)/shard_map/ppermute | solution.py:60
  12.0 24.2 %collective-permute-start.5 = (f32[4,16]{1,0:T(4,128)S(1)}, f32[4,16]{1,0:T(4,128)S(1)}, u32[]{:S(2)}, u32[]{:S(2)}) collective-permute-start(f32[4,16]{1,0:T(4,128)S(1)} %fusion.2), channel_id=1, source_target_pairs={{0,253},{1,254},{2,255},{3,0},{4,1},{5,2},{6,3},{7,4},{8,5},{9,6},... | collective-permute-start | bytes 776 | tf_op jit(solution)/shard_map/ppermute | solution.py:60
  12.8 23.4 %collective-permute-start.3 = (f32[4,16]{1,0:T(4,128)S(1)}, f32[4,16]{1,0:T(4,128)S(1)}, u32[]{:S(2)}, u32[]{:S(2)}) collective-permute-start(f32[4,16]{1,0:T(4,128)S(1)} %fusion.2), channel_id=1, source_target_pairs={{0,255},{1,0},{2,1},{3,2},{4,3},{5,4},{6,5},{7,6},{8,7},{9,8},{10,... | collective-permute-start | bytes 776 | tf_op jit(solution)/shard_map/ppermute | solution.py:60
  15.4 20.8 %collective-permute-start.2 = (f32[4,16]{1,0:T(4,128)S(1)}, f32[4,16]{1,0:T(4,128)S(1)}, u32[]{:S(2)}, u32[]{:S(2)}) collective-permute-start(f32[4,16]{1,0:T(4,128)S(1)} %fusion.2), channel_id=1, source_target_pairs={{0,3},{1,4},{2,5},{3,6},{4,7},{5,8},{6,9},{7,10},{8,11},{9,12},{10... | collective-permute-start | bytes 776 | tf_op jit(solution)/shard_map/ppermute | solution.py:60
  15.5 20.8 %collective-permute-start.1 = (f32[4,16]{1,0:T(4,128)S(1)}, f32[4,16]{1,0:T(4,128)S(1)}, u32[]{:S(2)}, u32[]{:S(2)}) collective-permute-start(f32[4,16]{1,0:T(4,128)S(1)} %fusion.2), channel_id=1, source_target_pairs={{0,2},{1,3},{2,4},{3,5},{4,6},{5,7},{6,8},{7,9},{8,10},{9,11},{10,... | collective-permute-start | bytes 776 | tf_op jit(solution)/shard_map/ppermute | solution.py:60
  23.9 35.4 %all-to-all-start = ((f32[512,4,128]{2,1,0:T(4,128)}), f32[512,4,128]{2,1,0:T(4,128)S(1)}, u32[]{:S(2)}, u32[]{:S(2)}) async-start(f32[512,4,128]{2,1,0:T(4,128)} %copy.36), calls=%async_computation | async-start | bytes 2097152 | tf_op jit(solution)/shard_map/all_to_all | solution.py:95
  32.0 2.2 %copy-start.6 = (s32[1,16]{1,0:T(1,128)S(1)}, s32[1,16]{1,0:T(1,128)}, u32[]{:S(2)}) copy-start(s32[1,16]{1,0:T(1,128)} %param.16) | copy-start | bytes 196
  32.0 16.4 %copy-start.2 = (f32[256,3,128]{2,0,1:T(8,128)S(1)}, f32[256,3,128]{2,0,1:T(8,128)}, u32[]{:S(2)}) copy-start(f32[256,3,128]{2,0,1:T(8,128)} %param.10) | copy-start | bytes 1179652
  32.0 17.6 %copy-start.1 = (f32[256,128]{1,0:T(8,128)S(1)}, f32[256,128]{1,0:T(8,128)}, u32[]{:S(2)}) copy-start(f32[256,128]{1,0:T(8,128)} %param.11) | copy-start | bytes 393220
  34.6 13.7 %collective-permute-start = (f32[4,16]{1,0:T(4,128)S(1)}, f32[4,16]{1,0:T(4,128)S(1)}, u32[]{:S(2)}, u32[]{:S(2)}) collective-permute-start(f32[4,16]{1,0:T(4,128)S(1)} %fusion.2), channel_id=1, source_target_pairs={{0,1},{1,2},{2,3},{3,4},{4,5},{5,6},{6,7},{7,8},{8,9},{9,10},{10,1... | collective-permute-start | bytes 776 | tf_op jit(solution)/shard_map/ppermute | solution.py:60
  51.1 6.5 %collective-permute-start.6 = (f32[4]{0:T(128)S(1)}, f32[4]{0:T(128)S(1)}, u32[]{:S(2)}, u32[]{:S(2)}) collective-permute-start(f32[4]{0:T(128)S(1)} %get-tuple-element.15), channel_id=1, source_target_pairs={{0,1},{1,2},{2,3},{3,4},{4,5},{5,6},{6,7},{7,8},{8,9},{9,10},{10,1... | collective-permute-start | bytes 56 | tf_op jit(solution)/shard_map/ppermute | solution.py:60
  51.3 6.3 %collective-permute-start.8 = (f32[4]{0:T(128)S(1)}, f32[4]{0:T(128)S(1)}, u32[]{:S(2)}, u32[]{:S(2)}) collective-permute-start(f32[4]{0:T(128)S(1)} %get-tuple-element.16), channel_id=1, source_target_pairs={{0,3},{1,4},{2,5},{3,6},{4,7},{5,8},{6,9},{7,10},{8,11},{9,12},{10... | collective-permute-start | bytes 56 | tf_op jit(solution)/shard_map/ppermute | solution.py:60
  52.7 6.6 %collective-permute-start.7 = (f32[4]{0:T(128)S(1)}, f32[4]{0:T(128)S(1)}, u32[]{:S(2)}, u32[]{:S(2)}) collective-permute-start(f32[4]{0:T(128)S(1)} %get-tuple-element.17), channel_id=1, source_target_pairs={{0,2},{1,3},{2,4},{3,5},{4,6},{5,7},{6,8},{7,9},{8,10},{9,11},{10,... | collective-permute-start | bytes 56 | tf_op jit(solution)/shard_map/ppermute | solution.py:60
  59.9 10.3 %all-to-all-start.3 = ((f32[16,1,4]{2,1,0:T(1,128)}), f32[16,1,4]{2,1,0:T(1,128)S(1)}, u32[]{:S(2)}, u32[]{:S(2)}) async-start(f32[16,1,4]{2,1,0:T(1,128)} %broadcast_in_dim.92), calls=%async_computation.3 | async-start | bytes 16384 | tf_op jit(solution)/shard_map/all_to_all | solution.py:81
  70.2 12.6 %all-to-all-start.1 = ((f32[16,16,4,128]{3,1,2,0:T(8,128)}), f32[16,16,4,128]{3,1,2,0:T(8,128)S(1)}, u32[]{:S(2)}, u32[]{:S(2)}) async-start(f32[16,16,4,128]{3,1,2,0:T(8,128)} %fusion.14), calls=%async_computation.1 | async-start | bytes 1048576 | tf_op jit(solution)/shard_map/all_to_all | solution.py:102
  83.4 114.0 %all-to-all-start.4 = ((f32[16,16,4]{1,2,0:T(4,128)}), f32[16,16,4]{1,2,0:T(4,128)S(1)}, u32[]{:S(2)}, u32[]{:S(2)}) async-start(f32[16,16,4]{1,2,0:T(4,128)} %broadcast_in_dim.94), calls=%async_computation.4 | async-start | bytes 65536 | tf_op jit(solution)/shard_map/all_to_all | solution.py:84
  122.4 3.1 %copy-start.3 = (f32[512,1,128]{2,1,0:T(1,128)S(1)}, f32[512,1,128]{2,1,0:T(1,128)}, u32[]{:S(2)}) copy-start(f32[512,1,128]{2,1,0:T(1,128)} %get-tuple-element.10) | copy-start | bytes 786436
  197.4 12.0 %all-to-all-start.2 = ((f32[16,32,128]{2,1,0:T(8,128)}), f32[16,32,128]{2,1,0:T(8,128)S(1)}, u32[]{:S(2)}, u32[]{:S(2)}) async-start(f32[16,32,128]{2,1,0:T(8,128)} %bitcast.27), calls=%async_computation.2 | async-start | bytes 524288 | tf_op jit(solution)/shard_map/all_to_all | solution.py:109

commit v3 on v2

--- a/solution.py
+++ b/solution.py
@@ -50,6 +50,25 @@
             "kp,gp->kg", stats, member, precision=exact, preferred_element_type=jnp.float32
         )
 
+    onehot = (destination[:, None] == jnp.arange(owners, dtype=jnp.int32)[None, :]).astype(jnp.int32)
+    leaf_rank = jnp.sum((jnp.cumsum(onehot, axis=0) - onehot) * onehot, axis=1)
+    target = destination * capacity + leaf_rank
+    payload = jnp.concatenate([positions, masses[:, None, :]], axis=1)
+    placing = (jnp.arange(slot_count, dtype=jnp.int32)[:, None] == target[None, :]).astype(jnp.float32)
+    outgoing = jnp.dot(
+        placing, payload.reshape(leaves, -1), precision=exact, preferred_element_type=jnp.float32
+    ).reshape(slot_count, 4, leaf_width)
+    owned = lax.all_to_all(outgoing, "grp", split_axis=0, concat_axis=0, tiled=True)
+
+    per_peer = send_list.shape[2]
+    pick = boundary_set[0].at[send_list[0]].get(mode="promise_in_bounds")
+    live = jnp.arange(per_peer, dtype=jnp.int32)[None, :] < send_count[0][:, None]
+    sending = owned.at[pick].get(mode="promise_in_bounds")
+    sending = jnp.where(live[:, :, None, None], sending, jnp.zeros_like(sending))
+    remote = lax.all_to_all(sending, "grp", split_axis=0, concat_axis=0, tiled=True)
+    remote = remote.reshape(owners * per_peer, 4, leaf_width)
+    combined = jnp.concatenate([owned, remote], axis=0)
+
     blocks = lax.axis_size("dom") * owners
     quarters = GSPAN // GROUP_DEV
 
@@ -60,6 +79,7 @@
         return lax.ppermute(value, ("dom", "grp"), ring)
 
     first_sums = local_sums(jnp.concatenate([mass_flat[None, :], mass_flat[None, :] * speeds], axis=0))
+    first_sums, remote = lax.optimization_barrier((first_sums, remote))
     near_sums = {step: from_block(first_sums, step) for step in range(-quarters + 1, quarters)}
     near_parts = []
     for ahead in range(quarters):
@@ -84,30 +104,11 @@
     every = lax.all_to_all(every, "dom", split_axis=0, concat_axis=0, tiled=True)
     group_kinetic = every.reshape(groups)
 
-    onehot = (destination[:, None] == jnp.arange(owners, dtype=jnp.int32)[None, :]).astype(jnp.int32)
-    leaf_rank = jnp.sum((jnp.cumsum(onehot, axis=0) - onehot) * onehot, axis=1)
-    target = destination * capacity + leaf_rank
-    payload = jnp.concatenate([positions, masses[:, None, :]], axis=1)
-    placing = (jnp.arange(slot_count, dtype=jnp.int32)[:, None] == target[None, :]).astype(jnp.float32)
-    outgoing = jnp.dot(
-        placing, payload.reshape(leaves, -1), precision=exact, preferred_element_type=jnp.float32
-    ).reshape(slot_count, 4, leaf_width)
-    owned = lax.all_to_all(outgoing, "grp", split_axis=0, concat_axis=0, tiled=True)
-
-    per_peer = send_list.shape[2]
-    pick = jnp.take(boundary_set[0], send_list[0], axis=0)
-    live = jnp.arange(per_peer, dtype=jnp.int32)[None, :] < send_count[0][:, None]
-    sending = jnp.take(owned, pick, axis=0)
-    sending = jnp.where(live[:, :, None, None], sending, jnp.zeros_like(sending))
-    remote = lax.all_to_all(sending, "grp", split_axis=0, concat_axis=0, tiled=True)
-    remote = remote.reshape(owners * per_peer, 4, leaf_width)
-    combined = jnp.concatenate([owned, remote], axis=0)
-
     coupling = 1.0 / (partners.shape[1] * leaf_width)
-    sources = jnp.take(combined, partners, axis=0)
+    sources = combined.at[partners].get(mode="promise_in_bounds")
     potential = tile_potential(owned, sources) * coupling
     returned = lax.all_to_all(potential, "grp", split_axis=0, concat_axis=0, tiled=True)
-    own_potential = jnp.take(returned, target, axis=0)
+    own_potential = returned.at[target].get(mode="promise_in_bounds")
     energy = kinetic.reshape(leaves, leaf_width) + own_potential
     return (energy, group_kinetic)
 

time: 212 us -> 213 us (level)
  local copies, waits for them, and re-layouts: 30.7 us -> 38.9 us
  other arithmetic: 89.4 us -> 82.3 us
    ppermute x9, waiting for transfers between devices: 18.6 us -> 5.12 us  [from_block(): return lax.ppermute(value, ('dom', 'grp'), ring)]
    all_to_all x1, waiting for transfers between devices: 0.01 us -> 11.3 us  [shards(): lax.all_to_all(outgoing, 'grp', split_axis=0, concat_axis=0, tiled=True)]
    select_n x5 -> x4, other arithmetic: 10.1 us -> 0.7 us  [the longest x1 0.68 us: shards(): own_potential = returned.at[target].get(mode='promise_in_bounds')]
    slice x1, local copies, waits for them, and re-layouts: 3.12 us -> 11.2 us  [tile_potential(): weights = sources[:, :, 3, None, :] * lax.rsqrt(distance)]
    all_to_all x1, waiting for transfers between devices: 0.01 us -> 5.72 us  [shards(): lax.all_to_all(every, 'dom', split_axis=0, concat_axis=0, tiled=True)]
    all_to_all x1, waiting for transfers between devices: 4.42 us -> 0.01 us  [shards(): lax.all_to_all(across, 'grp', split_axis=0, concat_axis=0, tiled=True)]
    all_to_all x1, starting transfers between devices: 3.91 us -> 8.16 us  [shards(): lax.all_to_all(across, 'grp', split_axis=0, concat_axis=0, tiled=True)]
    reduce_sum x1, other arithmetic: 71.1 us -> 75.2 us  [tile_potential(): return -jnp.sum(weights, axis=(1, 3))]
  transfers between devices with their start and end apart: 14 -> 14, of which waited for: 6 -> 7; matrix products, arithmetic and copies ran while one was open for 56% -> 52% of each run, Pallas kernels for 0% -> 0%
where the time goes in v3:
time: 213 us
  other arithmetic  82.3 us (39%)
  starting transfers between devices  48 us (23%)
  local copies, waits for them, and re-layouts  38.9 us (18%)
  waiting for transfers between devices  37.8 us (18%)
  matrix products  4.81 us (2%)
    reduce_sum x1, other arithmetic, tile_potential(): return -jnp.sum(weights, axis=(1, 3))  75.2 us
    gather x1, local copies, waits for them, and re-layouts, shards(): sources = combined.at[partners].get(mode='promise_in_bounds')  15.4 us
    ppermute x9, starting transfers between devices, from_block(): return lax.ppermute(value, ('dom', 'grp'), ring)  11.6 us
    all_to_all x1, waiting for transfers between devices, shards(): lax.all_to_all(outgoing, 'grp', split_axis=0, concat_axis=0, tiled=True)  11.3 us
    slice x1, local copies, waits for them, and re-layouts, tile_potential(): weights = sources[:, :, 3, None, :] * lax.rsqrt(distance)  11.2 us
    all_to_all x1, starting transfers between devices, shards(): lax.all_to_all(every, 'dom', split_axis=0, concat_axis=0, tiled=True)  9.65 us
    all_to_all x1, waiting for transfers between devices, shards(): lax.all_to_all(sending, 'grp', split_axis=0, concat_axis=0, tiled=True)  8.38 us
    all_to_all x1, starting transfers between devices, shards(): lax.all_to_all(across, 'grp', split_axis=0, concat_axis=0, tiled=True)  8.16 us
  transfers between devices with their start and end apart: 14, of which 7 were waited for; matrix products, arithmetic and copies ran while one was open for 52% of the time, Pallas kernels for 0%

profile of v3, /device:TPU:1, one launch (start us, length us, event | category | flops | bytes accessed | tf_op | source)
XLA Modules:
  0.0 212.7 jit_solution(18232095749616010300)
XLA Ops:
  0.6 0.0 copy-start
  0.7 0.7 fusion.21
  1.4 0.6 reduce-window.6
  1.9 0.2 slice_reduce_fusion
  2.2 0.8 fusion.20
  2.9 0.7 compare_select_fusion.3
  3.6 1.0 copy.30
  4.6 1.2 copy.31
  5.8 0.6 fusion.11
  6.4 1.7 copy.32
  8.1 7.6 %all-to-all-start = ((f32[512,4,128]{2,1,0:T(4,128)}), f32[512,4,128]{2,1,0:T(4,128)S(1)}, u32[]{:S(2)}, u32[]{:S(2)}) async-start(f32[512,4,128]{2,1,0:T(4,128)} %copy.32), calls=%async_computation | async-start | bytes 2097152 | tf_op jit(solution)/shard_map/all_to_all | solution.py:61
  15.7 0.1 iota_compare_fusion.11
  15.8 0.1 reshape.156
  15.9 0.0 copy-start.6
  15.9 0.0 copy-start.4
  15.9 1.9 gather_fusion
  17.8 0.1 gather.15
  17.9 0.1 reshape.164
  18.0 0.1 copy.35
  18.2 0.2 reshape.172
  18.4 0.3 bitcast_multiply_fusion
  18.7 0.1 add_select_fusion
  18.8 1.6 fusion.2
  20.4 11.3 %all-to-all-done = f32[512,4,128]{2,1,0:T(4,128)S(1)} async-done(((f32[512,4,128]{2,1,0:T(4,128)}), f32[512,4,128]{2,1,0:T(4,128)S(1)}, u32[]{:S(2)}, u32[]{:S(2)}) %all-to-all-start) | async-done | bytes 1048608 | tf_op jit(solution)/shard_map/all_to_all | solution.py:61
  31.7 1.0 gather_fusion.1
  32.7 0.9 copy_select_fusion
  33.6 4.2 %all-to-all-start.1 = ((f32[16,16,4,128]{3,1,2,0:T(8,128)}), f32[16,16,4,128]{3,1,2,0:T(8,128)S(1)}, u32[]{:S(2)}, u32[]{:S(2)}) async-start(f32[16,16,4,128]{3,1,2,0:T(8,128)} %copy_select_fusion), calls=%async_computation.1 | async-start | bytes 1048576 | tf_op jit(solution)/shard_map/all_to_all | solution.py:68
  37.9 1.5 fusion.28
  39.4 8.4 %all-to-all-done.1 = f32[16,16,4,128]{3,1,2,0:T(8,128)S(1)} async-done(((f32[16,16,4,128]{3,1,2,0:T(8,128)}), f32[16,16,4,128]{3,1,2,0:T(8,128)S(1)}, u32[]{:S(2)}, u32[]{:S(2)}) %all-to-all-start.1) | async-done | bytes 524320 | tf_op jit(solution)/shard_map/all_to_all | solution.py:68
  47.7 0.2 copy.34
  47.9 3.7 %collective-permute-start.4 = (f32[4,16]{1,0:T(4,128)S(1)}, f32[4,16]{1,0:T(4,128)S(1)}, u32[]{:S(2)}, u32[]{:S(2)}) collective-permute-start(f32[4,16]{1,0:T(4,128)S(1)} %fusion.2), channel_id=1, source_target_pairs={{0,254},{1,255},{2,0},{3,1},{4,2},{5,3},{6,4},{7,5},{8,6},{9,7},{1... | collective-permute-start | bytes 776 | tf_op jit(solution)/shard_map/ppermute | solution.py:79
  51.6 1.0 collective-permute-start.5
  52.6 2.6 %collective-permute-start.3 = (f32[4,16]{1,0:T(4,128)S(1)}, f32[4,16]{1,0:T(4,128)S(1)}, u32[]{:S(2)}, u32[]{:S(2)}) collective-permute-start(f32[4,16]{1,0:T(4,128)S(1)} %fusion.2), channel_id=1, source_target_pairs={{0,255},{1,0},{2,1},{3,2},{4,3},{5,4},{6,5},{7,6},{8,7},{9,8},{10,... | collective-permute-start | bytes 776 | tf_op jit(solution)/shard_map/ppermute | solution.py:79
  55.2 0.0 collective-permute-start.2
  55.3 0.9 collective-permute-start.1
  56.2 0.3 pad_maximum_fusion
  56.5 15.4 %gather_fusion.2 = f32[2048,4,128]{2,1,0:T(4,128)} fusion(f32[768,4,128]{2,1,0:T(4,128)S(1)} %pad_maximum_fusion, s32[2048]{0:T(1024)S(1)} %broadcast_clamp_fusion), kind=kCustom, calls=%fused_computation.2 | custom fusion | bytes 8396800 | tf_op jit(solution)/shard_map/gather | solution.py:108
  72.0 0.5 collective-permute-start
  72.5 11.2 %fusion.27 = (f32[512,4,1,128]{3,2,1,0:T(1,128)S(1)}, f32[512,4,1,128]{3,2,1,0:T(1,128)S(1)}, f32[512,4,1,128]{3,2,1,0:T(1,128)S(1)}, f32[512,4,1,128]{3,2,1,0:T(1,128)}) fusion(f32[512,4,4,128]{3,2,1,0:T(4,128)} %bitcast.75), kind=kLoop, calls=%fused_computation.66 | loop fusion | bytes 8388608 | tf_op jit(solution)/shard_map/slice | solution.py:19
  83.7 0.1 slice_add_fusion.3
  83.8 0.1 pad_maximum_fusion.1
  83.9 1.2 fusion.3
  85.1 1.4 fusion.4
  86.5 0.1 fusion.29
  86.6 1.2 collective-permute-start.6
  87.8 0.1 collective-permute-start.8
  87.9 1.5 collective-permute-start.7
  89.4 3.5 %collective-permute-done.6 = f32[4]{0:T(128)S(1)} collective-permute-done((f32[4]{0:T(128)S(1)}, f32[4]{0:T(128)S(1)}, u32[]{:S(2)}, u32[]{:S(2)}) %collective-permute-start.6) | collective-permute-done | bytes 48 | tf_op jit(solution)/shard_map/ppermute | solution.py:79
  92.9 1.1 collective-permute-done.8
  94.0 0.5 collective-permute-done.7
  94.5 0.6 broadcast_in_dim.27
  95.1 8.2 %all-to-all-start.3 = ((f32[16,1,4]{2,1,0:T(1,128)}), f32[16,1,4]{2,1,0:T(1,128)S(1)}, u32[]{:S(2)}, u32[]{:S(2)}) async-start(f32[16,1,4]{2,1,0:T(1,128)} %broadcast_in_dim.27), calls=%async_computation.3 | async-start | bytes 16384 | tf_op jit(solution)/shard_map/all_to_all | solution.py:101
  103.3 75.2 %multiply_reduce_fusion = f32[512,128]{1,0:T(8,128)} fusion(f32[512,4,128]{2,1,0:T(4,128)} %bitcast.84, f32[512,128]{1,0:T(8,128)} %bitcast.89, f32[512,4,128]{2,1,0:T(4,128)S(1)} %bitcast.82, f32[512,128]{1,0:T(8,128)} %bitcast.90, f32[512,4,128]{2,1,0:T(4,128)S(1)} %bitcast.83, f32[512,128]{1,0:T(8,128)} %bitcast.88, f32[512,4,128]{2,1,0:T(4,128)S(1)} %bitcast.81), kind=kLoop, calls=%fused_computation.4 | loop fusion | flops 369033216 | bytes 5242880 | tf_op jit(solution)/shard_map/reduce_sum | solution.py:20
  178.6 0.1 copy.36
  178.6 0.6 broadcast_in_dim.52
  179.3 9.6 %all-to-all-start.4 = ((f32[16,16,4]{1,2,0:T(4,128)}), f32[16,16,4]{1,2,0:T(4,128)S(1)}, u32[]{:S(2)}, u32[]{:S(2)}) async-start(f32[16,16,4]{1,2,0:T(4,128)} %broadcast_in_dim.52), calls=%async_computation.4 | async-start | bytes 65536 | tf_op jit(solution)/shard_map/all_to_all | solution.py:104
  188.9 1.7 negate_multiply_fusion
  190.6 5.7 %all-to-all-done.4 = f32[16,16,4]{1,2,0:T(4,128)S(1)} async-done(((f32[16,16,4]{1,2,0:T(4,128)}), f32[16,16,4]{1,2,0:T(4,128)S(1)}, u32[]{:S(2)}, u32[]{:S(2)}) %all-to-all-start.4) | async-done | bytes 4128 | tf_op jit(solution)/shard_map/all_to_all | solution.py:104
  196.3 6.9 %all-to-all-start.2 = ((f32[16,32,128]{2,1,0:T(8,128)}), f32[16,32,128]{2,1,0:T(8,128)S(1)}, u32[]{:S(2)}, u32[]{:S(2)}) async-start(f32[16,32,128]{2,1,0:T(8,128)} %bitcast.26), calls=%async_computation.2 | async-start | bytes 524288 | tf_op jit(solution)/shard_map/all_to_all | solution.py:110
  203.2 0.2 copy.37
  203.4 0.7 reshape.153
  204.1 7.2 %all-to-all-done.2 = f32[16,32,128]{2,1,0:T(8,128)S(1)} async-done(((f32[16,32,128]{2,1,0:T(8,128)}), f32[16,32,128]{2,1,0:T(8,128)S(1)}, u32[]{:S(2)}, u32[]{:S(2)}) %all-to-all-start.2) | async-done | bytes 262176 | tf_op jit(solution)/shard_map/all_to_all | solution.py:110
  211.3 0.7 gather_fusion.3
  212.0 0.7 bitcast_add_fusion
  (32 shorter events, 0.2 us)
Async XLA Ops:
  0.6 15.2 %copy-start = (s32[1,64]{1,0:T(1,128)S(1)}, s32[1,64]{1,0:T(1,128)}, u32[]{:S(2)}) copy-start(s32[1,64]{1,0:T(1,128)} %param.14) | copy-start | bytes 772
  0.6 15.1 %copy-start.7 = (s32[1,16]{1,0:T(1,128)S(1)}, s32[1,16]{1,0:T(1,128)}, u32[]{:S(2)}) copy-start(s32[1,16]{1,0:T(1,128)} %param.16) | copy-start | bytes 196
  0.7 15.1 %copy-start.5 = (s32[1,16,16]{2,1,0:T(8,128)S(1)}, s32[1,16,16]{2,1,0:T(8,128)}, u32[]{:S(2)}) copy-start(s32[1,16,16]{2,1,0:T(8,128)} %param.15) | copy-start | bytes 3076
  8.1 23.6 %all-to-all-start = ((f32[512,4,128]{2,1,0:T(4,128)}), f32[512,4,128]{2,1,0:T(4,128)S(1)}, u32[]{:S(2)}, u32[]{:S(2)}) async-start(f32[512,4,128]{2,1,0:T(4,128)} %copy.32), calls=%async_computation | async-start | bytes 2097152 | tf_op jit(solution)/shard_map/all_to_all | solution.py:61
  15.9 2.1 copy-start.6
  15.9 2.4 %copy-start.1 = (f32[256,128]{1,0:T(8,128)S(1)}, f32[256,128]{1,0:T(8,128)}, u32[]{:S(2)}) copy-start(f32[256,128]{1,0:T(8,128)} %param.11) | copy-start | bytes 393220
  15.9 2.4 %copy-start.2 = (f32[256,3,128]{2,0,1:T(8,128)S(1)}, f32[256,3,128]{2,0,1:T(8,128)}, u32[]{:S(2)}) copy-start(f32[256,3,128]{2,0,1:T(8,128)} %param.10) | copy-start | bytes 1179652
  15.9 2.8 %copy-start.4 = (s32[256,128]{1,0:T(8,128)S(1)}, s32[256,128]{1,0:T(8,128)}, u32[]{:S(2)}) copy-start(s32[256,128]{1,0:T(8,128)} %param.13) | copy-start | bytes 393220
  33.6 14.1 %all-to-all-start.1 = ((f32[16,16,4,128]{3,1,2,0:T(8,128)}), f32[16,16,4,128]{3,1,2,0:T(8,128)S(1)}, u32[]{:S(2)}, u32[]{:S(2)}) async-start(f32[16,16,4,128]{3,1,2,0:T(8,128)} %copy_select_fusion), calls=%async_computation.1 | async-start | bytes 1048576 | tf_op jit(solution)/shard_map/all_to_all | solution.py:68
  47.9 24.0 %collective-permute-start.4 = (f32[4,16]{1,0:T(4,128)S(1)}, f32[4,16]{1,0:T(4,128)S(1)}, u32[]{:S(2)}, u32[]{:S(2)}) collective-permute-start(f32[4,16]{1,0:T(4,128)S(1)} %fusion.2), channel_id=1, source_target_pairs={{0,254},{1,255},{2,0},{3,1},{4,2},{5,3},{6,4},{7,5},{8,6},{9,7},{1... | collective-permute-start | bytes 776 | tf_op jit(solution)/shard_map/ppermute | solution.py:79
  51.6 32.1 %collective-permute-start.5 = (f32[4,16]{1,0:T(4,128)S(1)}, f32[4,16]{1,0:T(4,128)S(1)}, u32[]{:S(2)}, u32[]{:S(2)}) collective-permute-start(f32[4,16]{1,0:T(4,128)S(1)} %fusion.2), channel_id=1, source_target_pairs={{0,253},{1,254},{2,255},{3,0},{4,1},{5,2},{6,3},{7,4},{8,5},{9,6},... | collective-permute-start | bytes 776 | tf_op jit(solution)/shard_map/ppermute | solution.py:79
  52.6 31.1 %collective-permute-start.3 = (f32[4,16]{1,0:T(4,128)S(1)}, f32[4,16]{1,0:T(4,128)S(1)}, u32[]{:S(2)}, u32[]{:S(2)}) collective-permute-start(f32[4,16]{1,0:T(4,128)S(1)} %fusion.2), channel_id=1, source_target_pairs={{0,255},{1,0},{2,1},{3,2},{4,3},{5,4},{6,5},{7,6},{8,7},{9,8},{10,... | collective-permute-start | bytes 776 | tf_op jit(solution)/shard_map/ppermute | solution.py:79
  55.2 28.5 %collective-permute-start.2 = (f32[4,16]{1,0:T(4,128)S(1)}, f32[4,16]{1,0:T(4,128)S(1)}, u32[]{:S(2)}, u32[]{:S(2)}) collective-permute-start(f32[4,16]{1,0:T(4,128)S(1)} %fusion.2), channel_id=1, source_target_pairs={{0,3},{1,4},{2,5},{3,6},{4,7},{5,8},{6,9},{7,10},{8,11},{9,12},{10... | collective-permute-start | bytes 776 | tf_op jit(solution)/shard_map/ppermute | solution.py:79
  55.3 28.5 %collective-permute-start.1 = (f32[4,16]{1,0:T(4,128)S(1)}, f32[4,16]{1,0:T(4,128)S(1)}, u32[]{:S(2)}, u32[]{:S(2)}) collective-permute-start(f32[4,16]{1,0:T(4,128)S(1)} %fusion.2), channel_id=1, source_target_pairs={{0,2},{1,3},{2,4},{3,5},{4,6},{5,7},{6,8},{7,9},{8,10},{9,11},{10,... | collective-permute-start | bytes 776 | tf_op jit(solution)/shard_map/ppermute | solution.py:79
  72.0 11.8 %collective-permute-start = (f32[4,16]{1,0:T(4,128)S(1)}, f32[4,16]{1,0:T(4,128)S(1)}, u32[]{:S(2)}, u32[]{:S(2)}) collective-permute-start(f32[4,16]{1,0:T(4,128)S(1)} %fusion.2), channel_id=1, source_target_pairs={{0,1},{1,2},{2,3},{3,4},{4,5},{5,6},{6,7},{7,8},{8,9},{9,10},{10,1... | collective-permute-start | bytes 776 | tf_op jit(solution)/shard_map/ppermute | solution.py:79
  72.5 11.5 %copy-start.3 = (f32[256,3,128]{2,0,1:T(8,128)S(1)}, f32[256,3,128]{2,0,1:T(8,128)}, u32[]{:S(2)}) copy-start(f32[256,3,128]{2,0,1:T(8,128)} %param.10) | copy-start | bytes 1179652
  86.6 6.3 %collective-permute-start.6 = (f32[4]{0:T(128)S(1)}, f32[4]{0:T(128)S(1)}, u32[]{:S(2)}, u32[]{:S(2)}) collective-permute-start(f32[4]{0:T(128)S(1)} %get-tuple-element.17), channel_id=1, source_target_pairs={{0,1},{1,2},{2,3},{3,4},{4,5},{5,6},{6,7},{7,8},{8,9},{9,10},{10,1... | collective-permute-start | bytes 56 | tf_op jit(solution)/shard_map/ppermute | solution.py:79
  87.8 6.3 %collective-permute-start.8 = (f32[4]{0:T(128)S(1)}, f32[4]{0:T(128)S(1)}, u32[]{:S(2)}, u32[]{:S(2)}) collective-permute-start(f32[4]{0:T(128)S(1)} %get-tuple-element.18), channel_id=1, source_target_pairs={{0,3},{1,4},{2,5},{3,6},{4,7},{5,8},{6,9},{7,10},{8,11},{9,12},{10... | collective-permute-start | bytes 56 | tf_op jit(solution)/shard_map/ppermute | solution.py:79
  87.9 6.6 %collective-permute-start.7 = (f32[4]{0:T(128)S(1)}, f32[4]{0:T(128)S(1)}, u32[]{:S(2)}, u32[]{:S(2)}) collective-permute-start(f32[4]{0:T(128)S(1)} %get-tuple-element.19), channel_id=1, source_target_pairs={{0,2},{1,3},{2,4},{3,5},{4,6},{5,7},{6,8},{7,9},{8,10},{9,11},{10,... | collective-permute-start | bytes 56 | tf_op jit(solution)/shard_map/ppermute | solution.py:79
  95.1 83.4 %all-to-all-start.3 = ((f32[16,1,4]{2,1,0:T(1,128)}), f32[16,1,4]{2,1,0:T(1,128)S(1)}, u32[]{:S(2)}, u32[]{:S(2)}) async-start(f32[16,1,4]{2,1,0:T(1,128)} %broadcast_in_dim.27), calls=%async_computation.3 | async-start | bytes 16384 | tf_op jit(solution)/shard_map/all_to_all | solution.py:101
  179.3 17.0 %all-to-all-start.4 = ((f32[16,16,4]{1,2,0:T(4,128)}), f32[16,16,4]{1,2,0:T(4,128)S(1)}, u32[]{:S(2)}, u32[]{:S(2)}) async-start(f32[16,16,4]{1,2,0:T(4,128)} %broadcast_in_dim.52), calls=%async_computation.4 | async-start | bytes 65536 | tf_op jit(solution)/shard_map/all_to_all | solution.py:104
  196.3 15.0 %all-to-all-start.2 = ((f32[16,32,128]{2,1,0:T(8,128)}), f32[16,32,128]{2,1,0:T(8,128)S(1)}, u32[]{:S(2)}, u32[]{:S(2)}) async-start(f32[16,32,128]{2,1,0:T(8,128)} %bitcast.26), calls=%async_computation.2 | async-start | bytes 524288 | tf_op jit(solution)/shard_map/all_to_all | solution.py:110

commit v4 on v3

--- a/solution.py
+++ b/solution.py
@@ -2,6 +2,8 @@
 import jax.numpy as jnp
 from jax import lax
 from jax.sharding import PartitionSpec as P
+from jax.experimental import pallas as pl
+from jax.experimental.pallas import tpu as pltpu
 
 GSPAN = 16
 GROUP_DEV = 4
@@ -18,6 +20,59 @@
         distance = distance + offset * offset
     weights = sources[:, :, 3, None, :] * lax.rsqrt(distance)
     return -jnp.sum(weights, axis=(1, 3))
+
+
+def pair_kernel(index_ref, table_ref, out_ref, acc_ref, *, rows, pairs, coupling):
+    width = table_ref.shape[2]
+    ones = jnp.ones((8, width), jnp.float32)
+    first = pl.program_id(0) * rows
+
+    def one_slot(t, carry):
+        slot = first + t
+        target = table_ref[slot]
+        columns = jnp.transpose(jnp.concatenate([target, jnp.zeros_like(target)], axis=0))
+        picked = [table_ref[index_ref[slot * pairs + p]] for p in range(pairs)]
+        for c in range(width // 8):
+            tx = columns[8 * c:8 * c + 8, 0:1]
+            ty = columns[8 * c:8 * c + 8, 1:2]
+            tz = columns[8 * c:8 * c + 8, 2:3]
+            acc = jnp.zeros((8, width), jnp.float32)
+            for src in picked:
+                dx = tx - src[0:1, :]
+                dy = ty - src[1:2, :]
+                dz = tz - src[2:3, :]
+                distance = softening + dx * dx
+                distance = distance + dy * dy
+                distance = distance + dz * dz
+                acc = acc + src[3:4, :] * lax.rsqrt(distance)
+            acc_ref[8 * c:8 * c + 8, :] = acc
+        total = lax.dot_general(
+            ones, acc_ref[...], (((1,), (1,)), ((), ())), precision=exact,
+            preferred_element_type=jnp.float32,
+        )
+        out_ref[pl.ds(t, 1), :] = -total[0:1, :] * coupling
+        return carry
+
+    lax.fori_loop(0, rows, one_slot, 0)
+
+
+def slot_potential(combined, partners, slot_count, coupling):
+    rows = 8
+    width = combined.shape[2]
+    pairs = partners.shape[1]
+    grid_spec = pltpu.PrefetchScalarGridSpec(
+        num_scalar_prefetch=1,
+        grid=(slot_count // rows,),
+        in_specs=[pl.BlockSpec(combined.shape, lambda i, index: (0, 0, 0))],
+        out_specs=pl.BlockSpec((rows, width), lambda i, index: (i, 0)),
+        scratch_shapes=[pltpu.VMEM((width, width), jnp.float32)],
+    )
+    body = lambda *refs: pair_kernel(*refs, rows=rows, pairs=pairs, coupling=coupling)
+    return pl.pallas_call(
+        body,
+        grid_spec=grid_spec,
+        out_shape=jax.ShapeDtypeStruct((slot_count, width), jnp.float32),
+    )(partners.reshape(-1), combined)
 
 
 def shards(
@@ -105,8 +160,7 @@
     group_kinetic = every.reshape(groups)
 
     coupling = 1.0 / (partners.shape[1] * leaf_width)
-    sources = combined.at[partners].get(mode="promise_in_bounds")
-    potential = tile_potential(owned, sources) * coupling
+    potential = slot_potential(combined, partners, slot_count, coupling)
     returned = lax.all_to_all(potential, "grp", split_axis=0, concat_axis=0, tiled=True)
     own_potential = returned.at[target].get(mode="promise_in_bounds")
     energy = kinetic.reshape(leaves, leaf_width) + own_potential

time: 213 us -> 345 us (1.62)
  Pallas kernels: 0 us -> 230 us
  other arithmetic: 82.3 us -> 6.75 us
  local copies, waits for them, and re-layouts: 38.9 us -> 11.1 us
  waiting for transfers between devices: 37.8 us -> 42.8 us
    pallas_call x0 -> x1, Pallas kernels: none -> 230 us  [slot_potential(): pl.pallas_call(body, grid_spec=grid_spec, out_shape=jax.ShapeDtypeStruct(...]
    reduce_sum x1 -> x0, other arithmetic: 75.2 us -> none  [tile_potential(): return -jnp.sum(weights, axis=(1, 3))]
    gather x1 -> x0, local copies, waits for them, and re-layouts: 15.4 us -> none  [shards(): sources = combined.at[partners].get(mode='promise_in_bounds')]
    slice x3 -> x1, local copies, waits for them, and re-layouts: 12.9 us -> 0.18 us  [the longest x1 11.2 us: tile_potential(): weights = sources[:, :, 3, None, :] * lax.rsqrt(distance)]
    all_to_all x1, waiting for transfers between devices: 5.72 us -> 0.01 us  [shards(): lax.all_to_all(every, 'dom', split_axis=0, concat_axis=0, tiled=True)]
    all_to_all x1, waiting for transfers between devices: 0.01 us -> 5.43 us  [shards(): lax.all_to_all(across, 'grp', split_axis=0, concat_axis=0, tiled=True)]
    all_to_all x1, starting transfers between devices: 9.65 us -> 13.6 us  [shards(): lax.all_to_all(every, 'dom', split_axis=0, concat_axis=0, tiled=True)]
  transfers between devices with their start and end apart: 14 -> 14, of which waited for: 7 -> 7; matrix products, arithmetic and copies ran while one was open for 52% -> 2% of each run, Pallas kernels for 0% -> 67%
where the time goes in v4:
time: 345 us; the launch traced here: 344 us
  Pallas kernels  230 us (67%)
  starting transfers between devices  48.6 us (14%)
  waiting for transfers between devices  42.8 us (12%)
  local copies, waits for them, and re-layouts  11.1 us (3%)
  other arithmetic  6.75 us (2%)
  matrix products  4.79 us (1%)
    pallas_call x1, Pallas kernels, slot_potential(): pl.pallas_call(body, grid_spec=grid_spec, out_shape=jax.ShapeDtypeStruct(...  230 us
    all_to_all x1, starting transfers between devices, shards(): lax.all_to_all(every, 'dom', split_axis=0, concat_axis=0, tiled=True)  13.6 us
    all_to_all x1, waiting for transfers between devices, shards(): lax.all_to_all(outgoing, 'grp', split_axis=0, concat_axis=0, tiled=True)  13.4 us
    ppermute x9, starting transfers between devices, from_block(): return lax.ppermute(value, ('dom', 'grp'), ring)  10.9 us
    all_to_all x1, starting transfers between devices, shards(): lax.all_to_all(across, 'grp', split_axis=0, concat_axis=0, tiled=True)  8.7 us
    all_to_all x1, waiting for transfers between devices, shards(): lax.all_to_all(sending, 'grp', split_axis=0, concat_axis=0, tiled=True)  8.19 us
    ppermute x9, waiting for transfers between devices, from_block(): return lax.ppermute(value, ('dom', 'grp'), ring)  8.17 us
    all_to_all x1, starting transfers between devices, shards(): lax.all_to_all(outgoing, 'grp', split_axis=0, concat_axis=0, tiled=True)  7.7 us
  transfers between devices with their start and end apart: 14, of which 7 were waited for; matrix products, arithmetic and copies ran while one was open for 2% of the time, Pallas kernels for 67%

profile of v4, /device:TPU:1, one launch (start us, length us, event | category | flops | bytes accessed | tf_op | source)
XLA Modules:
  0.0 344.4 jit_solution(946231335083599199)
XLA Ops:
  0.6 0.0 copy-start
  0.6 1.0 copy.20
  1.7 1.2 copy.21
  2.8 0.7 fusion.21
  3.5 0.6 reduce-window.6
  4.1 0.2 slice_reduce_fusion
  4.3 0.8 fusion.20
  5.1 0.7 compare_select_fusion.2
  5.8 0.6 fusion.11
  6.4 1.7 copy.22
  8.1 7.7 %all-to-all-start = ((f32[512,4,128]{2,1,0:T(4,128)}), f32[512,4,128]{2,1,0:T(4,128)S(1)}, u32[]{:S(2)}, u32[]{:S(2)}) async-start(f32[512,4,128]{2,1,0:T(4,128)} %copy.22), calls=%async_computation | async-start | bytes 2097152 | tf_op jit(solution)/shard_map/all_to_all | solution.py:116
  15.8 0.3 bitcast_multiply_fusion
  16.2 0.1 reshape.153
  16.3 0.0 copy-start.6
  16.3 1.9 gather_fusion
  18.2 0.1 gather.12
  18.3 0.1 reshape.161
  18.4 0.1 iota_compare_fusion.11
  18.4 13.4 %all-to-all-done = f32[512,4,128]{2,1,0:T(4,128)S(1)} async-done(((f32[512,4,128]{2,1,0:T(4,128)}), f32[512,4,128]{2,1,0:T(4,128)S(1)}, u32[]{:S(2)}, u32[]{:S(2)}) %all-to-all-start) | async-done | bytes 1048608 | tf_op jit(solution)/shard_map/all_to_all | solution.py:116
  31.8 1.0 gather_fusion.1
  32.8 1.1 broadcast_select_fusion
  34.0 4.2 %all-to-all-start.1 = ((f32[16,16,4,128]{3,2,1,0:T(4,128)}), f32[16,16,4,128]{3,2,1,0:T(4,128)S(1)}, u32[]{:S(2)}, u32[]{:S(2)}) async-start(f32[16,16,4,128]{3,2,1,0:T(4,128)} %broadcast_select_fusion), calls=%async_computation.1 | async-start | bytes 1048576 | tf_op jit(solution)/shard_map/all_to_all | solution.py:123
  38.2 0.1 add_select_fusion
  38.2 1.6 fusion.2
  39.9 8.2 %all-to-all-done.1 = f32[16,16,4,128]{3,2,1,0:T(4,128)S(1)} async-done(((f32[16,16,4,128]{3,2,1,0:T(4,128)}), f32[16,16,4,128]{3,2,1,0:T(4,128)S(1)}, u32[]{:S(2)}, u32[]{:S(2)}) %all-to-all-start.1) | async-done | bytes 524320 | tf_op jit(solution)/shard_map/all_to_all | solution.py:123
  48.1 1.0 collective-permute-start.2
  49.0 0.1 collective-permute-start.1
  49.1 0.5 collective-permute-start
  49.6 4.6 %collective-permute-start.3 = (f32[4,16]{1,0:T(4,128)S(1)}, f32[4,16]{1,0:T(4,128)S(1)}, u32[]{:S(2)}, u32[]{:S(2)}) collective-permute-start(f32[4,16]{1,0:T(4,128)S(1)} %fusion.2), channel_id=1, source_target_pairs={{0,255},{1,0},{2,1},{3,2},{4,3},{5,4},{6,5},{7,6},{8,7},{9,8},{10,... | collective-permute-start | bytes 776 | tf_op jit(solution)/shard_map/ppermute | solution.py:134
  54.2 2.2 collective-permute-start.4
  56.4 0.0 collective-permute-done.2
  56.4 2.0 collective-permute-start.5
  58.4 0.0 collective-permute-done.1
  58.4 0.0 collective-permute-done
  58.4 0.0 collective-permute-done.4
  58.4 1.9 collective-permute-done.5
  60.4 0.1 slice_add_fusion.3
  60.4 0.1 pad_maximum_fusion.1
  60.5 1.1 fusion.3
  61.7 1.4 fusion.4
  63.1 0.1 fusion.27
  63.2 0.0 collective-permute-start.8
  63.2 0.2 collective-permute-start.7
  63.4 0.3 collective-permute-start.6
  63.7 4.6 %collective-permute-done.8 = f32[4]{0:T(128)S(1)} collective-permute-done((f32[4]{0:T(128)S(1)}, f32[4]{0:T(128)S(1)}, u32[]{:S(2)}, u32[]{:S(2)}) %collective-permute-start.8) | collective-permute-done | bytes 48 | tf_op jit(solution)/shard_map/ppermute | solution.py:134
  68.3 1.6 collective-permute-done.7
  69.9 0.0 collective-permute-done.6
  69.9 0.6 broadcast_in_dim.24
  70.5 8.7 %all-to-all-start.3 = ((f32[16,1,4]{2,1,0:T(1,128)}), f32[16,1,4]{2,1,0:T(1,128)S(1)}, u32[]{:S(2)}, u32[]{:S(2)}) async-start(f32[16,1,4]{2,1,0:T(1,128)} %broadcast_in_dim.24), calls=%async_computation.3 | async-start | bytes 16384 | tf_op jit(solution)/shard_map/all_to_all | solution.py:156
  79.2 0.1 copy.23
  79.4 0.8 reshape.149.refs_0_
  80.2 5.4 %all-to-all-done.3 = f32[16,1,4]{2,1,0:T(1,128)S(1)} async-done(((f32[16,1,4]{2,1,0:T(1,128)}), f32[16,1,4]{2,1,0:T(1,128)S(1)}, u32[]{:S(2)}, u32[]{:S(2)}) %all-to-all-start.3) | async-done | bytes 288 | tf_op jit(solution)/shard_map/all_to_all | solution.py:156
  85.6 0.1 copy.24
  85.7 0.6 broadcast_in_dim.26
  86.3 13.6 %all-to-all-start.4 = ((f32[16,16,4]{1,2,0:T(4,128)}), f32[16,16,4]{1,2,0:T(4,128)S(1)}, u32[]{:S(2)}, u32[]{:S(2)}) async-start(f32[16,16,4]{1,2,0:T(4,128)} %broadcast_in_dim.26), calls=%async_computation.4 | async-start | bytes 65536 | tf_op jit(solution)/shard_map/all_to_all | solution.py:159
  99.9 1.5 pad_maximum_fusion.refs_1_
  101.4 229.6 %shard_map.104 = f32[512,128]{1,0:T(8,128)} custom-call(s32[2048]{0:T(1024)} %reshape.149.refs_0_, f32[768,4,128]{2,1,0:T(4,128)} %pad_maximum_fusion.refs_1_), custom_call_target="tpu_custom_call" | custom-call | tf_op jit(solution)/shard_map/pallas_call | solution.py:71
  331.0 0.0 all-to-all-done.4
  331.0 3.5 %all-to-all-start.2 = ((f32[16,32,128]{2,1,0:T(8,128)}), f32[16,32,128]{2,1,0:T(8,128)S(1)}, u32[]{:S(2)}, u32[]{:S(2)}) async-start(f32[16,32,128]{2,1,0:T(8,128)} %bitcast.72), calls=%async_computation.2 | async-start | bytes 524288 | tf_op jit(solution)/shard_map/all_to_all | solution.py:164
  334.5 0.2 copy.25
  334.7 0.7 reshape.150
  335.4 7.6 %all-to-all-done.2 = f32[16,32,128]{2,1,0:T(8,128)S(1)} async-done(((f32[16,32,128]{2,1,0:T(8,128)}), f32[16,32,128]{2,1,0:T(8,128)S(1)}, u32[]{:S(2)}, u32[]{:S(2)}) %all-to-all-start.2) | async-done | bytes 262176 | tf_op jit(solution)/shard_map/all_to_all | solution.py:164
  343.0 0.7 gather_fusion.2
  343.7 0.7 bitcast_add_fusion
  (23 shorter events, 0.1 us)
Async XLA Ops:
  0.6 15.6 %copy-start = (s32[1,64]{1,0:T(1,128)S(1)}, s32[1,64]{1,0:T(1,128)}, u32[]{:S(2)}) copy-start(s32[1,64]{1,0:T(1,128)} %param.14) | copy-start | bytes 772
  8.1 7.7 %copy-start.1 = (f32[256,128]{1,0:T(8,128)S(1)}, f32[256,128]{1,0:T(8,128)}, u32[]{:S(2)}) copy-start(f32[256,128]{1,0:T(8,128)} %param.11) | copy-start | bytes 393220
  8.1 7.7 %copy-start.2 = (f32[256,3,128]{2,0,1:T(8,128)S(1)}, f32[256,3,128]{2,0,1:T(8,128)}, u32[]{:S(2)}) copy-start(f32[256,3,128]{2,0,1:T(8,128)} %param.10) | copy-start | bytes 1179652
  8.1 8.1 %copy-start.5 = (s32[1,16,16]{2,1,0:T(8,128)S(1)}, s32[1,16,16]{2,1,0:T(8,128)}, u32[]{:S(2)}) copy-start(s32[1,16,16]{2,1,0:T(8,128)} %param.15) | copy-start | bytes 3076
  8.1 23.8 %all-to-all-start = ((f32[512,4,128]{2,1,0:T(4,128)}), f32[512,4,128]{2,1,0:T(4,128)S(1)}, u32[]{:S(2)}, u32[]{:S(2)}) async-start(f32[512,4,128]{2,1,0:T(4,128)} %copy.22), calls=%async_computation | async-start | bytes 2097152 | tf_op jit(solution)/shard_map/all_to_all | solution.py:116
  16.3 2.1 copy-start.6
  18.4 19.7 %copy-start.3 = (s32[256,128]{1,0:T(8,128)S(1)}, s32[256,128]{1,0:T(8,128)}, u32[]{:S(2)}) copy-start(s32[256,128]{1,0:T(8,128)} %param.13) | copy-start | bytes 393220
  34.0 14.1 %all-to-all-start.1 = ((f32[16,16,4,128]{3,2,1,0:T(4,128)}), f32[16,16,4,128]{3,2,1,0:T(4,128)S(1)}, u32[]{:S(2)}, u32[]{:S(2)}) async-start(f32[16,16,4,128]{3,2,1,0:T(4,128)} %broadcast_select_fusion), calls=%async_computation.1 | async-start | bytes 1048576 | tf_op jit(solution)/shard_map/all_to_all | solution.py:123
  39.9 39.4 %copy-start.4 = (s32[512,4]{0,1:T(4,128)S(1)}, s32[512,4]{0,1:T(4,128)}, u32[]{:S(2)}) copy-start(s32[512,4]{0,1:T(4,128)} %param.17) | copy-start | bytes 24580
  48.1 8.4 %collective-permute-start.2 = (f32[4,16]{1,0:T(4,128)S(1)}, f32[4,16]{1,0:T(4,128)S(1)}, u32[]{:S(2)}, u32[]{:S(2)}) collective-permute-start(f32[4,16]{1,0:T(4,128)S(1)} %fusion.2), channel_id=1, source_target_pairs={{0,3},{1,4},{2,5},{3,6},{4,7},{5,8},{6,9},{7,10},{8,11},{9,12},{10... | collective-permute-start | bytes 776 | tf_op jit(solution)/shard_map/ppermute | solution.py:134
  49.0 9.4 %collective-permute-start.1 = (f32[4,16]{1,0:T(4,128)S(1)}, f32[4,16]{1,0:T(4,128)S(1)}, u32[]{:S(2)}, u32[]{:S(2)}) collective-permute-start(f32[4,16]{1,0:T(4,128)S(1)} %fusion.2), channel_id=1, source_target_pairs={{0,2},{1,3},{2,4},{3,5},{4,6},{5,7},{6,8},{7,9},{8,10},{9,11},{10,... | collective-permute-start | bytes 776 | tf_op jit(solution)/shard_map/ppermute | solution.py:134
  49.1 9.3 %collective-permute-start = (f32[4,16]{1,0:T(4,128)S(1)}, f32[4,16]{1,0:T(4,128)S(1)}, u32[]{:S(2)}, u32[]{:S(2)}) collective-permute-start(f32[4,16]{1,0:T(4,128)S(1)} %fusion.2), channel_id=1, source_target_pairs={{0,1},{1,2},{2,3},{3,4},{4,5},{5,6},{6,7},{7,8},{8,9},{9,10},{10,1... | collective-permute-start | bytes 776 | tf_op jit(solution)/shard_map/ppermute | solution.py:134
  49.6 8.8 %collective-permute-start.3 = (f32[4,16]{1,0:T(4,128)S(1)}, f32[4,16]{1,0:T(4,128)S(1)}, u32[]{:S(2)}, u32[]{:S(2)}) collective-permute-start(f32[4,16]{1,0:T(4,128)S(1)} %fusion.2), channel_id=1, source_target_pairs={{0,255},{1,0},{2,1},{3,2},{4,3},{5,4},{6,5},{7,6},{8,7},{9,8},{10,... | collective-permute-start | bytes 776 | tf_op jit(solution)/shard_map/ppermute | solution.py:134
  54.2 4.2 %collective-permute-start.4 = (f32[4,16]{1,0:T(4,128)S(1)}, f32[4,16]{1,0:T(4,128)S(1)}, u32[]{:S(2)}, u32[]{:S(2)}) collective-permute-start(f32[4,16]{1,0:T(4,128)S(1)} %fusion.2), channel_id=1, source_target_pairs={{0,254},{1,255},{2,0},{3,1},{4,2},{5,3},{6,4},{7,5},{8,6},{9,7},{1... | collective-permute-start | bytes 776 | tf_op jit(solution)/shard_map/ppermute | solution.py:134
  56.4 3.9 %collective-permute-start.5 = (f32[4,16]{1,0:T(4,128)S(1)}, f32[4,16]{1,0:T(4,128)S(1)}, u32[]{:S(2)}, u32[]{:S(2)}) collective-permute-start(f32[4,16]{1,0:T(4,128)S(1)} %fusion.2), channel_id=1, source_target_pairs={{0,253},{1,254},{2,255},{3,0},{4,1},{5,2},{6,3},{7,4},{8,5},{9,6},... | collective-permute-start | bytes 776 | tf_op jit(solution)/shard_map/ppermute | solution.py:134
  63.2 5.1 %collective-permute-start.8 = (f32[4]{0:T(128)S(1)}, f32[4]{0:T(128)S(1)}, u32[]{:S(2)}, u32[]{:S(2)}) collective-permute-start(f32[4]{0:T(128)S(1)} %get-tuple-element.11), channel_id=1, source_target_pairs={{0,3},{1,4},{2,5},{3,6},{4,7},{5,8},{6,9},{7,10},{8,11},{9,12},{10... | collective-permute-start | bytes 56 | tf_op jit(solution)/shard_map/ppermute | solution.py:134
  63.2 6.7 %collective-permute-start.7 = (f32[4]{0:T(128)S(1)}, f32[4]{0:T(128)S(1)}, u32[]{:S(2)}, u32[]{:S(2)}) collective-permute-start(f32[4]{0:T(128)S(1)} %get-tuple-element.12), channel_id=1, source_target_pairs={{0,2},{1,3},{2,4},{3,5},{4,6},{5,7},{6,8},{7,9},{8,10},{9,11},{10,... | collective-permute-start | bytes 56 | tf_op jit(solution)/shard_map/ppermute | solution.py:134
  63.4 6.5 %collective-permute-start.6 = (f32[4]{0:T(128)S(1)}, f32[4]{0:T(128)S(1)}, u32[]{:S(2)}, u32[]{:S(2)}) collective-permute-start(f32[4]{0:T(128)S(1)} %get-tuple-element.10), channel_id=1, source_target_pairs={{0,1},{1,2},{2,3},{3,4},{4,5},{5,6},{6,7},{7,8},{8,9},{9,10},{10,1... | collective-permute-start | bytes 56 | tf_op jit(solution)/shard_map/ppermute | solution.py:134
  70.5 15.1 %all-to-all-start.3 = ((f32[16,1,4]{2,1,0:T(1,128)}), f32[16,1,4]{2,1,0:T(1,128)S(1)}, u32[]{:S(2)}, u32[]{:S(2)}) async-start(f32[16,1,4]{2,1,0:T(1,128)} %broadcast_in_dim.24), calls=%async_computation.3 | async-start | bytes 16384 | tf_op jit(solution)/shard_map/all_to_all | solution.py:156
  86.3 244.7 %all-to-all-start.4 = ((f32[16,16,4]{1,2,0:T(4,128)}), f32[16,16,4]{1,2,0:T(4,128)S(1)}, u32[]{:S(2)}, u32[]{:S(2)}) async-start(f32[16,16,4]{1,2,0:T(4,128)} %broadcast_in_dim.26), calls=%async_computation.4 | async-start | bytes 65536 | tf_op jit(solution)/shard_map/all_to_all | solution.py:159
  331.0 12.0 %all-to-all-start.2 = ((f32[16,32,128]{2,1,0:T(8,128)}), f32[16,32,128]{2,1,0:T(8,128)S(1)}, u32[]{:S(2)}, u32[]{:S(2)}) async-start(f32[16,32,128]{2,1,0:T(8,128)} %bitcast.72), calls=%async_computation.2 | async-start | bytes 524288 | tf_op jit(solution)/shard_map/all_to_all | solution.py:164

commit v5 on v3

--- a/solution.py
+++ b/solution.py
@@ -93,20 +93,26 @@
     relative = speeds - per_particle
     kinetic = 0.5 * jnp.sum(relative * relative, axis=0)
     heat_local = local_sums((mass_flat * kinetic)[None, :])[0]
-    heat_own = heat_local[:GROUP_DEV]
-    for back in range(1, quarters):
-        heat_own = heat_own + from_block(heat_local[back * GROUP_DEV:(back + 1) * GROUP_DEV], -back)
-    kinetic_own = heat_own / near[0, :GROUP_DEV]
-    across = jnp.broadcast_to(kinetic_own[None, :], (owners, GROUP_DEV))
+    partial = jnp.stack([heat_local, first_sums[0]])
+    across = jnp.broadcast_to(partial[None], (owners,) + partial.shape)
     across = lax.all_to_all(across, "grp", split_axis=0, concat_axis=0, tiled=True)
     domains = lax.axis_size("dom")
-    every = jnp.broadcast_to(across[None], (domains, owners, GROUP_DEV))
+    every = jnp.broadcast_to(across[None], (domains,) + across.shape)
     every = lax.all_to_all(every, "dom", split_axis=0, concat_axis=0, tiled=True)
-    group_kinetic = every.reshape(groups)
+    every = every.reshape(blocks, 2, quarters, GROUP_DEV)
+    totals = every[:, :, 0, :]
+    for back in range(1, quarters):
+        totals = totals + jnp.roll(every[:, :, back, :], back, axis=0)
+    group_kinetic = totals[:, 0, :].reshape(groups) / totals[:, 1, :].reshape(groups)
 
     coupling = 1.0 / (partners.shape[1] * leaf_width)
-    sources = combined.at[partners].get(mode="promise_in_bounds")
-    potential = tile_potential(owned, sources) * coupling
+    halves = []
+    half = slot_count // 2
+    for part in range(2):
+        rows = partners[part * half:(part + 1) * half]
+        sources = combined.at[rows].get(mode="promise_in_bounds")
+        halves.append(tile_potential(owned[part * half:(part + 1) * half], sources))
+    potential = jnp.concatenate(halves, axis=0) * coupling
     returned = lax.all_to_all(potential, "grp", split_axis=0, concat_axis=0, tiled=True)
     own_potential = returned.at[target].get(mode="promise_in_bounds")
     energy = kinetic.reshape(leaves, leaf_width) + own_potential

time: 213 us -> 206 us (0.967)
  starting transfers between devices: 48 us -> 42.6 us
    all_to_all x1, starting transfers between devices: 8.16 us -> 3.49 us  [shards(): lax.all_to_all(across, 'grp', split_axis=0, concat_axis=0, tiled=True)]
    slice x1 -> x2, local copies, waits for them, and re-layouts: 11.2 us -> 8.09 us  [tile_potential(): weights = sources[:, :, 3, None, :] * lax.rsqrt(distance)]
    ppermute x9 -> x6, starting transfers between devices: 11.6 us -> 8.93 us  [from_block(): return lax.ppermute(value, ('dom', 'grp'), ring)]
    reduce_sum x1 -> x2, other arithmetic: 75.2 us -> 73.6 us  [tile_potential(): return -jnp.sum(weights, axis=(1, 3))]
    ppermute x9 -> x6, waiting for transfers between devices: 5.12 us -> 6.28 us  [from_block(): return lax.ppermute(value, ('dom', 'grp'), ring)]
    gather x1 -> x2, local copies, waits for them, and re-layouts: 15.4 us -> 15.9 us  [shards(): sources = combined.at[rows].get(mode='promise_in_bounds')]
  transfers between devices with their start and end apart: 14 -> 11, of which waited for: 7 -> 5; matrix products, arithmetic and copies ran while one was open for 52% -> 53% of each run, Pallas kernels for 0% -> 0%
where the time goes in v5:
time: 206 us; the launch traced here: 205 us
  other arithmetic  81.9 us (40%)
  starting transfers between devices  42.6 us (21%)
  local copies, waits for them, and re-layouts  37.6 us (18%)
  waiting for transfers between devices  37.2 us (18%)
  matrix products  4.81 us (2%)
    reduce_sum x2, other arithmetic, tile_potential(): return -jnp.sum(weights, axis=(1, 3))  73.6 us
    gather x2, local copies, waits for them, and re-layouts, shards(): sources = combined.at[rows].get(mode='promise_in_bounds')  15.9 us
    all_to_all x1, waiting for transfers between devices, shards(): lax.all_to_all(outgoing, 'grp', split_axis=0, concat_axis=0, tiled=True)  12.7 us
    all_to_all x1, starting transfers between devices, shards(): lax.all_to_all(every, 'dom', split_axis=0, concat_axis=0, tiled=True)  11.5 us
    ppermute x6, starting transfers between devices, from_block(): return lax.ppermute(value, ('dom', 'grp'), ring)  8.93 us
    slice x2, local copies, waits for them, and re-layouts, tile_potential(): weights = sources[:, :, 3, None, :] * lax.rsqrt(distance)  8.09 us
    all_to_all x1, starting transfers between devices, shards(): lax.all_to_all(outgoing, 'grp', split_axis=0, concat_axis=0, tiled=True)  7.57 us
    all_to_all x1, starting transfers between devices, shards(): lax.all_to_all(potential, 'grp', split_axis=0, concat_axis=0, tiled=True)  6.87 us
  transfers between devices with their start and end apart: 11, of which 5 were waited for; matrix products, arithmetic and copies ran while one was open for 53% of the time, Pallas kernels for 0%

profile of v5, /device:TPU:1, one launch (start us, length us, event | category | flops | bytes accessed | tf_op | source)
XLA Modules:
  0.0 205.2 jit_solution(7551838452958901272)
XLA Ops:
  0.6 0.7 fusion.20
  1.3 0.6 reduce-window.6
  1.9 0.2 slice_reduce_fusion
  2.1 0.8 fusion.19
  2.9 0.7 compare_select_fusion.4
  3.6 1.0 copy.67
  4.6 1.2 copy.68
  5.8 0.6 fusion.10
  6.4 1.7 copy.69
  8.1 7.6 %all-to-all-start = ((f32[512,4,128]{2,1,0:T(4,128)}), f32[512,4,128]{2,1,0:T(4,128)S(1)}, u32[]{:S(2)}, u32[]{:S(2)}) async-start(f32[512,4,128]{2,1,0:T(4,128)} %copy.69), calls=%async_computation | async-start | bytes 2097152 | tf_op jit(solution)/shard_map/all_to_all | solution.py:61
  15.8 0.1 reshape.157
  15.9 1.9 gather_fusion
  17.8 0.1 gather.18
  17.9 0.1 reshape.165
  18.0 0.1 copy.72
  18.1 0.1 reshape.173
  18.3 0.1 copy.73
  18.4 0.1 reshape.181
  18.6 0.3 bitcast_multiply_fusion
  19.0 12.7 %all-to-all-done = f32[512,4,128]{2,1,0:T(4,128)S(1)} async-done(((f32[512,4,128]{2,1,0:T(4,128)}), f32[512,4,128]{2,1,0:T(4,128)S(1)}, u32[]{:S(2)}, u32[]{:S(2)}) %all-to-all-start) | async-done | bytes 1048608 | tf_op jit(solution)/shard_map/all_to_all | solution.py:61
  31.7 1.0 gather_fusion.1
  32.7 0.9 copy_select_fusion
  33.6 4.2 %all-to-all-start.1 = ((f32[16,16,4,128]{3,1,2,0:T(8,128)}), f32[16,16,4,128]{3,1,2,0:T(8,128)S(1)}, u32[]{:S(2)}, u32[]{:S(2)}) async-start(f32[16,16,4,128]{3,1,2,0:T(8,128)} %copy_select_fusion), calls=%async_computation.1 | async-start | bytes 1048576 | tf_op jit(solution)/shard_map/all_to_all | solution.py:68
  37.8 0.6 pad_clamp_fusion
  38.4 1.6 fusion.2
  40.0 1.4 fusion.31
  41.4 6.3 %all-to-all-done.1 = f32[16,16,4,128]{3,1,2,0:T(8,128)S(1)} async-done(((f32[16,16,4,128]{3,1,2,0:T(8,128)}), f32[16,16,4,128]{3,1,2,0:T(8,128)S(1)}, u32[]{:S(2)}, u32[]{:S(2)}) %all-to-all-start.1) | async-done | bytes 524320 | tf_op jit(solution)/shard_map/all_to_all | solution.py:68
  47.7 0.2 copy.71
  47.9 3.2 %collective-permute-start.5 = (f32[4,16]{1,0:T(4,128)S(1)}, f32[4,16]{1,0:T(4,128)}, u32[]{:S(2)}, u32[]{:S(2)}) collective-permute-start(f32[4,16]{1,0:T(4,128)S(1)} %fusion.2), channel_id=1, source_target_pairs={{0,253},{1,254},{2,255},{3,0},{4,1},{5,2},{6,3},{7,4},{8,5},{9,6},... | collective-permute-start | bytes 776 | tf_op jit(solution)/shard_map/ppermute | solution.py:79
  51.1 2.1 %collective-permute-start.4 = (f32[4,16]{1,0:T(4,128)S(1)}, f32[4,16]{1,0:T(4,128)}, u32[]{:S(2)}, u32[]{:S(2)}) collective-permute-start(f32[4,16]{1,0:T(4,128)S(1)} %fusion.2), channel_id=1, source_target_pairs={{0,254},{1,255},{2,0},{3,1},{4,2},{5,3},{6,4},{7,5},{8,6},{9,7},{1... | collective-permute-start | bytes 776 | tf_op jit(solution)/shard_map/ppermute | solution.py:79
  53.2 1.4 collective-permute-start.3
  54.6 2.1 %collective-permute-start.1 = (f32[4,16]{1,0:T(4,128)S(1)}, f32[4,16]{1,0:T(4,128)}, u32[]{:S(2)}, u32[]{:S(2)}) collective-permute-start(f32[4,16]{1,0:T(4,128)S(1)} %fusion.2), channel_id=1, source_target_pairs={{0,2},{1,3},{2,4},{3,5},{4,6},{5,7},{6,8},{7,9},{8,10},{9,11},{10,... | collective-permute-start | bytes 776 | tf_op jit(solution)/shard_map/ppermute | solution.py:79
  56.8 0.3 pad_maximum_fusion
  57.1 7.9 %gather_fusion.3 = f32[1024,4,128]{2,1,0:T(4,128)} fusion(f32[768,4,128]{2,1,0:T(4,128)S(1)} %pad_maximum_fusion, s32[1024]{0:T(1024)S(1)} %broadcast_clamp_fusion), kind=kCustom, calls=%fused_computation.3 | custom fusion | bytes 4198400 | tf_op jit(solution)/shard_map/gather | solution.py:113
  65.0 6.6 %fusion.30 = (f32[256,4,1,128]{3,2,1,0:T(1,128)S(1)}, f32[256,4,1,128]{3,2,1,0:T(1,128)S(1)}, f32[256,4,1,128]{3,2,1,0:T(1,128)S(1)}, f32[256,4,1,128]{3,2,1,0:T(1,128)}) fusion(f32[256,4,4,128]{3,2,1,0:T(4,128)} %bitcast.115), kind=kLoop, calls=%fused_computation.81 | loop fusion | bytes 4194304 | tf_op jit(solution)/shard_map/slice | solution.py:19
  71.6 7.9 %gather_fusion.2 = f32[1024,4,128]{2,1,0:T(4,128)} fusion(f32[768,4,128]{2,1,0:T(4,128)S(1)} %pad_maximum_fusion, s32[1024]{0:T(1024)S(1)} %broadcast_clamp_fusion.1), kind=kCustom, calls=%fused_computation.2 | custom fusion | bytes 4198400 | tf_op jit(solution)/shard_map/gather | solution.py:113
  79.5 37.8 %multiply_reduce_fusion = f32[256,128]{1,0:T(8,128)S(1)} fusion(f32[256,4,128]{2,1,0:T(4,128)} %bitcast.130, f32[256,128]{1,0:T(8,128)} %bitcast.136, f32[256,4,128]{2,1,0:T(4,128)S(1)} %bitcast.128, f32[256,128]{1,0:T(8,128)} %bitcast.137, f32[256,4,128]{2,1,0:T(4,128)S(1)} %bitcast.129, f32[256,128]{1,0:T(8,128)} %bitcast.138, f32[256,4,128]{2,1,0:T(4,128)S(1)} %bitcast.127), kind=kLoop, calls=%fused_computation.5 | loop fusion | flops 184516608 | bytes 2621440 | tf_op jit(solution)/shard_map/reduce_sum | solution.py:20
  117.4 1.5 fusion.29
  118.9 0.1 collective-permute-start
  119.1 6.3 %collective-permute-done = f32[4,16]{1,0:T(4,128)S(1)} collective-permute-done((f32[4,16]{1,0:T(4,128)S(1)}, f32[4,16]{1,0:T(4,128)S(1)}, u32[]{:S(2)}, u32[]{:S(2)}) %collective-permute-start) | collective-permute-done | bytes 288 | tf_op jit(solution)/shard_map/ppermute | solution.py:79
  125.3 0.8 slice_add_fusion.3
  126.2 0.1 pad_maximum_fusion.1
  126.3 1.1 fusion.3
  127.4 1.4 fusion.1
  128.9 0.6 broadcast_in_dim.28
  129.5 3.5 %all-to-all-start.3 = ((f32[16,2,16]{2,1,0:T(2,128)}), f32[16,2,16]{2,1,0:T(2,128)S(1)}, u32[]{:S(2)}, u32[]{:S(2)}) async-start(f32[16,2,16]{2,1,0:T(2,128)} %broadcast_in_dim.28), calls=%async_computation.3 | async-start | bytes 32768 | tf_op jit(solution)/shard_map/all_to_all | solution.py:98
  133.0 35.8 %multiply_reduce_fusion.1 = f32[256,128]{1,0:T(8,128)S(1)} fusion(f32[256,4,128]{2,1,0:T(4,128)S(1)} %bitcast.126, f32[256,128]{1,0:T(8,128)S(1)} %bitcast.134, f32[256,4,128]{2,1,0:T(4,128)S(1)} %bitcast.124, f32[256,128]{1,0:T(8,128)S(1)} %bitcast.135, f32[256,4,128]{2,1,0:T(4,128)S(1)} %bitcast.125, f32[256,128]{1,0:T(8,128)S(1)} %bitcast.133, ...), kind=kLoop, calls=%fused_computation.6 | loop fusion | flops 184516608 | bytes 2621440 | tf_op jit(solution)/shard_map/reduce_sum | solution.py:20
  168.9 0.1 copy.74
  169.0 0.8 reshape.207
  169.7 11.5 %all-to-all-start.4 = ((f32[16,1,512]{2,1,0:T(1,128)}), f32[16,1,512]{2,1,0:T(1,128)S(1)}, u32[]{:S(2)}, u32[]{:S(2)}) async-start(f32[16,1,512]{2,1,0:T(1,128)} %reshape.207), calls=%async_computation.4 | async-start | bytes 65536 | tf_op jit(solution)/shard_map/all_to_all | solution.py:101
  181.3 0.7 maximum_multiply_fusion
  182.0 6.7 %all-to-all-done.4 = f32[16,1,512]{2,1,0:T(1,128)S(1)} async-done(((f32[16,1,512]{2,1,0:T(1,128)}), f32[16,1,512]{2,1,0:T(1,128)S(1)}, u32[]{:S(2)}, u32[]{:S(2)}) %all-to-all-start.4) | async-done | bytes 32800 | tf_op jit(solution)/shard_map/all_to_all | solution.py:101
  188.7 6.9 %all-to-all-start.2 = ((f32[16,32,128]{2,1,0:T(8,128)}), f32[16,32,128]{2,1,0:T(8,128)S(1)}, u32[]{:S(2)}, u32[]{:S(2)}) async-start(f32[16,32,128]{2,1,0:T(8,128)} %bitcast.34), calls=%async_computation.2 | async-start | bytes 524288 | tf_op jit(solution)/shard_map/all_to_all | solution.py:116
  195.6 0.5 broadcast.150
  196.1 0.7 reduce.2
  196.8 0.1 reshape.208
  196.9 0.2 copy.75
  197.1 0.2 reshape.154
  197.5 0.1 fusion.23
  197.6 0.1 copy.84
  197.7 0.7 div.20
  198.4 5.2 %all-to-all-done.2 = f32[16,32,128]{2,1,0:T(8,128)S(1)} async-done(((f32[16,32,128]{2,1,0:T(8,128)}), f32[16,32,128]{2,1,0:T(8,128)S(1)}, u32[]{:S(2)}, u32[]{:S(2)}) %all-to-all-start.2) | async-done | bytes 262176 | tf_op jit(solution)/shard_map/all_to_all | solution.py:116
  203.7 0.9 gather_fusion.4
  204.5 0.7 bitcast_add_fusion
  (56 shorter events, 0.6 us)
Async XLA Ops:
  0.6 15.2 %copy-start = (s32[1,64]{1,0:T(1,128)S(1)}, s32[1,64]{1,0:T(1,128)}, u32[]{:S(2)}) copy-start(s32[1,64]{1,0:T(1,128)} %param.14) | copy-start | bytes 772
  6.4 9.3 %copy-start.11 = (s32[1,16]{1,0:T(1,128)S(1)}, s32[1,16]{1,0:T(1,128)}, u32[]{:S(2)}) copy-start(s32[1,16]{1,0:T(1,128)} %param.16) | copy-start | bytes 196
  6.4 9.3 %copy-start.9 = (s32[1,16,16]{2,1,0:T(8,128)S(1)}, s32[1,16,16]{2,1,0:T(8,128)}, u32[]{:S(2)}) copy-start(s32[1,16,16]{2,1,0:T(8,128)} %param.15) | copy-start | bytes 3076
  8.1 23.6 %all-to-all-start = ((f32[512,4,128]{2,1,0:T(4,128)}), f32[512,4,128]{2,1,0:T(4,128)S(1)}, u32[]{:S(2)}, u32[]{:S(2)}) async-start(f32[512,4,128]{2,1,0:T(4,128)} %copy.69), calls=%async_computation | async-start | bytes 2097152 | tf_op jit(solution)/shard_map/all_to_all | solution.py:61
  15.9 2.1 %copy-start.10 = (s32[512,4]{0,1:T(4,128)S(1)}, s32[512,4]{0,1:T(4,128)}, u32[]{:S(2)}) copy-start(s32[512,4]{0,1:T(4,128)} %param.17) | copy-start | bytes 24580
  15.9 2.7 %copy-start.2 = (f32[256,128]{1,0:T(8,128)S(1)}, f32[256,128]{1,0:T(8,128)}, u32[]{:S(2)}) copy-start(f32[256,128]{1,0:T(8,128)} %param.11) | copy-start | bytes 393220
  15.9 2.7 %copy-start.3 = (f32[256,3,128]{2,0,1:T(8,128)S(1)}, f32[256,3,128]{2,0,1:T(8,128)}, u32[]{:S(2)}) copy-start(f32[256,3,128]{2,0,1:T(8,128)} %param.10) | copy-start | bytes 1179652
  15.9 3.0 %copy-start.6 = (s32[256,128]{1,0:T(8,128)S(1)}, s32[256,128]{1,0:T(8,128)}, u32[]{:S(2)}) copy-start(s32[256,128]{1,0:T(8,128)} %param.13) | copy-start | bytes 393220
  19.0 19.4 %copy-start.7 = (s32[32768]{0:T(1024)}, s32[32768]{0:T(1024)S(1)}, u32[]{:S(2)}) copy-start(s32[32768]{0:T(1024)S(1)} %add_select_fusion) | copy-start | bytes 393220
  33.6 14.1 %all-to-all-start.1 = ((f32[16,16,4,128]{3,1,2,0:T(8,128)}), f32[16,16,4,128]{3,1,2,0:T(8,128)S(1)}, u32[]{:S(2)}, u32[]{:S(2)}) async-start(f32[16,16,4,128]{3,1,2,0:T(8,128)} %copy_select_fusion), calls=%async_computation.1 | async-start | bytes 1048576 | tf_op jit(solution)/shard_map/all_to_all | solution.py:68
  47.9 71.0 %collective-permute-start.5 = (f32[4,16]{1,0:T(4,128)S(1)}, f32[4,16]{1,0:T(4,128)}, u32[]{:S(2)}, u32[]{:S(2)}) collective-permute-start(f32[4,16]{1,0:T(4,128)S(1)} %fusion.2), channel_id=1, source_target_pairs={{0,253},{1,254},{2,255},{3,0},{4,1},{5,2},{6,3},{7,4},{8,5},{9,6},... | collective-permute-start | bytes 776 | tf_op jit(solution)/shard_map/ppermute | solution.py:79
  51.1 67.9 %collective-permute-start.4 = (f32[4,16]{1,0:T(4,128)S(1)}, f32[4,16]{1,0:T(4,128)}, u32[]{:S(2)}, u32[]{:S(2)}) collective-permute-start(f32[4,16]{1,0:T(4,128)S(1)} %fusion.2), channel_id=1, source_target_pairs={{0,254},{1,255},{2,0},{3,1},{4,2},{5,3},{6,4},{7,5},{8,6},{9,7},{1... | collective-permute-start | bytes 776 | tf_op jit(solution)/shard_map/ppermute | solution.py:79
  53.2 65.9 %collective-permute-start.3 = (f32[4,16]{1,0:T(4,128)S(1)}, f32[4,16]{1,0:T(4,128)}, u32[]{:S(2)}, u32[]{:S(2)}) collective-permute-start(f32[4,16]{1,0:T(4,128)S(1)} %fusion.2), channel_id=1, source_target_pairs={{0,255},{1,0},{2,1},{3,2},{4,3},{5,4},{6,5},{7,6},{8,7},{9,8},{10,... | collective-permute-start | bytes 776 | tf_op jit(solution)/shard_map/ppermute | solution.py:79
  54.6 64.5 %collective-permute-start.2 = (f32[4,16]{1,0:T(4,128)S(1)}, f32[4,16]{1,0:T(4,128)}, u32[]{:S(2)}, u32[]{:S(2)}) collective-permute-start(f32[4,16]{1,0:T(4,128)S(1)} %fusion.2), channel_id=1, source_target_pairs={{0,3},{1,4},{2,5},{3,6},{4,7},{5,8},{6,9},{7,10},{8,11},{9,12},{10... | collective-permute-start | bytes 776 | tf_op jit(solution)/shard_map/ppermute | solution.py:79
  54.6 64.5 %collective-permute-start.1 = (f32[4,16]{1,0:T(4,128)S(1)}, f32[4,16]{1,0:T(4,128)}, u32[]{:S(2)}, u32[]{:S(2)}) collective-permute-start(f32[4,16]{1,0:T(4,128)S(1)} %fusion.2), channel_id=1, source_target_pairs={{0,2},{1,3},{2,4},{3,5},{4,6},{5,7},{6,8},{7,9},{8,10},{9,11},{10,... | collective-permute-start | bytes 776 | tf_op jit(solution)/shard_map/ppermute | solution.py:79
  79.5 37.8 %copy-start.1 = (f32[1024,4,128]{2,1,0:T(4,128)S(1)}, f32[1024,4,128]{2,1,0:T(4,128)}, u32[]{:S(2)}) copy-start(f32[1024,4,128]{2,1,0:T(4,128)} %gather_fusion.2) | copy-start | bytes 6291460
  117.3 8.9 %copy-start.4 = (f32[256,3,128]{2,0,1:T(8,128)S(1)}, f32[256,3,128]{2,0,1:T(8,128)}, u32[]{:S(2)}) copy-start(f32[256,3,128]{2,0,1:T(8,128)} %param.10) | copy-start | bytes 1179652
  117.4 8.9 %copy-start.8 = (s32[32768]{0:T(1024)S(1)}, s32[32768]{0:T(1024)}, u32[]{:S(2)}) copy-start(s32[32768]{0:T(1024)} %copy-done.7) | copy-start | bytes 393220
  118.9 14.1 %copy-start.5 = (f32[256,1,128]{2,1,0:T(1,128)S(1)}, f32[256,1,128]{2,1,0:T(1,128)}, u32[]{:S(2)}) copy-start(f32[256,1,128]{2,1,0:T(1,128)} %get-tuple-element.19) | copy-start | bytes 393220
  118.9 6.4 %collective-permute-start = (f32[4,16]{1,0:T(4,128)S(1)}, f32[4,16]{1,0:T(4,128)S(1)}, u32[]{:S(2)}, u32[]{:S(2)}) collective-permute-start(f32[4,16]{1,0:T(4,128)S(1)} %fusion.2), channel_id=1, source_target_pairs={{0,1},{1,2},{2,3},{3,4},{4,5},{5,6},{6,7},{7,8},{8,9},{9,10},{10,1... | collective-permute-start | bytes 776 | tf_op jit(solution)/shard_map/ppermute | solution.py:79
  129.5 39.4 %all-to-all-start.3 = ((f32[16,2,16]{2,1,0:T(2,128)}), f32[16,2,16]{2,1,0:T(2,128)S(1)}, u32[]{:S(2)}, u32[]{:S(2)}) async-start(f32[16,2,16]{2,1,0:T(2,128)} %broadcast_in_dim.28), calls=%async_computation.3 | async-start | bytes 32768 | tf_op jit(solution)/shard_map/all_to_all | solution.py:98
  169.7 18.9 %all-to-all-start.4 = ((f32[16,1,512]{2,1,0:T(1,128)}), f32[16,1,512]{2,1,0:T(1,128)S(1)}, u32[]{:S(2)}, u32[]{:S(2)}) async-start(f32[16,1,512]{2,1,0:T(1,128)} %reshape.207), calls=%async_computation.4 | async-start | bytes 65536 | tf_op jit(solution)/shard_map/all_to_all | solution.py:101
  188.7 15.0 %all-to-all-start.2 = ((f32[16,32,128]{2,1,0:T(8,128)}), f32[16,32,128]{2,1,0:T(8,128)S(1)}, u32[]{:S(2)}, u32[]{:S(2)}) async-start(f32[16,32,128]{2,1,0:T(8,128)} %bitcast.34), calls=%async_computation.2 | async-start | bytes 524288 | tf_op jit(solution)/shard_map/all_to_all | solution.py:116

commit v6 on v5

--- a/solution.py
+++ b/solution.py
@@ -65,22 +65,26 @@
     live = jnp.arange(per_peer, dtype=jnp.int32)[None, :] < send_count[0][:, None]
     sending = owned.at[pick].get(mode="promise_in_bounds")
     sending = jnp.where(live[:, :, None, None], sending, jnp.zeros_like(sending))
-    remote = lax.all_to_all(sending, "grp", split_axis=0, concat_axis=0, tiled=True)
-    remote = remote.reshape(owners * per_peer, 4, leaf_width)
+    blocks = lax.axis_size("dom") * owners
+    quarters = GSPAN // GROUP_DEV
+    first_sums = local_sums(jnp.concatenate([mass_flat[None, :], mass_flat[None, :] * speeds], axis=0))
+    leaf_size = per_peer * 4 * leaf_width
+    packed = jnp.concatenate(
+        [sending.reshape(owners, leaf_size), jnp.broadcast_to(first_sums.reshape(1, -1), (owners, first_sums.size))],
+        axis=1,
+    )
+    packed = lax.all_to_all(packed, "grp", split_axis=0, concat_axis=0, tiled=True)
+    remote = packed[:, :leaf_size].reshape(owners * per_peer, 4, leaf_width)
+    row_sums = packed[:, leaf_size:].reshape((owners,) + first_sums.shape)
+    domains = lax.axis_size("dom")
+    before = lax.ppermute(row_sums, "dom", [(i, (i + 1) % domains) for i in range(domains)])
+    after = lax.ppermute(row_sums, "dom", [(i, (i - 1) % domains) for i in range(domains)])
+    three_rows = jnp.concatenate([before, row_sums, after], axis=0)
+    span = 2 * quarters - 1
+    window = lax.dynamic_slice_in_dim(three_rows, owners + lax.axis_index("grp") - (quarters - 1), span, axis=0)
+    near_sums = {step: window[step + quarters - 1] for step in range(-quarters + 1, quarters)}
     combined = jnp.concatenate([owned, remote], axis=0)
 
-    blocks = lax.axis_size("dom") * owners
-    quarters = GSPAN // GROUP_DEV
-
-    def from_block(value, step):
-        if step == 0:
-            return value
-        ring = [(i, (i - step) % blocks) for i in range(blocks)]
-        return lax.ppermute(value, ("dom", "grp"), ring)
-
-    first_sums = local_sums(jnp.concatenate([mass_flat[None, :], mass_flat[None, :] * speeds], axis=0))
-    first_sums, remote = lax.optimization_barrier((first_sums, remote))
-    near_sums = {step: from_block(first_sums, step) for step in range(-quarters + 1, quarters)}
     near_parts = []
     for ahead in range(quarters):
         part = 0.0
@@ -96,7 +100,6 @@
     partial = jnp.stack([heat_local, first_sums[0]])
     across = jnp.broadcast_to(partial[None], (owners,) + partial.shape)
     across = lax.all_to_all(across, "grp", split_axis=0, concat_axis=0, tiled=True)
-    domains = lax.axis_size("dom")
     every = jnp.broadcast_to(across[None], (domains,) + across.shape)
     every = lax.all_to_all(every, "dom", split_axis=0, concat_axis=0, tiled=True)
     every = every.reshape(blocks, 2, quarters, GROUP_DEV)

time: 206 us -> 193 us (0.937)
  starting transfers between devices: 42.6 us -> 33.8 us
  waiting for transfers between devices: 37.2 us -> 30.9 us
  local copies, waits for them, and re-layouts: 37.6 us -> 41 us
    ppermute x6 -> x2, waiting for transfers between devices: 6.28 us -> 0.01 us  [the longest x1 0.01 us: shards(): lax.ppermute(row_sums, 'dom', [(i, (i - 1) % domains) for i in range(doma...]
    ppermute x6 -> x2, starting transfers between devices: 8.93 us -> 4.15 us  [the longest x1 2.61 us: shards(): lax.ppermute(row_sums, 'dom', [(i, (i - 1) % domains) for i in range(doma...]
    all_to_all x1, starting transfers between devices: 11.5 us -> 7.68 us  [shards(): lax.all_to_all(every, 'dom', split_axis=0, concat_axis=0, tiled=True)]
    all_to_all x1, waiting for transfers between devices: 6.3 us -> 8.52 us  [shards(): lax.all_to_all(packed, 'grp', split_axis=0, concat_axis=0, tiled=True)]
    all_to_all x1, waiting for transfers between devices: 12.7 us -> 10.5 us  [shards(): lax.all_to_all(outgoing, 'grp', split_axis=0, concat_axis=0, tiled=True)]
  transfers between devices with their start and end apart: 11 -> 7, of which waited for: 5 -> 4; matrix products, arithmetic and copies ran while one was open for 53% -> 56% of each run, Pallas kernels for 0% -> 0%
where the time goes in v6:
time: 193 us; the launch traced here: 192 us
  other arithmetic  80.6 us (42%)
  local copies, waits for them, and re-layouts  41 us (21%)
  starting transfers between devices  33.8 us (18%)
  waiting for transfers between devices  30.9 us (16%)
  matrix products  4.8 us (2%)
    reduce_sum x2, other arithmetic, tile_potential(): return -jnp.sum(weights, axis=(1, 3))  73.6 us
    gather x2, local copies, waits for them, and re-layouts, shards(): sources = combined.at[rows].get(mode='promise_in_bounds')  15.9 us
    all_to_all x1, waiting for transfers between devices, shards(): lax.all_to_all(outgoing, 'grp', split_axis=0, concat_axis=0, tiled=True)  10.5 us
    all_to_all x1, waiting for transfers between devices, shards(): lax.all_to_all(packed, 'grp', split_axis=0, concat_axis=0, tiled=True)  8.52 us
    slice x2, local copies, waits for them, and re-layouts, tile_potential(): weights = sources[:, :, 3, None, :] * lax.rsqrt(distance)  8.19 us
    all_to_all x1, starting transfers between devices, shards(): lax.all_to_all(every, 'dom', split_axis=0, concat_axis=0, tiled=True)  7.68 us
    all_to_all x1, starting transfers between devices, shards(): lax.all_to_all(outgoing, 'grp', split_axis=0, concat_axis=0, tiled=True)  7.57 us
    all_to_all x1, waiting for transfers between devices, shards(): lax.all_to_all(every, 'dom', split_axis=0, concat_axis=0, tiled=True)  6.68 us
  transfers between devices with their start and end apart: 7, of which 4 were waited for; matrix products, arithmetic and copies ran while one was open for 56% of the time, Pallas kernels for 0%

profile of v6, /device:TPU:1, one launch (start us, length us, event | category | flops | bytes accessed | tf_op | source)
XLA Modules:
  0.0 192.3 jit_solution(15331880921726310401)
XLA Ops:
  0.6 0.7 fusion.20
  1.3 0.6 reduce-window.6
  1.9 0.2 slice_reduce_fusion.7
  2.1 0.8 fusion.19
  2.9 0.7 compare_select_fusion.4
  3.6 1.0 copy.90
  4.6 1.2 copy.91
  5.8 0.6 fusion.7
  6.4 1.7 copy.92
  8.1 7.6 %all-to-all-start = ((f32[512,4,128]{2,1,0:T(4,128)}), f32[512,4,128]{2,1,0:T(4,128)S(1)}, u32[]{:S(2)}, u32[]{:S(2)}) async-start(f32[512,4,128]{2,1,0:T(4,128)} %copy.92), calls=%async_computation | async-start | bytes 2097152 | tf_op jit(solution)/shard_map/all_to_all | solution.py:61
  15.7 0.1 reshape.170
  15.8 1.9 gather_fusion
  17.7 0.1 gather.18
  17.9 0.3 bitcast_multiply_fusion
  18.3 1.6 fusion.2
  19.9 0.1 reshape.227
  20.0 0.5 copy-done.13
  20.5 0.1 reshape.178
  20.6 0.1 copy.97
  20.7 0.1 reshape.186
  20.8 0.1 copy.98
  21.0 0.1 reshape.194
  21.2 10.5 %all-to-all-done = f32[512,4,128]{2,1,0:T(4,128)S(1)} async-done(((f32[512,4,128]{2,1,0:T(4,128)}), f32[512,4,128]{2,1,0:T(4,128)S(1)}, u32[]{:S(2)}, u32[]{:S(2)}) %all-to-all-start) | async-done | bytes 1048608 | tf_op jit(solution)/shard_map/all_to_all | solution.py:61
  31.7 1.0 gather_fusion.1
  32.7 0.3 broadcast_select_fusion
  33.1 0.2 select_n.54
  33.4 1.3 copy.93
  34.7 4.2 %all-to-all-start.1 = ((f32[16,1,8256]{2,1,0:T(1,128)}), f32[16,1,8256]{2,1,0:T(1,128)S(1)}, u32[]{:S(2)}, u32[]{:S(2)}) async-start(f32[16,1,8256]{2,1,0:T(1,128)} %copy.93), calls=%async_computation.1 | async-start | bytes 1064960 | tf_op jit(solution)/shard_map/all_to_all | solution.py:76
  39.0 1.4 fusion.31
  40.4 8.5 %all-to-all-done.1 = f32[16,1,8256]{2,1,0:T(1,128)S(1)} async-done(((f32[16,1,8256]{2,1,0:T(1,128)}), f32[16,1,8256]{2,1,0:T(1,128)S(1)}, u32[]{:S(2)}, u32[]{:S(2)}) %all-to-all-start.1) | async-done | bytes 528416 | tf_op jit(solution)/shard_map/all_to_all | solution.py:76
  49.0 0.7 copy.112
  49.7 2.6 %collective-permute-start.1 = (f32[16,4,16]{0,2,1:T(8,128)}, f32[16,4,16]{0,2,1:T(8,128)}, u32[]{:S(2)}, u32[]{:S(2)}) collective-permute-start(f32[16,4,16]{0,2,1:T(8,128)} %bitcast.47), channel_id=1, source_target_pairs={{0,240},{16,0},{32,16},{48,32},{64,48},{80,64},{96,80},{112,96},{1... | collective-permute-start | bytes 12296 | tf_op jit(solution)/shard_map/ppermute | solution.py:81
  52.3 1.5 collective-permute-start
  53.8 0.3 reshape.166
  54.3 7.9 %gather_fusion.3 = f32[1024,4,128]{2,1,0:T(4,128)} fusion(f32[768,4,128]{2,1,0:T(4,128)S(1)} %constant_dynamic-update-slice_fusion, s32[1024]{0:T(1024)S(1)} %get-tuple-element.32), kind=kCustom, calls=%fused_computation.3 | custom fusion | bytes 4198400 | tf_op jit(solution)/shard_map/gather | solution.py:116
  62.2 6.6 %fusion.30 = (f32[256,4,1,128]{3,2,1,0:T(1,128)S(1)}, f32[256,4,1,128]{3,2,1,0:T(1,128)S(1)}, f32[256,4,1,128]{3,2,1,0:T(1,128)S(1)}, f32[256,4,1,128]{3,2,1,0:T(1,128)}) fusion(f32[256,4,4,128]{3,2,1,0:T(4,128)} %bitcast.120), kind=kLoop, calls=%fused_computation.93 | loop fusion | bytes 4194304 | tf_op jit(solution)/shard_map/slice | solution.py:19
  68.9 7.9 %gather_fusion.2 = f32[1024,4,128]{2,1,0:T(4,128)} fusion(f32[768,4,128]{2,1,0:T(4,128)S(1)} %constant_dynamic-update-slice_fusion, s32[1024]{0:T(1024)S(1)} %broadcast_clamp_fusion.1), kind=kCustom, calls=%fused_computation.2 | custom fusion | bytes 4198400 | tf_op jit(solution)/shard_map/gather | solution.py:116
  76.8 37.8 %multiply_reduce_fusion = f32[256,128]{1,0:T(8,128)S(1)} fusion(f32[256,4,128]{2,1,0:T(4,128)} %bitcast.136, f32[256,128]{1,0:T(8,128)S(1)} %bitcast.142, f32[256,4,128]{2,1,0:T(4,128)S(1)} %bitcast.134, f32[256,128]{1,0:T(8,128)} %bitcast.143, f32[256,4,128]{2,1,0:T(4,128)S(1)} %bitcast.135, f32[256,128]{1,0:T(8,128)} %bitcast.144, ...), kind=kLoop, calls=%fused_computation.5 | loop fusion | flops 184516608 | bytes 2621440 | tf_op jit(solution)/shard_map/reduce_sum | solution.py:20
  114.6 1.5 fusion.29
  116.2 1.0 dynamic-slice_maximum_fusion
  117.2 0.2 slice_reduce_fusion.3
  117.4 0.1 slice_add_fusion.3
  117.5 0.1 pad_maximum_fusion
  117.6 1.1 fusion.3
  118.8 1.4 fusion.1
  120.2 0.6 broadcast_in_dim.61
  120.8 3.5 %all-to-all-start.3 = ((f32[16,2,16]{2,1,0:T(2,128)}), f32[16,2,16]{2,1,0:T(2,128)S(1)}, u32[]{:S(2)}, u32[]{:S(2)}) async-start(f32[16,2,16]{2,1,0:T(2,128)} %broadcast_in_dim.61), calls=%async_computation.3 | async-start | bytes 32768 | tf_op jit(solution)/shard_map/all_to_all | solution.py:102
  124.3 35.8 %multiply_reduce_fusion.1 = f32[256,128]{1,0:T(8,128)S(1)} fusion(f32[256,4,128]{2,1,0:T(4,128)S(1)} %bitcast.132, f32[256,128]{1,0:T(8,128)S(1)} %bitcast.140, f32[256,4,128]{2,1,0:T(4,128)S(1)} %bitcast.130, f32[256,128]{1,0:T(8,128)S(1)} %bitcast.141, f32[256,4,128]{2,1,0:T(4,128)S(1)} %bitcast.131, f32[256,128]{1,0:T(8,128)S(1)} %bitcast.139, ...), kind=kLoop, calls=%fused_computation.6 | loop fusion | flops 184516608 | bytes 2621440 | tf_op jit(solution)/shard_map/reduce_sum | solution.py:20
  160.3 0.8 reshape.228
  161.1 7.7 %all-to-all-start.4 = ((f32[16,1,512]{2,1,0:T(1,128)}), f32[16,1,512]{2,1,0:T(1,128)S(1)}, u32[]{:S(2)}, u32[]{:S(2)}) async-start(f32[16,1,512]{2,1,0:T(1,128)} %reshape.228), calls=%async_computation.4 | async-start | bytes 65536 | tf_op jit(solution)/shard_map/all_to_all | solution.py:104
  168.8 0.7 maximum_multiply_fusion
  169.5 6.7 %all-to-all-done.4 = f32[16,1,512]{2,1,0:T(1,128)S(1)} async-done(((f32[16,1,512]{2,1,0:T(1,128)}), f32[16,1,512]{2,1,0:T(1,128)S(1)}, u32[]{:S(2)}, u32[]{:S(2)}) %all-to-all-start.4) | async-done | bytes 32800 | tf_op jit(solution)/shard_map/all_to_all | solution.py:104
  176.1 6.7 %all-to-all-start.2 = ((f32[16,32,128]{2,1,0:T(8,128)}), f32[16,32,128]{2,1,0:T(8,128)S(1)}, u32[]{:S(2)}, u32[]{:S(2)}) async-start(f32[16,32,128]{2,1,0:T(8,128)} %bitcast.34), calls=%async_computation.2 | async-start | bytes 524288 | tf_op jit(solution)/shard_map/all_to_all | solution.py:119
  182.8 0.5 broadcast.163
  183.3 0.7 reduce.16
  184.1 0.1 reshape.229
  184.2 0.2 copy.100
  184.4 0.2 reshape.167
  184.7 0.1 fusion.23
  184.8 0.1 copy.109
  185.0 0.7 div.20
  185.7 5.2 %all-to-all-done.2 = f32[16,32,128]{2,1,0:T(8,128)S(1)} async-done(((f32[16,32,128]{2,1,0:T(8,128)}), f32[16,32,128]{2,1,0:T(8,128)S(1)}, u32[]{:S(2)}, u32[]{:S(2)}) %all-to-all-start.2) | async-done | bytes 262176 | tf_op jit(solution)/shard_map/all_to_all | solution.py:119
  190.9 0.7 gather_fusion.4
  191.7 0.7 bitcast_add_fusion
  (66 shorter events, 1.0 us)
Async XLA Ops:
  0.6 15.2 %copy-start = (s32[1,64]{1,0:T(1,128)S(1)}, s32[1,64]{1,0:T(1,128)}, u32[]{:S(2)}) copy-start(s32[1,64]{1,0:T(1,128)} %param.14) | copy-start | bytes 772
  6.4 9.3 %copy-start.11 = (s32[1,16,16]{2,1,0:T(8,128)S(1)}, s32[1,16,16]{2,1,0:T(8,128)}, u32[]{:S(2)}) copy-start(s32[1,16,16]{2,1,0:T(8,128)} %param.15) | copy-start | bytes 3076
  8.1 23.6 %all-to-all-start = ((f32[512,4,128]{2,1,0:T(4,128)}), f32[512,4,128]{2,1,0:T(4,128)S(1)}, u32[]{:S(2)}, u32[]{:S(2)}) async-start(f32[512,4,128]{2,1,0:T(4,128)} %copy.92), calls=%async_computation | async-start | bytes 2097152 | tf_op jit(solution)/shard_map/all_to_all | solution.py:61
  15.8 2.0 %copy-start.8 = (s32[256,128]{1,0:T(8,128)S(1)}, s32[256,128]{1,0:T(8,128)}, u32[]{:S(2)}) copy-start(s32[256,128]{1,0:T(8,128)} %param.13) | copy-start | bytes 393220
  15.8 2.1 %copy-start.2 = (f32[256,128]{1,0:T(8,128)S(1)}, f32[256,128]{1,0:T(8,128)}, u32[]{:S(2)}) copy-start(f32[256,128]{1,0:T(8,128)} %param.11) | copy-start | bytes 393220
  15.8 2.1 %copy-start.3 = (f32[256,3,128]{2,0,1:T(8,128)S(1)}, f32[256,3,128]{2,0,1:T(8,128)}, u32[]{:S(2)}) copy-start(f32[256,3,128]{2,0,1:T(8,128)} %param.10) | copy-start | bytes 1179652
  17.7 2.8 %copy-start.12 = (s32[512,4]{0,1:T(4,128)S(1)}, s32[512,4]{0,1:T(4,128)}, u32[]{:S(2)}) copy-start(s32[512,4]{0,1:T(4,128)} %param.17) | copy-start | bytes 24580
  17.7 3.4 %copy-start.14 = (s32[1,16]{1,0:T(1,128)S(1)}, s32[1,16]{1,0:T(1,128)}, u32[]{:S(2)}) copy-start(s32[1,16]{1,0:T(1,128)} %param.16) | copy-start | bytes 196
  17.9 2.0 %copy-start.9 = (s32[32768]{0:T(1024)}, s32[32768]{0:T(1024)S(1)}, u32[]{:S(2)}) copy-start(s32[32768]{0:T(1024)S(1)} %add_select_fusion) | copy-start | bytes 393220
  19.9 0.6 copy-start.13
  34.7 14.2 %all-to-all-start.1 = ((f32[16,1,8256]{2,1,0:T(1,128)}), f32[16,1,8256]{2,1,0:T(1,128)S(1)}, u32[]{:S(2)}, u32[]{:S(2)}) async-start(f32[16,1,8256]{2,1,0:T(1,128)} %copy.93), calls=%async_computation.1 | async-start | bytes 1064960 | tf_op jit(solution)/shard_map/all_to_all | solution.py:76
  49.7 66.5 %collective-permute-start.1 = (f32[16,4,16]{0,2,1:T(8,128)}, f32[16,4,16]{0,2,1:T(8,128)}, u32[]{:S(2)}, u32[]{:S(2)}) collective-permute-start(f32[16,4,16]{0,2,1:T(8,128)} %bitcast.47), channel_id=1, source_target_pairs={{0,240},{16,0},{32,16},{48,32},{64,48},{80,64},{96,80},{112,96},{1... | collective-permute-start | bytes 12296 | tf_op jit(solution)/shard_map/ppermute | solution.py:81
  52.3 63.9 %collective-permute-start = (f32[16,4,16]{0,2,1:T(8,128)}, f32[16,4,16]{0,2,1:T(8,128)}, u32[]{:S(2)}, u32[]{:S(2)}) collective-permute-start(f32[16,4,16]{0,2,1:T(8,128)} %bitcast.47), channel_id=1, source_target_pairs={{0,16},{16,32},{32,48},{48,64},{64,80},{80,96},{96,112},{112,128},... | collective-permute-start | bytes 12296 | tf_op jit(solution)/shard_map/ppermute | solution.py:80
  68.9 7.9 %copy-start.7 = (f32[256,1,128]{2,1,0:T(1,128)S(1)}, f32[256,1,128]{2,1,0:T(1,128)}, u32[]{:S(2)}) copy-start(f32[256,1,128]{2,1,0:T(1,128)} %get-tuple-element.20) | copy-start | bytes 393220
  76.8 37.8 %copy-start.1 = (f32[1024,4,128]{2,1,0:T(4,128)S(1)}, f32[1024,4,128]{2,1,0:T(4,128)}, u32[]{:S(2)}) copy-start(f32[1024,4,128]{2,1,0:T(4,128)} %gather_fusion.2) | copy-start | bytes 6291460
  114.6 3.0 %copy-start.4 = (f32[256,3,128]{2,0,1:T(8,128)S(1)}, f32[256,3,128]{2,0,1:T(8,128)}, u32[]{:S(2)}) copy-start(f32[256,3,128]{2,0,1:T(8,128)} %param.10) | copy-start | bytes 1179652
  114.6 3.0 %copy-start.10 = (s32[32768]{0:T(1024)S(1)}, s32[32768]{0:T(1024)}, u32[]{:S(2)}) copy-start(s32[32768]{0:T(1024)} %copy-done.9) | copy-start | bytes 393220
  116.1 4.0 %slice-start = ((f32[4,16]{1,0:T(4,128)}), f32[1,16]{1,0:T(1,128)S(1)}, s32[]{:S(2)}) async-start(f32[4,16]{1,0:T(4,128)} %copy-done.13), calls=%async_computation.5 | async-start | bytes 1024 | tf_op jit(solution)/shard_map/slice | solution.py:100
  116.2 8.2 %copy-start.5 = (f32[256,1,128]{2,1,0:T(1,128)S(1)}, f32[256,1,128]{2,1,0:T(1,128)}, u32[]{:S(2)}) copy-start(f32[256,1,128]{2,1,0:T(1,128)} %get-tuple-element.23) | copy-start | bytes 393220
  116.2 8.2 %copy-start.6 = (f32[256,1,128]{2,1,0:T(1,128)S(1)}, f32[256,1,128]{2,1,0:T(1,128)}, u32[]{:S(2)}) copy-start(f32[256,1,128]{2,1,0:T(1,128)} %get-tuple-element.24) | copy-start | bytes 393220
  120.8 39.4 %all-to-all-start.3 = ((f32[16,2,16]{2,1,0:T(2,128)}), f32[16,2,16]{2,1,0:T(2,128)S(1)}, u32[]{:S(2)}, u32[]{:S(2)}) async-start(f32[16,2,16]{2,1,0:T(2,128)} %broadcast_in_dim.61), calls=%async_computation.3 | async-start | bytes 32768 | tf_op jit(solution)/shard_map/all_to_all | solution.py:102
  161.1 15.1 %all-to-all-start.4 = ((f32[16,1,512]{2,1,0:T(1,128)}), f32[16,1,512]{2,1,0:T(1,128)S(1)}, u32[]{:S(2)}, u32[]{:S(2)}) async-start(f32[16,1,512]{2,1,0:T(1,128)} %reshape.228), calls=%async_computation.4 | async-start | bytes 65536 | tf_op jit(solution)/shard_map/all_to_all | solution.py:104
  176.1 14.8 %all-to-all-start.2 = ((f32[16,32,128]{2,1,0:T(8,128)}), f32[16,32,128]{2,1,0:T(8,128)S(1)}, u32[]{:S(2)}, u32[]{:S(2)}) async-start(f32[16,32,128]{2,1,0:T(8,128)} %bitcast.34), calls=%async_computation.2 | async-start | bytes 524288 | tf_op jit(solution)/shard_map/all_to_all | solution.py:119

commit v7 on v6

--- a/solution.py
+++ b/solution.py
@@ -20,7 +20,7 @@
     return -jnp.sum(weights, axis=(1, 3))
 
 
-def shards(
+def layer(
     positions,
     velocities,
     masses,
@@ -98,15 +98,8 @@
     kinetic = 0.5 * jnp.sum(relative * relative, axis=0)
     heat_local = local_sums((mass_flat * kinetic)[None, :])[0]
     partial = jnp.stack([heat_local, first_sums[0]])
-    across = jnp.broadcast_to(partial[None], (owners,) + partial.shape)
-    across = lax.all_to_all(across, "grp", split_axis=0, concat_axis=0, tiled=True)
-    every = jnp.broadcast_to(across[None], (domains,) + across.shape)
-    every = lax.all_to_all(every, "dom", split_axis=0, concat_axis=0, tiled=True)
-    every = every.reshape(blocks, 2, quarters, GROUP_DEV)
-    totals = every[:, :, 0, :]
-    for back in range(1, quarters):
-        totals = totals + jnp.roll(every[:, :, back, :], back, axis=0)
-    group_kinetic = totals[:, 0, :].reshape(groups) / totals[:, 1, :].reshape(groups)
+    down = jnp.broadcast_to(partial[None], (domains,) + partial.shape)
+    down = lax.all_to_all(down, "dom", split_axis=0, concat_axis=0, tiled=True)
 
     coupling = 1.0 / (partners.shape[1] * leaf_width)
     halves = []
@@ -116,7 +109,16 @@
         sources = combined.at[rows].get(mode="promise_in_bounds")
         halves.append(tile_potential(owned[part * half:(part + 1) * half], sources))
     potential = jnp.concatenate(halves, axis=0) * coupling
-    returned = lax.all_to_all(potential, "grp", split_axis=0, concat_axis=0, tiled=True)
+    flat = potential.reshape(owners, capacity * leaf_width)
+    extra = jnp.broadcast_to(down.reshape(1, -1), (owners, down.size))
+    back = lax.all_to_all(jnp.concatenate([flat, extra], axis=1), "grp", split_axis=0, concat_axis=0, tiled=True)
+    returned = back[:, :capacity * leaf_width].reshape(slot_count, leaf_width)
+    every = back[:, capacity * leaf_width:].reshape((owners, domains) + partial.shape)
+    every = jnp.transpose(every, (1, 0, 2, 3)).reshape(blocks, 2, quarters, GROUP_DEV)
+    totals = every[:, :, 0, :]
+    for shift in range(1, quarters):
+        totals = totals + jnp.roll(every[:, :, shift, :], shift, axis=0)
+    group_kinetic = totals[:, 0, :].reshape(groups) / totals[:, 1, :].reshape(groups)
     own_potential = returned.at[target].get(mode="promise_in_bounds")
     energy = kinetic.reshape(leaves, leaf_width) + own_potential
     return (energy, group_kinetic)
@@ -135,4 +137,4 @@
         P(("dom", "grp"), None),
     )
     out_specs = (P(("dom", "grp"), None), P())
-    return jax.shard_map(shards, mesh=mesh, in_specs=in_specs, out_specs=out_specs, check_vma=False)
+    return jax.shard_map(layer, mesh=mesh, in_specs=in_specs, out_specs=out_specs, check_vma=False)

time: 193 us -> 188 us (0.974)
  blocking collectives: 0 us -> 11.1 us
  starting transfers between devices: 33.8 us -> 23.6 us
  other arithmetic: 80.6 us -> 76.2 us
  waiting for transfers between devices: 30.9 us -> 26.8 us
  local copies, waits for them, and re-layouts: 41 us -> 43.7 us
    all_to_all x0 -> x1, blocking collectives: none -> 11.1 us  [layer(): lax.all_to_all(jnp.concatenate([flat, extra], axis=1), 'grp', split_axis=...]
    all_to_all x5 -> x3, starting transfers between devices: 29.6 us -> 19.5 us  [the longest x1 7.68 us: layer(): down = lax.all_to_all(down, 'dom', split_axis=0, concat_axis=0, tiled=True)]
    slice x2, local copies, waits for them, and re-layouts: 8.19 us -> 12.5 us  [tile_potential(): weights = sources[:, :, 3, None, :] * lax.rsqrt(distance)]
    all_to_all x5 -> x3, waiting for transfers between devices: 30.9 us -> 26.8 us  [the longest x1 11 us: layer(): lax.all_to_all(outgoing, 'grp', split_axis=0, concat_axis=0, tiled=True)]
    reduce_sum x2, other arithmetic: 73.6 us -> 71.4 us  [tile_potential(): return -jnp.sum(weights, axis=(1, 3))]
  transfers between devices with their start and end apart: 7 -> 5, of which waited for: 4 -> 3; matrix products, arithmetic and copies ran while one was open for 56% -> 57% of each run, Pallas kernels for 0% -> 0%
where the time goes in v7:
time: 188 us; the launch traced here: 187 us
  other arithmetic  76.2 us (41%)
  local copies, waits for them, and re-layouts  43.7 us (23%)
  waiting for transfers between devices  26.8 us (14%)
  starting transfers between devices  23.6 us (13%)
  blocking collectives  11.1 us (6%)
  matrix products  4.79 us (3%)
    reduce_sum x2, other arithmetic, tile_potential(): return -jnp.sum(weights, axis=(1, 3))  71.4 us
    gather x2, local copies, waits for them, and re-layouts, layer(): sources = combined.at[rows].get(mode='promise_in_bounds')  15.9 us
    slice x2, local copies, waits for them, and re-layouts, tile_potential(): weights = sources[:, :, 3, None, :] * lax.rsqrt(distance)  12.5 us
    all_to_all x1, blocking collectives, layer(): lax.all_to_all(jnp.concatenate([flat, extra], axis=1), 'grp', split_axis=...  11.1 us
    all_to_all x1, waiting for transfers between devices, layer(): lax.all_to_all(outgoing, 'grp', split_axis=0, concat_axis=0, tiled=True)  11 us
    all_to_all x1, waiting for transfers between devices, layer(): lax.all_to_all(packed, 'grp', split_axis=0, concat_axis=0, tiled=True)  8.5 us
    all_to_all x1, starting transfers between devices, layer(): down = lax.all_to_all(down, 'dom', split_axis=0, concat_axis=0, tiled=True)  7.68 us
    all_to_all x1, starting transfers between devices, layer(): lax.all_to_all(outgoing, 'grp', split_axis=0, concat_axis=0, tiled=True)  7.57 us
  transfers between devices with their start and end apart: 5, of which 3 were waited for; matrix products, arithmetic and copies ran while one was open for 57% of the time, Pallas kernels for 0%

profile of v7, /device:TPU:1, one launch (start us, length us, event | category | flops | bytes accessed | tf_op | source)
XLA Modules:
  0.0 187.4 jit_solution(1635062981733963933)
XLA Ops:
  0.6 0.7 fusion.20
  1.3 0.6 reduce-window.6
  1.9 0.2 slice_reduce_fusion.7
  2.1 0.8 fusion.19
  2.9 0.7 compare_select_fusion.4
  3.6 1.0 copy.89
  4.6 1.2 copy.90
  5.8 0.6 fusion.7
  6.4 1.7 copy.91
  8.1 7.6 %all-to-all-start = ((f32[512,4,128]{2,1,0:T(4,128)}), f32[512,4,128]{2,1,0:T(4,128)S(1)}, u32[]{:S(2)}, u32[]{:S(2)}) async-start(f32[512,4,128]{2,1,0:T(4,128)} %copy.91), calls=%async_computation | async-start | bytes 2097152 | tf_op jit(solution)/shard_map/all_to_all | solution.py:61
  15.7 0.1 reshape.180
  15.8 1.9 gather_fusion
  17.7 0.1 gather.18
  17.9 0.3 bitcast_multiply_fusion
  18.3 0.1 reshape.188
  18.4 0.1 copy.96
  18.5 0.1 reshape.196
  18.6 0.1 copy.97
  18.8 0.1 reshape.204
  18.9 1.6 fusion.2
  20.5 0.1 reshape.237
  20.6 0.1 iota_compare_fusion.9
  20.7 11.0 %all-to-all-done = f32[512,4,128]{2,1,0:T(4,128)S(1)} async-done(((f32[512,4,128]{2,1,0:T(4,128)}), f32[512,4,128]{2,1,0:T(4,128)S(1)}, u32[]{:S(2)}, u32[]{:S(2)}) %all-to-all-start) | async-done | bytes 1048608 | tf_op jit(solution)/shard_map/all_to_all | solution.py:61
  31.7 1.0 gather_fusion.1
  32.7 0.3 broadcast_select_fusion
  33.1 0.2 select_n.54
  33.4 1.3 copy.92
  34.7 4.2 %all-to-all-start.1 = ((f32[16,1,8256]{2,1,0:T(1,128)}), f32[16,1,8256]{2,1,0:T(1,128)S(1)}, u32[]{:S(2)}, u32[]{:S(2)}) async-start(f32[16,1,8256]{2,1,0:T(1,128)} %copy.92), calls=%async_computation.1 | async-start | bytes 1064960 | tf_op jit(solution)/shard_map/all_to_all | solution.py:76
  39.0 1.4 fusion.31
  40.4 8.5 %all-to-all-done.1 = f32[16,1,8256]{2,1,0:T(1,128)S(1)} async-done(((f32[16,1,8256]{2,1,0:T(1,128)}), f32[16,1,8256]{2,1,0:T(1,128)S(1)}, u32[]{:S(2)}, u32[]{:S(2)}) %all-to-all-start.1) | async-done | bytes 528416 | tf_op jit(solution)/shard_map/all_to_all | solution.py:76
  49.0 0.1 copy.110
  49.1 2.6 %collective-permute-start.1 = (f32[16,4,16]{0,2,1:T(8,128)S(1)}, f32[16,4,16]{0,2,1:T(8,128)S(1)}, u32[]{:S(2)}, u32[]{:S(2)}) collective-permute-start(f32[16,4,16]{0,2,1:T(8,128)S(1)} %bitcast.146), channel_id=1, source_target_pairs={{0,240},{16,0},{32,16},{48,32},{64,48},{80,64},{96,80},{112,96},{1... | collective-permute-start | bytes 12296 | tf_op jit(solution)/shard_map/ppermute | solution.py:81
  51.7 1.5 collective-permute-start
  53.3 0.3 reshape.174
  53.6 0.1 constant_dynamic-update-slice_fusion
  53.7 7.9 %gather_fusion.3 = f32[1024,4,128]{2,1,0:T(4,128)} fusion(f32[768,4,128]{2,1,0:T(4,128)S(1)} %constant_dynamic-update-slice_fusion, s32[1024]{0:T(1024)S(1)} %get-tuple-element.33), kind=kCustom, calls=%fused_computation.3 | custom fusion | bytes 4198400 | tf_op jit(solution)/shard_map/gather | solution.py:109
  61.6 6.6 %fusion.30 = (f32[256,4,1,128]{3,2,1,0:T(1,128)S(1)}, f32[256,4,1,128]{3,2,1,0:T(1,128)S(1)}, f32[256,4,1,128]{3,2,1,0:T(1,128)S(1)}, f32[256,4,1,128]{3,2,1,0:T(1,128)}) fusion(f32[256,4,4,128]{3,2,1,0:T(4,128)} %bitcast.119), kind=kLoop, calls=%fused_computation.95 | loop fusion | bytes 4194304 | tf_op jit(solution)/shard_map/slice | solution.py:19
  68.3 7.9 %gather_fusion.2 = f32[1024,4,128]{2,1,0:T(4,128)} fusion(f32[768,4,128]{2,1,0:T(4,128)S(1)} %constant_dynamic-update-slice_fusion, s32[1024]{0:T(1024)S(1)} %get-tuple-element.34), kind=kCustom, calls=%fused_computation.2 | custom fusion | bytes 4198400 | tf_op jit(solution)/shard_map/gather | solution.py:109
  76.2 5.9 %fusion.29 = (f32[256,4,1,128]{3,2,1,0:T(1,128)S(1)}, f32[256,4,1,128]{3,2,1,0:T(1,128)S(1)}, f32[256,4,1,128]{3,2,1,0:T(1,128)S(1)}, f32[256,4,1,128]{3,2,1,0:T(1,128)S(1)}) fusion(f32[256,4,4,128]{3,2,1,0:T(4,128)} %bitcast.118), kind=kLoop, calls=%fused_computation.94 | loop fusion | bytes 4194304 | tf_op jit(solution)/shard_map/slice | solution.py:19
  82.1 35.8 %multiply_reduce_fusion = f32[256,128]{1,0:T(8,128)S(1)} fusion(f32[256,4,128]{2,1,0:T(4,128)S(1)} %bitcast.132, f32[256,128]{1,0:T(8,128)S(1)} %bitcast.142, f32[256,4,128]{2,1,0:T(4,128)S(1)} %bitcast.130, f32[256,128]{1,0:T(8,128)S(1)} %bitcast.143, f32[256,4,128]{2,1,0:T(4,128)S(1)} %bitcast.131, f32[256,128]{1,0:T(8,128)S(1)} %bitcast.144, ...), kind=kLoop, calls=%fused_computation.5 | loop fusion | flops 184516608 | bytes 2621440 | tf_op jit(solution)/shard_map/reduce_sum | solution.py:20
  118.0 35.6 %multiply_reduce_fusion.1 = f32[256,128]{1,0:T(8,128)S(1)} fusion(f32[256,4,128]{2,1,0:T(4,128)S(1)} %bitcast.136, f32[256,128]{1,0:T(8,128)S(1)} %bitcast.140, f32[256,4,128]{2,1,0:T(4,128)S(1)} %bitcast.134, f32[256,128]{1,0:T(8,128)S(1)} %bitcast.141, f32[256,4,128]{2,1,0:T(4,128)S(1)} %bitcast.135, f32[256,128]{1,0:T(8,128)S(1)} %bitcast.139, ...), kind=kLoop, calls=%fused_computation.6 | loop fusion | flops 184516608 | bytes 2621440 | tf_op jit(solution)/shard_map/reduce_sum | solution.py:20
  153.7 0.1 dynamic-slice_maximum_fusion
  153.8 0.2 slice_reduce_fusion.3
  154.1 0.1 slice_add_fusion.3
  154.1 0.1 pad_maximum_fusion.1
  154.2 1.1 fusion.3
  155.4 1.4 fusion.1
  156.8 0.6 broadcast_in_dim.61
  157.5 7.7 %all-to-all-start.2 = ((f32[16,2,16]{2,1,0:T(2,128)}), f32[16,2,16]{2,1,0:T(2,128)S(1)}, u32[]{:S(2)}, u32[]{:S(2)}) async-start(f32[16,2,16]{2,1,0:T(2,128)} %broadcast_in_dim.61), calls=%async_computation.2 | async-start | bytes 32768 | tf_op jit(solution)/shard_map/all_to_all | solution.py:102
  165.2 7.3 %all-to-all-done.2 = f32[16,2,16]{2,1,0:T(2,128)S(1)} async-done(((f32[16,2,16]{2,1,0:T(2,128)}), f32[16,2,16]{2,1,0:T(2,128)S(1)}, u32[]{:S(2)}, u32[]{:S(2)}) %all-to-all-start.2) | async-done | bytes 2080 | tf_op jit(solution)/shard_map/all_to_all | solution.py:102
  172.5 0.1 reshape.238
  172.6 0.2 all_to_all.27
  172.8 11.1 %all_to_all.34 = f32[16,1,4608]{2,1,0:T(1,128)S(1)} all-to-all(f32[16,1,4608]{2,1,0:T(1,128)S(1)} %all_to_all.27), channel_id=1, replica_groups=mesh['dom'=16,'grp'=16] {'grp'}, dimensions={0} | all-to-all | bytes 589824 | tf_op jit(solution)/shard_map/all_to_all | solution.py:114
  184.0 0.4 reshape.176
  184.4 0.3 copy.98
  184.6 0.2 reshape.177
  184.8 0.1 slice_bitcast_fusion.4
  184.9 0.1 slice_bitcast_fusion.5
  184.9 0.1 slice_bitcast_fusion.6
  185.1 0.7 gather_fusion.4
  185.8 0.7 bitcast_add_fusion
  186.5 0.1 fusion.23
  186.6 0.1 copy.107
  186.7 0.7 div.20
  (70 shorter events, 0.7 us)
Async XLA Ops:
  0.6 15.2 %copy-start = (s32[1,64]{1,0:T(1,128)S(1)}, s32[1,64]{1,0:T(1,128)}, u32[]{:S(2)}) copy-start(s32[1,64]{1,0:T(1,128)} %param.14) | copy-start | bytes 772
  6.4 9.3 %copy-start.13 = (s32[1,16,16]{2,1,0:T(8,128)S(1)}, s32[1,16,16]{2,1,0:T(8,128)}, u32[]{:S(2)}) copy-start(s32[1,16,16]{2,1,0:T(8,128)} %param.15) | copy-start | bytes 3076
  8.1 23.6 %all-to-all-start = ((f32[512,4,128]{2,1,0:T(4,128)}), f32[512,4,128]{2,1,0:T(4,128)S(1)}, u32[]{:S(2)}, u32[]{:S(2)}) async-start(f32[512,4,128]{2,1,0:T(4,128)} %copy.91), calls=%async_computation | async-start | bytes 2097152 | tf_op jit(solution)/shard_map/all_to_all | solution.py:61
  15.8 2.0 %copy-start.10 = (s32[256,128]{1,0:T(8,128)S(1)}, s32[256,128]{1,0:T(8,128)}, u32[]{:S(2)}) copy-start(s32[256,128]{1,0:T(8,128)} %param.13) | copy-start | bytes 393220
  15.8 2.1 %copy-start.1 = (f32[256,128]{1,0:T(8,128)S(1)}, f32[256,128]{1,0:T(8,128)}, u32[]{:S(2)}) copy-start(f32[256,128]{1,0:T(8,128)} %param.11) | copy-start | bytes 393220
  15.8 2.1 %copy-start.3 = (f32[256,3,128]{2,0,1:T(8,128)S(1)}, f32[256,3,128]{2,0,1:T(8,128)}, u32[]{:S(2)}) copy-start(f32[256,3,128]{2,0,1:T(8,128)} %param.10) | copy-start | bytes 1179652
  15.8 2.5 %copy-start.14 = (s32[512,4]{0,1:T(4,128)S(1)}, s32[512,4]{0,1:T(4,128)}, u32[]{:S(2)}) copy-start(s32[512,4]{0,1:T(4,128)} %param.17) | copy-start | bytes 24580
  17.7 2.9 %copy-start.16 = (s32[1,16]{1,0:T(1,128)S(1)}, s32[1,16]{1,0:T(1,128)}, u32[]{:S(2)}) copy-start(s32[1,16]{1,0:T(1,128)} %param.16) | copy-start | bytes 196
  17.9 14.8 %copy-start.11 = (s32[32768]{0:T(1024)}, s32[32768]{0:T(1024)S(1)}, u32[]{:S(2)}) copy-start(s32[32768]{0:T(1024)S(1)} %add_select_fusion) | copy-start | bytes 393220
  20.5 18.4 %copy-start.15 = (f32[4,16]{1,0:T(4,128)}, f32[4,16]{1,0:T(4,128)S(1)}, u32[]{:S(2)}) copy-start(f32[4,16]{1,0:T(4,128)S(1)} %fusion.2) | copy-start | bytes 772
  34.7 14.2 %all-to-all-start.1 = ((f32[16,1,8256]{2,1,0:T(1,128)}), f32[16,1,8256]{2,1,0:T(1,128)S(1)}, u32[]{:S(2)}, u32[]{:S(2)}) async-start(f32[16,1,8256]{2,1,0:T(1,128)} %copy.92), calls=%async_computation.1 | async-start | bytes 1064960 | tf_op jit(solution)/shard_map/all_to_all | solution.py:76
  49.1 104.6 %collective-permute-start.1 = (f32[16,4,16]{0,2,1:T(8,128)S(1)}, f32[16,4,16]{0,2,1:T(8,128)S(1)}, u32[]{:S(2)}, u32[]{:S(2)}) collective-permute-start(f32[16,4,16]{0,2,1:T(8,128)S(1)} %bitcast.146), channel_id=1, source_target_pairs={{0,240},{16,0},{32,16},{48,32},{64,48},{80,64},{96,80},{112,96},{1... | collective-permute-start | bytes 12296 | tf_op jit(solution)/shard_map/ppermute | solution.py:81
  51.7 102.0 %collective-permute-start = (f32[16,4,16]{0,2,1:T(8,128)S(1)}, f32[16,4,16]{0,2,1:T(8,128)S(1)}, u32[]{:S(2)}, u32[]{:S(2)}) collective-permute-start(f32[16,4,16]{0,2,1:T(8,128)S(1)} %bitcast.147), channel_id=1, source_target_pairs={{0,16},{16,32},{32,48},{48,64},{64,80},{80,96},{96,112},{112,128},... | collective-permute-start | bytes 12296 | tf_op jit(solution)/shard_map/ppermute | solution.py:80
  76.2 5.9 %copy-start.2 = (f32[256,4,1,128]{3,2,1,0:T(1,128)S(1)}, f32[256,4,1,128]{3,2,1,0:T(1,128)}, u32[]{:S(2)}) copy-start(f32[256,4,1,128]{3,2,1,0:T(1,128)} %get-tuple-element.18) | copy-start | bytes 1572868
  76.2 5.9 %copy-start.7 = (f32[256,1,128]{2,1,0:T(1,128)S(1)}, f32[256,1,128]{2,1,0:T(1,128)}, u32[]{:S(2)}) copy-start(f32[256,1,128]{2,1,0:T(1,128)} %get-tuple-element.20) | copy-start | bytes 393220
  76.2 5.9 %copy-start.8 = (f32[256,1,128]{2,1,0:T(1,128)S(1)}, f32[256,1,128]{2,1,0:T(1,128)}, u32[]{:S(2)}) copy-start(f32[256,1,128]{2,1,0:T(1,128)} %get-tuple-element.21) | copy-start | bytes 393220
  76.2 5.9 %copy-start.9 = (f32[256,1,128]{2,1,0:T(1,128)S(1)}, f32[256,1,128]{2,1,0:T(1,128)}, u32[]{:S(2)}) copy-start(f32[256,1,128]{2,1,0:T(1,128)} %get-tuple-element.22) | copy-start | bytes 393220
  82.1 35.8 %copy-start.5 = (f32[256,1,128]{2,1,0:T(1,128)S(1)}, f32[256,1,128]{2,1,0:T(1,128)}, u32[]{:S(2)}) copy-start(f32[256,1,128]{2,1,0:T(1,128)} %get-tuple-element.23) | copy-start | bytes 393220
  82.1 35.8 %copy-start.6 = (f32[256,1,128]{2,1,0:T(1,128)S(1)}, f32[256,1,128]{2,1,0:T(1,128)}, u32[]{:S(2)}) copy-start(f32[256,1,128]{2,1,0:T(1,128)} %get-tuple-element.24) | copy-start | bytes 393220
  118.0 36.2 %copy-start.4 = (f32[256,3,128]{2,0,1:T(8,128)S(1)}, f32[256,3,128]{2,0,1:T(8,128)}, u32[]{:S(2)}) copy-start(f32[256,3,128]{2,0,1:T(8,128)} %param.10) | copy-start | bytes 1179652
  118.0 36.2 %copy-start.12 = (s32[32768]{0:T(1024)S(1)}, s32[32768]{0:T(1024)}, u32[]{:S(2)}) copy-start(s32[32768]{0:T(1024)} %copy-done.11) | copy-start | bytes 393220
  153.6 3.2 %slice-start = ((f32[4,16]{1,0:T(4,128)}), f32[1,16]{1,0:T(1,128)S(1)}, s32[]{:S(2)}) async-start(f32[4,16]{1,0:T(4,128)} %copy-done.15), calls=%async_computation.4 | async-start | bytes 1024 | tf_op jit(solution)/shard_map/slice | solution.py:100
  157.5 15.0 %all-to-all-start.2 = ((f32[16,2,16]{2,1,0:T(2,128)}), f32[16,2,16]{2,1,0:T(2,128)S(1)}, u32[]{:S(2)}, u32[]{:S(2)}) async-start(f32[16,2,16]{2,1,0:T(2,128)} %broadcast_in_dim.61), calls=%async_computation.2 | async-start | bytes 32768 | tf_op jit(solution)/shard_map/all_to_all | solution.py:102

commit v8 on v7

--- a/solution.py
+++ b/solution.py
@@ -58,7 +58,16 @@
     outgoing = jnp.dot(
         placing, payload.reshape(leaves, -1), precision=exact, preferred_element_type=jnp.float32
     ).reshape(slot_count, 4, leaf_width)
-    owned = lax.all_to_all(outgoing, "grp", split_axis=0, concat_axis=0, tiled=True)
+    quarters = GSPAN // GROUP_DEV
+    first_sums = local_sums(jnp.concatenate([mass_flat[None, :], mass_flat[None, :] * speeds], axis=0))
+    table_size = capacity * 4 * leaf_width
+    packed = jnp.concatenate(
+        [outgoing.reshape(owners, table_size), jnp.broadcast_to(first_sums.reshape(1, -1), (owners, first_sums.size))],
+        axis=1,
+    )
+    packed = lax.all_to_all(packed, "grp", split_axis=0, concat_axis=0, tiled=True)
+    owned = packed[:, :table_size].reshape(slot_count, 4, leaf_width)
+    row_sums = packed[:, table_size:].reshape((owners,) + first_sums.shape)
 
     per_peer = send_list.shape[2]
     pick = boundary_set[0].at[send_list[0]].get(mode="promise_in_bounds")
@@ -66,16 +75,8 @@
     sending = owned.at[pick].get(mode="promise_in_bounds")
     sending = jnp.where(live[:, :, None, None], sending, jnp.zeros_like(sending))
     blocks = lax.axis_size("dom") * owners
-    quarters = GSPAN // GROUP_DEV
-    first_sums = local_sums(jnp.concatenate([mass_flat[None, :], mass_flat[None, :] * speeds], axis=0))
-    leaf_size = per_peer * 4 * leaf_width
-    packed = jnp.concatenate(
-        [sending.reshape(owners, leaf_size), jnp.broadcast_to(first_sums.reshape(1, -1), (owners, first_sums.size))],
-        axis=1,
-    )
-    packed = lax.all_to_all(packed, "grp", split_axis=0, concat_axis=0, tiled=True)
-    remote = packed[:, :leaf_size].reshape(owners * per_peer, 4, leaf_width)
-    row_sums = packed[:, leaf_size:].reshape((owners,) + first_sums.shape)
+    remote = lax.all_to_all(sending, "grp", split_axis=0, concat_axis=0, tiled=True)
+    remote = remote.reshape(owners * per_peer, 4, leaf_width)
     domains = lax.axis_size("dom")
     before = lax.ppermute(row_sums, "dom", [(i, (i + 1) % domains) for i in range(domains)])
     after = lax.ppermute(row_sums, "dom", [(i, (i - 1) % domains) for i in range(domains)])
@@ -83,7 +84,6 @@
     span = 2 * quarters - 1
     window = lax.dynamic_slice_in_dim(three_rows, owners + lax.axis_index("grp") - (quarters - 1), span, axis=0)
     near_sums = {step: window[step + quarters - 1] for step in range(-quarters + 1, quarters)}
-    combined = jnp.concatenate([owned, remote], axis=0)
 
     near_parts = []
     for ahead in range(quarters):
@@ -98,6 +98,8 @@
     kinetic = 0.5 * jnp.sum(relative * relative, axis=0)
     heat_local = local_sums((mass_flat * kinetic)[None, :])[0]
     partial = jnp.stack([heat_local, first_sums[0]])
+    partial, remote = lax.optimization_barrier((partial, remote))
+    combined = jnp.concatenate([owned, remote], axis=0)
     down = jnp.broadcast_to(partial[None], (domains,) + partial.shape)
     down = lax.all_to_all(down, "dom", split_axis=0, concat_axis=0, tiled=True)
 

time: 188 us -> 185 us (0.984)
  waiting for transfers between devices: 26.8 us -> 19.1 us
  starting transfers between devices: 23.6 us -> 26.3 us
    all_to_all x1, waiting for transfers between devices: 7.25 us -> 0.01 us  [layer(): down = lax.all_to_all(down, 'dom', split_axis=0, concat_axis=0, tiled=True)]
    all_to_all x1, waiting for transfers between devices: 11 us -> 5.84 us  [layer(): lax.all_to_all(sending, 'grp', split_axis=0, concat_axis=0, tiled=True)]
    all_to_all x1, waiting for transfers between devices: 8.5 us -> 13.3 us  [layer(): lax.all_to_all(packed, 'grp', split_axis=0, concat_axis=0, tiled=True)]
    all_to_all x1, starting transfers between devices: 7.57 us -> 3.58 us  [layer(): lax.all_to_all(sending, 'grp', split_axis=0, concat_axis=0, tiled=True)]
    all_to_all x1, starting transfers between devices: 4.21 us -> 7.57 us  [layer(): lax.all_to_all(packed, 'grp', split_axis=0, concat_axis=0, tiled=True)]
    all_to_all x1, starting transfers between devices: 7.68 us -> 11 us  [layer(): down = lax.all_to_all(down, 'dom', split_axis=0, concat_axis=0, tiled=True)]
  transfers between devices with their start and end apart: 5 -> 5, of which waited for: 3 -> 2; matrix products, arithmetic and copies ran while one was open for 57% -> 60% of each run, Pallas kernels for 0% -> 0%
where the time goes in v8:
time: 185 us
  other arithmetic  76.8 us (42%)
  local copies, waits for them, and re-layouts  44.7 us (24%)
  starting transfers between devices  26.3 us (14%)
  waiting for transfers between devices  19.1 us (10%)
  blocking collectives  11.6 us (6%)
  matrix products  4.82 us (3%)
    reduce_sum x2, other arithmetic, tile_potential(): return -jnp.sum(weights, axis=(1, 3))  71.2 us
    gather x2, local copies, waits for them, and re-layouts, layer(): sources = combined.at[rows].get(mode='promise_in_bounds')  15.9 us
    all_to_all x1, waiting for transfers between devices, layer(): lax.all_to_all(packed, 'grp', split_axis=0, concat_axis=0, tiled=True)  13.3 us
    slice x2, local copies, waits for them, and re-layouts, tile_potential(): weights = sources[:, :, 3, None, :] * lax.rsqrt(distance)  11.7 us
    all_to_all x1, blocking collectives, layer(): lax.all_to_all(jnp.concatenate([flat, extra], axis=1), 'grp', split_axis=...  11.6 us
    all_to_all x1, starting transfers between devices, layer(): down = lax.all_to_all(down, 'dom', split_axis=0, concat_axis=0, tiled=True)  11 us
    all_to_all x1, starting transfers between devices, layer(): lax.all_to_all(packed, 'grp', split_axis=0, concat_axis=0, tiled=True)  7.57 us
    all_to_all x1, waiting for transfers between devices, layer(): lax.all_to_all(sending, 'grp', split_axis=0, concat_axis=0, tiled=True)  5.84 us
  transfers between devices with their start and end apart: 5, of which 2 were waited for; matrix products, arithmetic and copies ran while one was open for 60% of the time, Pallas kernels for 0%

profile of v8, /device:TPU:1, one launch (start us, length us, event | category | flops | bytes accessed | tf_op | source)
XLA Modules:
  0.0 184.5 jit_solution(120814304202953381)
XLA Ops:
  0.6 0.7 fusion.16
  1.3 0.6 reduce-window.6
  1.9 0.2 slice_reduce_fusion.7
  2.1 0.8 fusion.15
  2.9 0.7 compare_select_fusion.4
  3.6 1.0 copy.77
  4.6 1.2 copy.78
  5.8 0.6 fusion.10
  6.5 0.2 reshape_reshape.3
  6.8 0.2 copy-done.3
  6.9 0.3 bitcast_multiply_fusion
  7.3 1.6 fusion.2
  8.9 0.1 reshape.235
  9.0 0.1 pad_maximum_fusion
  9.1 1.7 all_to_all.22
  10.8 7.6 %all-to-all-start = ((f32[16,1,16448]{2,1,0:T(1,128)}), f32[16,1,16448]{2,1,0:T(1,128)S(1)}, u32[]{:S(2)}, u32[]{:S(2)}) async-start(f32[16,1,16448]{2,1,0:T(1,128)} %all_to_all.22), calls=%async_computation | async-start | bytes 2113536 | tf_op jit(solution)/shard_map/all_to_all | solution.py:68
  18.5 0.1 reshape.179
  18.6 1.9 %gather_fusion = s32[256]{0:T(256)S(1)} fusion(s32[64]{0:T(128)S(1)} %bitcast.124, s32[1024]{0:T(1024)S(1)} %pad_clamp_fusion.2), kind=kCustom, calls=%fused_computation | custom fusion | bytes 3072 | tf_op jit(solution)/shard_map/gather | solution.py:73
  20.4 0.1 gather.18
  20.5 0.1 reshape.187
  20.6 0.1 copy.82
  20.8 0.1 reshape.195
  20.9 0.1 copy.87
  21.0 0.1 reshape.203
  21.3 13.3 %all-to-all-done = f32[16,1,16448]{2,1,0:T(1,128)S(1)} async-done(((f32[16,1,16448]{2,1,0:T(1,128)}), f32[16,1,16448]{2,1,0:T(1,128)S(1)}, u32[]{:S(2)}, u32[]{:S(2)}) %all-to-all-start) | async-done | bytes 1052704 | tf_op jit(solution)/shard_map/all_to_all | solution.py:68
  34.6 0.1 copy.104
  34.7 2.6 %collective-permute-start.1 = (f32[16,4,16]{0,2,1:T(8,128)S(1)}, f32[16,4,16]{0,2,1:T(8,128)S(1)}, u32[]{:S(2)}, u32[]{:S(2)}) collective-permute-start(f32[16,4,16]{0,2,1:T(8,128)S(1)} %bitcast.150), channel_id=1, source_target_pairs={{0,240},{16,0},{32,16},{48,32},{64,48},{80,64},{96,80},{112,96},{1... | collective-permute-start | bytes 12296 | tf_op jit(solution)/shard_map/ppermute | solution.py:82
  37.3 1.5 collective-permute-start
  38.9 0.9 fusion.26
  39.8 0.7 reshape.172
  40.5 0.3 copy-done.1
  40.8 0.4 slice.251
  41.2 1.0 fusion.27
  42.2 0.4 slice.261
  42.6 1.0 fusion.28
  43.6 1.0 gather_fusion.1
  44.6 1.1 broadcast_select_fusion
  45.8 3.6 %all-to-all-start.1 = ((f32[16,16,4,128]{3,2,1,0:T(4,128)}), f32[16,16,4,128]{3,2,1,0:T(4,128)S(1)}, u32[]{:S(2)}, u32[]{:S(2)}) async-start(f32[16,16,4,128]{3,2,1,0:T(4,128)} %broadcast_select_fusion), calls=%async_computation.1 | async-start | bytes 1048576 | tf_op jit(solution)/shard_map/all_to_all | solution.py:78
  49.4 0.1 dynamic-slice_maximum_fusion
  49.5 0.2 slice_reduce_fusion.3
  49.8 0.1 slice_add_fusion.3
  49.8 0.1 pad_maximum_fusion.3
  49.9 1.2 fusion.3
  51.1 1.4 fusion.1
  52.5 5.8 %all-to-all-done.1 = f32[16,16,4,128]{3,2,1,0:T(4,128)S(1)} async-done(((f32[16,16,4,128]{3,2,1,0:T(4,128)}), f32[16,16,4,128]{3,2,1,0:T(4,128)S(1)}, u32[]{:S(2)}, u32[]{:S(2)}) %all-to-all-start.1) | async-done | bytes 524320 | tf_op jit(solution)/shard_map/all_to_all | solution.py:78
  58.4 0.6 broadcast_in_dim.61
  59.0 11.0 %all-to-all-start.2 = ((f32[16,2,16]{2,1,0:T(2,128)}), f32[16,2,16]{2,1,0:T(2,128)S(1)}, u32[]{:S(2)}, u32[]{:S(2)}) async-start(f32[16,2,16]{2,1,0:T(2,128)} %broadcast_in_dim.61), calls=%async_computation.2 | async-start | bytes 32768 | tf_op jit(solution)/shard_map/all_to_all | solution.py:104
  70.1 7.9 %gather_fusion.3 = f32[1024,4,128]{2,1,0:T(4,128)} fusion(f32[768,4,128]{2,1,0:T(4,128)S(1)} %constant_dynamic-update-slice_fusion, s32[1024]{0:T(1024)S(1)} %get-tuple-element.39), kind=kCustom, calls=%fused_computation.3 | custom fusion | bytes 4198400 | tf_op jit(solution)/shard_map/gather | solution.py:111
  78.0 5.9 %fusion.25 = (f32[256,4,1,128]{3,2,1,0:T(1,128)S(1)}, f32[256,4,1,128]{3,2,1,0:T(1,128)S(1)}, f32[256,4,1,128]{3,2,1,0:T(1,128)S(1)}, f32[256,4,1,128]{3,2,1,0:T(1,128)S(1)}) fusion(f32[256,4,4,128]{3,2,1,0:T(4,128)} %bitcast.129), kind=kLoop, calls=%fused_computation.91 | loop fusion | bytes 4194304 | tf_op jit(solution)/shard_map/slice | solution.py:19
  83.9 35.6 %multiply_reduce_fusion = f32[256,128]{1,0:T(8,128)S(1)} fusion(f32[256,4,128]{2,1,0:T(4,128)S(1)} %bitcast.142, f32[256,128]{1,0:T(8,128)S(1)} %bitcast.157, f32[256,4,128]{2,1,0:T(4,128)S(1)} %bitcast.140, f32[256,128]{1,0:T(8,128)S(1)} %bitcast.158, f32[256,4,128]{2,1,0:T(4,128)S(1)} %bitcast.141, f32[256,128]{1,0:T(8,128)S(1)} %bitcast.156, ...), kind=kLoop, calls=%fused_computation.5 | loop fusion | flops 184516608 | bytes 2621440 | tf_op jit(solution)/shard_map/reduce_sum | solution.py:20
  119.5 7.9 %gather_fusion.2 = f32[1024,4,128]{2,1,0:T(4,128)} fusion(f32[768,4,128]{2,1,0:T(4,128)S(1)} %constant_dynamic-update-slice_fusion, s32[1024]{0:T(1024)S(1)} %get-tuple-element.40), kind=kCustom, calls=%fused_computation.2 | custom fusion | bytes 4198400 | tf_op jit(solution)/shard_map/gather | solution.py:111
  127.5 5.9 %fusion.24 = (f32[256,4,1,128]{3,2,1,0:T(1,128)S(1)}, f32[256,4,1,128]{3,2,1,0:T(1,128)S(1)}, f32[256,4,1,128]{3,2,1,0:T(1,128)S(1)}, f32[256,4,1,128]{3,2,1,0:T(1,128)S(1)}) fusion(f32[256,4,4,128]{3,2,1,0:T(4,128)} %bitcast.128), kind=kLoop, calls=%fused_computation.90 | loop fusion | bytes 4194304 | tf_op jit(solution)/shard_map/slice | solution.py:19
  133.4 35.6 %multiply_reduce_fusion.1 = f32[256,128]{1,0:T(8,128)S(1)} fusion(f32[256,4,128]{2,1,0:T(4,128)S(1)} %bitcast.146, f32[256,128]{1,0:T(8,128)S(1)} %bitcast.154, f32[256,4,128]{2,1,0:T(4,128)S(1)} %bitcast.144, f32[256,128]{1,0:T(8,128)S(1)} %bitcast.155, f32[256,4,128]{2,1,0:T(4,128)S(1)} %bitcast.145, f32[256,128]{1,0:T(8,128)S(1)} %bitcast.153, ...), kind=kLoop, calls=%fused_computation.6 | loop fusion | flops 184516608 | bytes 2621440 | tf_op jit(solution)/shard_map/reduce_sum | solution.py:20
  169.1 0.1 reshape.236
  169.2 0.2 all_to_all.27
  169.4 11.6 %all_to_all.34 = f32[16,1,4608]{2,1,0:T(1,128)S(1)} all-to-all(f32[16,1,4608]{2,1,0:T(1,128)S(1)} %all_to_all.27), channel_id=1, replica_groups=mesh['dom'=16,'grp'=16] {'grp'}, dimensions={0} | all-to-all | bytes 589824 | tf_op jit(solution)/shard_map/all_to_all | solution.py:116
  181.1 0.4 reshape.175
  181.5 0.3 copy.92
  181.7 0.2 reshape.176
  182.2 0.7 gather_fusion.4
  182.9 0.7 bitcast_add_fusion
  183.6 0.1 fusion.19
  183.7 0.1 copy.101
  183.8 0.7 div.20
  (70 shorter events, 1.1 us)
Async XLA Ops:
  0.6 17.9 %copy-start = (s32[1,64]{1,0:T(1,128)S(1)}, s32[1,64]{1,0:T(1,128)}, u32[]{:S(2)}) copy-start(s32[1,64]{1,0:T(1,128)} %param.14) | copy-start | bytes 772
  5.8 0.9 copy-start.5
  5.8 1.0 copy-start.2
  5.8 1.1 copy-start.3
  8.9 9.5 %copy-start.13 = (f32[4,16]{1,0:T(4,128)}, f32[4,16]{1,0:T(4,128)S(1)}, u32[]{:S(2)}) copy-start(f32[4,16]{1,0:T(4,128)S(1)} %fusion.2) | copy-start | bytes 772
  9.1 9.3 %copy-start.11 = (s32[1,16,16]{2,1,0:T(8,128)S(1)}, s32[1,16,16]{2,1,0:T(8,128)}, u32[]{:S(2)}) copy-start(s32[1,16,16]{2,1,0:T(8,128)} %param.15) | copy-start | bytes 3076
  10.8 23.7 %all-to-all-start = ((f32[16,1,16448]{2,1,0:T(1,128)}), f32[16,1,16448]{2,1,0:T(1,128)S(1)}, u32[]{:S(2)}, u32[]{:S(2)}) async-start(f32[16,1,16448]{2,1,0:T(1,128)} %all_to_all.22), calls=%async_computation | async-start | bytes 2113536 | tf_op jit(solution)/shard_map/all_to_all | solution.py:68
  18.6 2.1 %copy-start.12 = (s32[512,4]{0,1:T(4,128)S(1)}, s32[512,4]{0,1:T(4,128)}, u32[]{:S(2)}) copy-start(s32[512,4]{0,1:T(4,128)} %param.17) | copy-start | bytes 24580
  18.6 2.6 %copy-start.14 = (s32[1,16]{1,0:T(1,128)S(1)}, s32[1,16]{1,0:T(1,128)}, u32[]{:S(2)}) copy-start(s32[1,16]{1,0:T(1,128)} %param.16) | copy-start | bytes 196
  34.7 14.7 %collective-permute-start.1 = (f32[16,4,16]{0,2,1:T(8,128)S(1)}, f32[16,4,16]{0,2,1:T(8,128)S(1)}, u32[]{:S(2)}, u32[]{:S(2)}) collective-permute-start(f32[16,4,16]{0,2,1:T(8,128)S(1)} %bitcast.150), channel_id=1, source_target_pairs={{0,240},{16,0},{32,16},{48,32},{64,48},{80,64},{96,80},{112,96},{1... | collective-permute-start | bytes 12296 | tf_op jit(solution)/shard_map/ppermute | solution.py:82
  37.3 12.1 %collective-permute-start = (f32[16,4,16]{0,2,1:T(8,128)S(1)}, f32[16,4,16]{0,2,1:T(8,128)S(1)}, u32[]{:S(2)}, u32[]{:S(2)}) collective-permute-start(f32[16,4,16]{0,2,1:T(8,128)S(1)} %bitcast.151), channel_id=1, source_target_pairs={{0,16},{16,32},{32,48},{48,64},{64,80},{80,96},{96,112},{112,128},... | collective-permute-start | bytes 12296 | tf_op jit(solution)/shard_map/ppermute | solution.py:81
  39.8 1.0 copy-start.1
  44.6 5.4 %copy-start.4 = (f32[256,3,128]{2,0,1:T(8,128)S(1)}, f32[256,3,128]{2,0,1:T(8,128)}, u32[]{:S(2)}) copy-start(f32[256,3,128]{2,0,1:T(8,128)} %param.10) | copy-start | bytes 1179652
  45.8 6.7 %slice-start = ((f32[4,16]{1,0:T(4,128)}), f32[1,16]{1,0:T(1,128)S(1)}, s32[]{:S(2)}) async-start(f32[4,16]{1,0:T(4,128)} %copy-done.13), calls=%async_computation.4 | async-start | bytes 1024 | tf_op jit(solution)/shard_map/slice | solution.py:100
  45.8 12.6 %all-to-all-start.1 = ((f32[16,16,4,128]{3,2,1,0:T(4,128)}), f32[16,16,4,128]{3,2,1,0:T(4,128)S(1)}, u32[]{:S(2)}, u32[]{:S(2)}) async-start(f32[16,16,4,128]{3,2,1,0:T(4,128)} %broadcast_select_fusion), calls=%async_computation.1 | async-start | bytes 1048576 | tf_op jit(solution)/shard_map/all_to_all | solution.py:78
  59.0 110.1 %all-to-all-start.2 = ((f32[16,2,16]{2,1,0:T(2,128)}), f32[16,2,16]{2,1,0:T(2,128)S(1)}, u32[]{:S(2)}, u32[]{:S(2)}) async-start(f32[16,2,16]{2,1,0:T(2,128)} %broadcast_in_dim.61), calls=%async_computation.2 | async-start | bytes 32768 | tf_op jit(solution)/shard_map/all_to_all | solution.py:104
  78.0 5.9 %copy-start.9 = (f32[256,1,128]{2,1,0:T(1,128)S(1)}, f32[256,1,128]{2,1,0:T(1,128)}, u32[]{:S(2)}) copy-start(f32[256,1,128]{2,1,0:T(1,128)} %get-tuple-element.29) | copy-start | bytes 393220
  78.0 5.9 %copy-start.10 = (f32[256,1,128]{2,1,0:T(1,128)S(1)}, f32[256,1,128]{2,1,0:T(1,128)}, u32[]{:S(2)}) copy-start(f32[256,1,128]{2,1,0:T(1,128)} %get-tuple-element.30) | copy-start | bytes 393220
  127.5 5.9 %copy-start.6 = (f32[256,1,128]{2,1,0:T(1,128)S(1)}, f32[256,1,128]{2,1,0:T(1,128)}, u32[]{:S(2)}) copy-start(f32[256,1,128]{2,1,0:T(1,128)} %get-tuple-element.25) | copy-start | bytes 393220
  127.5 5.9 %copy-start.7 = (f32[256,1,128]{2,1,0:T(1,128)S(1)}, f32[256,1,128]{2,1,0:T(1,128)}, u32[]{:S(2)}) copy-start(f32[256,1,128]{2,1,0:T(1,128)} %get-tuple-element.26) | copy-start | bytes 393220
  127.5 5.9 %copy-start.8 = (f32[256,1,128]{2,1,0:T(1,128)S(1)}, f32[256,1,128]{2,1,0:T(1,128)}, u32[]{:S(2)}) copy-start(f32[256,1,128]{2,1,0:T(1,128)} %get-tuple-element.27) | copy-start | bytes 393220

commit v9 on v7

--- a/solution.py
+++ b/solution.py
@@ -54,10 +54,8 @@
     leaf_rank = jnp.sum((jnp.cumsum(onehot, axis=0) - onehot) * onehot, axis=1)
     target = destination * capacity + leaf_rank
     payload = jnp.concatenate([positions, masses[:, None, :]], axis=1)
-    placing = (jnp.arange(slot_count, dtype=jnp.int32)[:, None] == target[None, :]).astype(jnp.float32)
-    outgoing = jnp.dot(
-        placing, payload.reshape(leaves, -1), precision=exact, preferred_element_type=jnp.float32
-    ).reshape(slot_count, 4, leaf_width)
+    holder = jnp.full((slot_count,), leaves, jnp.int32).at[target].set(jnp.arange(leaves, dtype=jnp.int32))
+    outgoing = payload.at[holder].get(mode="fill", fill_value=0.0)
     owned = lax.all_to_all(outgoing, "grp", split_axis=0, concat_axis=0, tiled=True)
 
     per_peer = send_list.shape[2]

time: 188 us -> 192 us (1.021)
  other arithmetic: 76.2 us -> 80 us
    select_n x1 -> x3, other arithmetic: 0.68 us -> 3.33 us  [the longest x2 2.64 us: layer(): outgoing = payload.at[holder].get(mode='fill', fill_value=0.0)]
    gather x0 -> x1, local copies, waits for them, and re-layouts: none -> 2.07 us  [layer(): outgoing = payload.at[holder].get(mode='fill', fill_value=0.0)]
  transfers between devices with their start and end apart: 5 -> 5, of which waited for: 3 -> 3; matrix products, arithmetic and copies ran while one was open for 57% -> 56% of each run, Pallas kernels for 0% -> 0%
where the time goes in v9:
time: 192 us
  other arithmetic  80 us (42%)
  local copies, waits for them, and re-layouts  44.6 us (23%)
  waiting for transfers between devices  26.8 us (14%)
  starting transfers between devices  23.6 us (12%)
  blocking collectives  11.1 us (6%)
  matrix products  4.14 us (2%)
    reduce_sum x2, other arithmetic, tile_potential(): return -jnp.sum(weights, axis=(1, 3))  71.4 us
    gather x2, local copies, waits for them, and re-layouts, layer(): sources = combined.at[rows].get(mode='promise_in_bounds')  15.9 us
    slice x2, local copies, waits for them, and re-layouts, tile_potential(): weights = sources[:, :, 3, None, :] * lax.rsqrt(distance)  12.5 us
    all_to_all x1, blocking collectives, layer(): lax.all_to_all(jnp.concatenate([flat, extra], axis=1), 'grp', split_axis=...  11.1 us
    all_to_all x1, waiting for transfers between devices, layer(): lax.all_to_all(outgoing, 'grp', split_axis=0, concat_axis=0, tiled=True)  11 us
    all_to_all x1, waiting for transfers between devices, layer(): lax.all_to_all(packed, 'grp', split_axis=0, concat_axis=0, tiled=True)  8.51 us
    all_to_all x1, starting transfers between devices, layer(): down = lax.all_to_all(down, 'dom', split_axis=0, concat_axis=0, tiled=True)  7.7 us
    all_to_all x1, starting transfers between devices, layer(): lax.all_to_all(outgoing, 'grp', split_axis=0, concat_axis=0, tiled=True)  7.57 us
  transfers between devices with their start and end apart: 5, of which 3 were waited for; matrix products, arithmetic and copies ran while one was open for 56% of the time, Pallas kernels for 0%

profile of v9, /device:TPU:1, one launch (start us, length us, event | category | flops | bytes accessed | tf_op | source)
XLA Modules:
  0.0 191.6 jit_solution(16888227353798434536)
XLA Ops:
  0.6 0.7 fusion.14
  1.3 0.6 reduce-window.6
  1.9 0.2 slice_reduce_fusion.7
  2.1 0.8 fusion.13
  2.9 0.7 compare_select_fusion.5
  3.6 1.4 scatter_custom_fusion
  5.0 1.3 copy.75
  6.3 1.1 pad_maximum_fusion
  7.5 2.1 %gather_fusion = f32[512,4,128]{2,1,0:T(4,128)S(1)} fusion(f32[256,4,128]{2,1,0:T(4,128)S(1)} %pad_maximum_fusion, s32[1024]{0:T(1024)S(1)} %pad_clamp_fusion.3), kind=kCustom, calls=%fused_computation | custom fusion | bytes 2099200 | tf_op jit(solution)/shard_map/gather | solution.py:58
  9.6 2.6 %broadcast_select_fusion = f32[512,4,128]{2,1,0:T(4,128)} fusion(f32[512,4,128]{2,1,0:T(4,128)S(1)} %gather_fusion, pred[512]{0:T(512)(128)(4,1)S(1)} %compare_and_fusion), kind=kLoop, calls=%fused_computation.25 | loop fusion | flops 262144 | bytes 2097664 | tf_op jit(solution)/shard_map/select_n | solution.py:58
  12.2 7.6 %all-to-all-start = ((f32[512,4,128]{2,1,0:T(4,128)}), f32[512,4,128]{2,1,0:T(4,128)S(1)}, u32[]{:S(2)}, u32[]{:S(2)}) async-start(f32[512,4,128]{2,1,0:T(4,128)} %broadcast_select_fusion), calls=%async_computation | async-start | bytes 2097152 | tf_op jit(solution)/shard_map/all_to_all | solution.py:59
  19.8 0.1 reshape.186
  19.9 1.9 gather_fusion.1
  21.8 0.1 gather.22
  22.0 0.3 bitcast_multiply_fusion
  22.4 0.1 reshape.194
  22.5 0.1 copy.80
  22.6 0.1 reshape.202
  22.7 0.1 copy.81
  22.9 0.1 reshape.210
  23.0 1.6 fusion.2
  24.6 0.1 reshape.252
  24.7 0.1 iota_compare_fusion.8
  24.8 11.0 %all-to-all-done = f32[512,4,128]{2,1,0:T(4,128)S(1)} async-done(((f32[512,4,128]{2,1,0:T(4,128)}), f32[512,4,128]{2,1,0:T(4,128)S(1)}, u32[]{:S(2)}, u32[]{:S(2)}) %all-to-all-start) | async-done | bytes 1048608 | tf_op jit(solution)/shard_map/all_to_all | solution.py:59
  35.8 1.0 gather_fusion.2
  36.8 0.3 broadcast_select_fusion.1
  37.2 0.2 select_n.64
  37.5 1.3 copy.76
  38.8 4.2 %all-to-all-start.1 = ((f32[16,1,8256]{2,1,0:T(1,128)}), f32[16,1,8256]{2,1,0:T(1,128)S(1)}, u32[]{:S(2)}, u32[]{:S(2)}) async-start(f32[16,1,8256]{2,1,0:T(1,128)} %copy.76), calls=%async_computation.1 | async-start | bytes 1064960 | tf_op jit(solution)/shard_map/all_to_all | solution.py:74
  43.1 1.4 fusion.26
  44.5 8.5 %all-to-all-done.1 = f32[16,1,8256]{2,1,0:T(1,128)S(1)} async-done(((f32[16,1,8256]{2,1,0:T(1,128)}), f32[16,1,8256]{2,1,0:T(1,128)S(1)}, u32[]{:S(2)}, u32[]{:S(2)}) %all-to-all-start.1) | async-done | bytes 528416 | tf_op jit(solution)/shard_map/all_to_all | solution.py:74
  53.1 0.1 copy.94
  53.2 2.6 %collective-permute-start.1 = (f32[16,4,16]{0,2,1:T(8,128)S(1)}, f32[16,4,16]{0,2,1:T(8,128)S(1)}, u32[]{:S(2)}, u32[]{:S(2)}) collective-permute-start(f32[16,4,16]{0,2,1:T(8,128)S(1)} %bitcast.137), channel_id=1, source_target_pairs={{0,240},{16,0},{32,16},{48,32},{64,48},{80,64},{96,80},{112,96},{1... | collective-permute-start | bytes 12296 | tf_op jit(solution)/shard_map/ppermute | solution.py:79
  55.8 1.5 collective-permute-start
  57.3 0.3 reshape.172
  57.8 7.9 %gather_fusion.4 = f32[1024,4,128]{2,1,0:T(4,128)} fusion(f32[768,4,128]{2,1,0:T(4,128)S(1)} %constant_dynamic-update-slice_fusion, s32[1024]{0:T(1024)S(1)} %get-tuple-element.31), kind=kCustom, calls=%fused_computation.4 | custom fusion | bytes 4198400 | tf_op jit(solution)/shard_map/gather | solution.py:107
  65.7 6.6 %fusion.25 = (f32[256,4,1,128]{3,2,1,0:T(1,128)S(1)}, f32[256,4,1,128]{3,2,1,0:T(1,128)S(1)}, f32[256,4,1,128]{3,2,1,0:T(1,128)S(1)}, f32[256,4,1,128]{3,2,1,0:T(1,128)}) fusion(f32[256,4,4,128]{3,2,1,0:T(4,128)} %bitcast.110), kind=kLoop, calls=%fused_computation.95 | loop fusion | bytes 4194304 | tf_op jit(solution)/shard_map/slice | solution.py:19
  72.4 7.9 %gather_fusion.3 = f32[1024,4,128]{2,1,0:T(4,128)} fusion(f32[768,4,128]{2,1,0:T(4,128)S(1)} %constant_dynamic-update-slice_fusion, s32[1024]{0:T(1024)S(1)} %get-tuple-element.32), kind=kCustom, calls=%fused_computation.3 | custom fusion | bytes 4198400 | tf_op jit(solution)/shard_map/gather | solution.py:107
  80.3 5.9 %fusion.24 = (f32[256,4,1,128]{3,2,1,0:T(1,128)S(1)}, f32[256,4,1,128]{3,2,1,0:T(1,128)S(1)}, f32[256,4,1,128]{3,2,1,0:T(1,128)S(1)}, f32[256,4,1,128]{3,2,1,0:T(1,128)S(1)}) fusion(f32[256,4,4,128]{3,2,1,0:T(4,128)} %bitcast.109), kind=kLoop, calls=%fused_computation.94 | loop fusion | bytes 4194304 | tf_op jit(solution)/shard_map/slice | solution.py:19
  86.2 35.8 %multiply_reduce_fusion = f32[256,128]{1,0:T(8,128)S(1)} fusion(f32[256,4,128]{2,1,0:T(4,128)S(1)} %bitcast.123, f32[256,128]{1,0:T(8,128)S(1)} %bitcast.133, f32[256,4,128]{2,1,0:T(4,128)S(1)} %bitcast.121, f32[256,128]{1,0:T(8,128)S(1)} %bitcast.134, f32[256,4,128]{2,1,0:T(4,128)S(1)} %bitcast.122, f32[256,128]{1,0:T(8,128)S(1)} %bitcast.135, ...), kind=kLoop, calls=%fused_computation.7 | loop fusion | flops 184516608 | bytes 2621440 | tf_op jit(solution)/shard_map/reduce_sum | solution.py:20
  122.1 35.6 %multiply_reduce_fusion.1 = f32[256,128]{1,0:T(8,128)S(1)} fusion(f32[256,4,128]{2,1,0:T(4,128)S(1)} %bitcast.127, f32[256,128]{1,0:T(8,128)S(1)} %bitcast.131, f32[256,4,128]{2,1,0:T(4,128)S(1)} %bitcast.125, f32[256,128]{1,0:T(8,128)S(1)} %bitcast.132, f32[256,4,128]{2,1,0:T(4,128)S(1)} %bitcast.126, f32[256,128]{1,0:T(8,128)S(1)} %bitcast.130, ...), kind=kLoop, calls=%fused_computation.8 | loop fusion | flops 184516608 | bytes 2621440 | tf_op jit(solution)/shard_map/reduce_sum | solution.py:20
  157.8 0.1 dynamic-slice_maximum_fusion
  157.9 0.2 slice_reduce_fusion.3
  158.2 0.1 slice_add_fusion.3
  158.2 0.1 pad_maximum_fusion.2
  158.3 1.1 fusion.3
  159.5 1.4 fusion.1
  160.9 0.6 broadcast_in_dim.73
  161.5 7.7 %all-to-all-start.2 = ((f32[16,2,16]{2,1,0:T(2,128)}), f32[16,2,16]{2,1,0:T(2,128)S(1)}, u32[]{:S(2)}, u32[]{:S(2)}) async-start(f32[16,2,16]{2,1,0:T(2,128)} %broadcast_in_dim.73), calls=%async_computation.2 | async-start | bytes 32768 | tf_op jit(solution)/shard_map/all_to_all | solution.py:100
  169.3 7.3 %all-to-all-done.2 = f32[16,2,16]{2,1,0:T(2,128)S(1)} async-done(((f32[16,2,16]{2,1,0:T(2,128)}), f32[16,2,16]{2,1,0:T(2,128)S(1)}, u32[]{:S(2)}, u32[]{:S(2)}) %all-to-all-start.2) | async-done | bytes 2080 | tf_op jit(solution)/shard_map/all_to_all | solution.py:100
  176.6 0.1 reshape.253
  176.7 0.2 all_to_all.27
  176.9 11.1 %all_to_all.34 = f32[16,1,4608]{2,1,0:T(1,128)S(1)} all-to-all(f32[16,1,4608]{2,1,0:T(1,128)S(1)} %all_to_all.27), channel_id=1, replica_groups=mesh['dom'=16,'grp'=16] {'grp'}, dimensions={0} | all-to-all | bytes 589824 | tf_op jit(solution)/shard_map/all_to_all | solution.py:112
  188.1 0.4 reshape.174
  188.5 0.3 copy.82
  188.7 0.2 reshape.175
  188.9 0.1 slice_bitcast_fusion.4
  189.0 0.1 slice_bitcast_fusion.5
  189.1 0.1 slice_bitcast_fusion.6
  189.2 0.7 gather_fusion.5
  189.9 0.7 bitcast_add_fusion
  190.6 0.1 fusion.17
  190.7 0.1 copy.91
  190.8 0.7 div.20
  (75 shorter events, 0.8 us)
Async XLA Ops:
  0.6 19.3 %copy-start = (s32[1,64]{1,0:T(1,128)S(1)}, s32[1,64]{1,0:T(1,128)}, u32[]{:S(2)}) copy-start(s32[1,64]{1,0:T(1,128)} %param.14) | copy-start | bytes 772
  9.5 10.2 %copy-start.13 = (s32[1,16,16]{2,1,0:T(8,128)S(1)}, s32[1,16,16]{2,1,0:T(8,128)}, u32[]{:S(2)}) copy-start(s32[1,16,16]{2,1,0:T(8,128)} %param.15) | copy-start | bytes 3076
  12.2 23.6 %all-to-all-start = ((f32[512,4,128]{2,1,0:T(4,128)}), f32[512,4,128]{2,1,0:T(4,128)S(1)}, u32[]{:S(2)}, u32[]{:S(2)}) async-start(f32[512,4,128]{2,1,0:T(4,128)} %broadcast_select_fusion), calls=%async_computation | async-start | bytes 2097152 | tf_op jit(solution)/shard_map/all_to_all | solution.py:59
  19.9 2.0 %copy-start.10 = (s32[256,128]{1,0:T(8,128)S(1)}, s32[256,128]{1,0:T(8,128)}, u32[]{:S(2)}) copy-start(s32[256,128]{1,0:T(8,128)} %param.13) | copy-start | bytes 393220
  19.9 2.1 %copy-start.1 = (f32[256,128]{1,0:T(8,128)S(1)}, f32[256,128]{1,0:T(8,128)}, u32[]{:S(2)}) copy-start(f32[256,128]{1,0:T(8,128)} %param.11) | copy-start | bytes 393220
  19.9 2.1 %copy-start.3 = (f32[256,3,128]{2,0,1:T(8,128)S(1)}, f32[256,3,128]{2,0,1:T(8,128)}, u32[]{:S(2)}) copy-start(f32[256,3,128]{2,0,1:T(8,128)} %param.10) | copy-start | bytes 1179652
  19.9 2.5 %copy-start.14 = (s32[512,4]{0,1:T(4,128)S(1)}, s32[512,4]{0,1:T(4,128)}, u32[]{:S(2)}) copy-start(s32[512,4]{0,1:T(4,128)} %param.17) | copy-start | bytes 24580
  21.8 2.9 %copy-start.16 = (s32[1,16]{1,0:T(1,128)S(1)}, s32[1,16]{1,0:T(1,128)}, u32[]{:S(2)}) copy-start(s32[1,16]{1,0:T(1,128)} %param.16) | copy-start | bytes 196
  22.0 14.8 %copy-start.11 = (s32[32768]{0:T(1024)}, s32[32768]{0:T(1024)S(1)}, u32[]{:S(2)}) copy-start(s32[32768]{0:T(1024)S(1)} %add_select_fusion) | copy-start | bytes 393220
  24.6 18.4 %copy-start.15 = (f32[4,16]{1,0:T(4,128)}, f32[4,16]{1,0:T(4,128)S(1)}, u32[]{:S(2)}) copy-start(f32[4,16]{1,0:T(4,128)S(1)} %fusion.2) | copy-start | bytes 772
  38.8 14.2 %all-to-all-start.1 = ((f32[16,1,8256]{2,1,0:T(1,128)}), f32[16,1,8256]{2,1,0:T(1,128)S(1)}, u32[]{:S(2)}, u32[]{:S(2)}) async-start(f32[16,1,8256]{2,1,0:T(1,128)} %copy.76), calls=%async_computation.1 | async-start | bytes 1064960 | tf_op jit(solution)/shard_map/all_to_all | solution.py:74
  53.2 104.6 %collective-permute-start.1 = (f32[16,4,16]{0,2,1:T(8,128)S(1)}, f32[16,4,16]{0,2,1:T(8,128)S(1)}, u32[]{:S(2)}, u32[]{:S(2)}) collective-permute-start(f32[16,4,16]{0,2,1:T(8,128)S(1)} %bitcast.137), channel_id=1, source_target_pairs={{0,240},{16,0},{32,16},{48,32},{64,48},{80,64},{96,80},{112,96},{1... | collective-permute-start | bytes 12296 | tf_op jit(solution)/shard_map/ppermute | solution.py:79
  55.8 102.0 %collective-permute-start = (f32[16,4,16]{0,2,1:T(8,128)S(1)}, f32[16,4,16]{0,2,1:T(8,128)S(1)}, u32[]{:S(2)}, u32[]{:S(2)}) collective-permute-start(f32[16,4,16]{0,2,1:T(8,128)S(1)} %bitcast.138), channel_id=1, source_target_pairs={{0,16},{16,32},{32,48},{48,64},{64,80},{80,96},{96,112},{112,128},... | collective-permute-start | bytes 12296 | tf_op jit(solution)/shard_map/ppermute | solution.py:78
  80.3 5.9 %copy-start.2 = (f32[256,4,1,128]{3,2,1,0:T(1,128)S(1)}, f32[256,4,1,128]{3,2,1,0:T(1,128)}, u32[]{:S(2)}) copy-start(f32[256,4,1,128]{3,2,1,0:T(1,128)} %get-tuple-element.16) | copy-start | bytes 1572868
  80.3 5.9 %copy-start.7 = (f32[256,1,128]{2,1,0:T(1,128)S(1)}, f32[256,1,128]{2,1,0:T(1,128)}, u32[]{:S(2)}) copy-start(f32[256,1,128]{2,1,0:T(1,128)} %get-tuple-element.18) | copy-start | bytes 393220
  80.3 5.9 %copy-start.8 = (f32[256,1,128]{2,1,0:T(1,128)S(1)}, f32[256,1,128]{2,1,0:T(1,128)}, u32[]{:S(2)}) copy-start(f32[256,1,128]{2,1,0:T(1,128)} %get-tuple-element.19) | copy-start | bytes 393220
  80.3 5.9 %copy-start.9 = (f32[256,1,128]{2,1,0:T(1,128)S(1)}, f32[256,1,128]{2,1,0:T(1,128)}, u32[]{:S(2)}) copy-start(f32[256,1,128]{2,1,0:T(1,128)} %get-tuple-element.20) | copy-start | bytes 393220
  86.2 35.8 %copy-start.5 = (f32[256,1,128]{2,1,0:T(1,128)S(1)}, f32[256,1,128]{2,1,0:T(1,128)}, u32[]{:S(2)}) copy-start(f32[256,1,128]{2,1,0:T(1,128)} %get-tuple-element.21) | copy-start | bytes 393220
  86.2 35.8 %copy-start.6 = (f32[256,1,128]{2,1,0:T(1,128)S(1)}, f32[256,1,128]{2,1,0:T(1,128)}, u32[]{:S(2)}) copy-start(f32[256,1,128]{2,1,0:T(1,128)} %get-tuple-element.22) | copy-start | bytes 393220
  122.1 36.2 %copy-start.4 = (f32[256,3,128]{2,0,1:T(8,128)S(1)}, f32[256,3,128]{2,0,1:T(8,128)}, u32[]{:S(2)}) copy-start(f32[256,3,128]{2,0,1:T(8,128)} %param.10) | copy-start | bytes 1179652
  122.1 36.2 %copy-start.12 = (s32[32768]{0:T(1024)S(1)}, s32[32768]{0:T(1024)}, u32[]{:S(2)}) copy-start(s32[32768]{0:T(1024)} %copy-done.11) | copy-start | bytes 393220
  157.7 3.2 %slice-start = ((f32[4,16]{1,0:T(4,128)}), f32[1,16]{1,0:T(1,128)S(1)}, s32[]{:S(2)}) async-start(f32[4,16]{1,0:T(4,128)} %copy-done.15), calls=%async_computation.4 | async-start | bytes 1024 | tf_op jit(solution)/shard_map/slice | solution.py:98
  161.5 15.0 %all-to-all-start.2 = ((f32[16,2,16]{2,1,0:T(2,128)}), f32[16,2,16]{2,1,0:T(2,128)S(1)}, u32[]{:S(2)}, u32[]{:S(2)}) async-start(f32[16,2,16]{2,1,0:T(2,128)} %broadcast_in_dim.73), calls=%async_computation.2 | async-start | bytes 32768 | tf_op jit(solution)/shard_map/all_to_all | solution.py:100
